TPU v7x, 256 devices: a whole 4x4x8 slice. The times are simulated.
256 devices in a mesh: seq: 8 (over x, core), tensor: 32 (over z, y).
Axes of the slice: x: 4, y: 4, z: 8, core: 2. Of those that a mesh axis runs over, the one named last changes fastest.
Arguments:
- tokens: bfloat16 [2048, 2048], P(('seq', 'tensor')), may hold values from -6 to 6
- attn_gain: bfloat16 [2048], replicated, may hold values from 0.25 to 1.75
- w_qkv: bfloat16 [2048, 3, 2048], P(None, None, 'tensor'), may hold values from -0.125 to 0.125
- q_gain: bfloat16 [2048], P('tensor'), may hold values from 0.25 to 1.75
- k_gain: bfloat16 [2048], P('tensor'), may hold values from 0.25 to 1.75
- w_out: bfloat16 [2048, 2048], P('tensor'), may hold values from -0.125 to 0.125
- prefix_keys: bfloat16 [8, 2048, 2048], P('seq', None, 'tensor'), may hold values from -150 to 150
- prefix_values: bfloat16 [8, 2048, 2048], P('seq', None, 'tensor'), may hold values from -6 to 6
- segments: int32 [2048], replicated, may hold values from 0 to 31, never falling along the last dimension, each value on 1 to 256 neighbouring positions
- request_group: int32 [32], replicated, may hold values from 0 to 3
- prefix_owner: int32 [4], replicated, may hold values from 0 to 7, as said below
- mlp_gain: bfloat16 [2048], replicated, may hold values from 0.25 to 1.75
- expert_ids: int32 [2048, 8], P(('seq', 'tensor')), may hold values from 0 to 63, all different within a row; in each aligned block of 8 rows (0 to 7, 8 to 15, ...) at most 2 rows name the same one
- gate_weights: float32 [2048, 8], P(('seq', 'tensor')), may hold values from 0.05 to 0.5
- w_gate: bfloat16 [256, 2048, 256], P(('tensor', 'seq')), may hold values from -0.125 to 0.125
- w_up: bfloat16 [256, 2048, 256], P(('tensor', 'seq')), may hold values from -0.125 to 0.125
- w_down: bfloat16 [256, 256, 2048], P(('tensor', 'seq')), may hold values from -0.1875 to 0.1875
Outputs:
- output: bfloat16 [2048, 2048], P(('seq', 'tensor'))
- new_keys: bfloat16 [2048, 2048], P('seq', 'tensor')
- new_values: bfloat16 [2048, 2048], P('seq', 'tensor')
Inputs may be any that keep to these rules, and one draw needn't show every extreme that they name: `segments`: each request's tokens are consecutive; a request has at most 256 tokens, and some request has exactly 256. `prefix_owner`: distinct slots. `expert_ids`: a token's experts are distinct; among the 8 rows of one device no expert is named more than 2 times, and that count is reached.
All inputs are finite; a program needn't handle non-finite values.
Results may differ from a plain program's by a relative error of at most 0.017.
Values may be sent and summed in bfloat16 or wider, within the bound.
No kernel may reach another device: no remote copies, remote signals or barrier semaphores. Data moves between devices by JAX's collectives and lax.ppermute only.
A program may use at most 64 MiB of HBM per device.

v0:
```python
import jax
import jax.numpy as jnp
from jax import lax
from jax.sharding import PartitionSpec as P

HD = 128
TOP = 8
EXP_DEV = 2


def from_partner(value, axis, stride):
    mask = 2**stride
    pairs = [(source, source ^ mask) for source in range(lax.axis_size(axis))]
    return lax.ppermute(value, axis, pairs)


def passed_along(value, axis, by):
    devices = lax.axis_size(axis)
    pairs = [(i, i + by) for i in range(devices) if 0 <= i + by < devices]
    return lax.ppermute(value, axis, pairs)


def rms_scale(values, gain):
    mean_square = jnp.mean(values * values, axis=-1, keepdims=True)
    return values * lax.rsqrt(mean_square + 1e-05) * gain.astype(jnp.float32)


def attend_block(carry, queries_heads, block, mask):
    largest, total, accum = carry
    heads_local = queries_heads.shape[1]
    count = block.shape[0]
    key_block = block[:, 0].reshape(count, heads_local, HD)
    value_block = block[:, 1].reshape(count, heads_local, HD)
    scores = jnp.einsum(
        "qhd,khd->hqk", queries_heads, key_block, preferred_element_type=jnp.float32
    ) * HD ** (-0.5)
    scores = jnp.where(mask[None], scores, -1e30)
    new_largest = jnp.maximum(largest, jnp.max(scores, axis=-1))
    weights = jnp.where(mask[None], jnp.exp(scores - new_largest[:, :, None]), 0.0)
    factor = jnp.exp(largest - new_largest)
    total = total * factor + jnp.sum(weights, axis=-1)
    update = jnp.einsum(
        "hqk,khd->hqd",
        weights.astype(jnp.bfloat16),
        value_block,
        preferred_element_type=jnp.float32,
    )
    accum = accum * factor[:, :, None] + update
    return (new_largest, total, accum)


def local(
    tokens,
    attn_gain,
    w_qkv,
    q_gain,
    k_gain,
    w_out,
    prefix_keys,
    prefix_values,
    segments,
    request_group,
    prefix_owner,
    mlp_gain,
    expert_ids,
    gate_weights,
    w_gate,
    w_up,
    w_down,
):
    tensor_size = lax.axis_size("tensor")
    seq_size = lax.axis_size("seq")
    seq_index = lax.axis_index("seq")
    tensor_index = lax.axis_index("tensor")
    tok_dev = tokens.shape[0]
    width = tokens.shape[1]
    tok_seq = tok_dev * tensor_size
    columns = w_qkv.shape[2]
    normed = rms_scale(tokens.astype(jnp.float32), attn_gain).astype(jnp.bfloat16)
    w_flat = w_qkv.reshape(width, 3 * columns)
    projected = jnp.dot(
        lax.all_gather(normed, "tensor", axis=0, tiled=True),
        w_flat,
        preferred_element_type=jnp.float32,
    )
    query_part = projected[:, :columns]
    key_part = projected[:, columns : 2 * columns]
    squares = lax.psum(
        (jnp.sum(query_part * query_part, axis=-1), jnp.sum(key_part * key_part, axis=-1)), "tensor"
    )
    query_rows = (
        query_part * lax.rsqrt(squares[0] / width + 1e-05)[:, None] * q_gain.astype(jnp.float32)
    ).astype(jnp.bfloat16)
    new_keys = (
        key_part * lax.rsqrt(squares[1] / width + 1e-05)[:, None] * k_gain.astype(jnp.float32)
    ).astype(jnp.bfloat16)
    new_values = projected[:, 2 * columns :].astype(jnp.bfloat16)
    stacked = jnp.stack(
        [
            jnp.concatenate([new_keys, prefix_keys[0]], axis=0),
            jnp.concatenate([new_values, prefix_values[0]], axis=0),
        ],
        axis=1,
    )
    half_rows = tok_seq // 2
    lower_bit = tensor_index % 2
    partner = from_partner(stacked, "tensor", 0)
    full = jnp.where(
        lower_bit == 0,
        jnp.concatenate([stacked, partner], axis=-1),
        jnp.concatenate([partner, stacked], axis=-1),
    )
    query_halves = query_rows.reshape(2, half_rows, columns)
    own_half = lax.dynamic_index_in_dim(query_halves, lower_bit, 0, keepdims=False)
    send_half = lax.dynamic_index_in_dim(query_halves, 1 - lower_bit, 0, keepdims=False)
    got_half = from_partner(send_half, "tensor", 0)
    query_full = jnp.where(
        lower_bit == 0,
        jnp.concatenate([own_half, got_half], axis=-1),
        jnp.concatenate([got_half, own_half], axis=-1),
    )
    query_offset = lower_bit * half_rows
    heads_local = 1
    suffix_full = full[:tok_seq]
    prefix_full = full[tok_seq:]
    queries_heads = query_full.reshape(half_rows, heads_local, HD)
    groups_count = prefix_owner.shape[0]
    request_count = request_group.shape[0]
    token_group = jnp.sum(
        jnp.where(
            segments[:, None] == jnp.arange(request_count, dtype=jnp.int32)[None, :],
            request_group[None, :],
            0,
        ),
        axis=1,
    )
    base_row = seq_index * tok_seq
    query_start = base_row + query_offset
    query_seg = lax.dynamic_slice_in_dim(segments, query_start, half_rows, 0)
    query_group = lax.dynamic_slice_in_dim(token_group, query_start, half_rows, 0)
    query_pos = query_start + jnp.arange(half_rows, dtype=jnp.int32)
    padded_seg = jnp.concatenate([jnp.full((tok_seq,), -1, jnp.int32), segments], axis=0)
    key_seg = lax.dynamic_slice_in_dim(padded_seg, base_row, 2 * tok_seq, 0)
    key_pos = base_row - tok_seq + jnp.arange(2 * tok_seq, dtype=jnp.int32)
    previous = passed_along(suffix_full, "seq", 1)
    suffix_keys = jnp.concatenate([previous, suffix_full], axis=0)
    suffix_mask = (key_seg[None, :] == query_seg[:, None]) & (
        key_pos[None, :] <= query_pos[:, None]
    )
    carry = (
        jnp.full((heads_local, half_rows), -1e30, jnp.float32),
        jnp.zeros((heads_local, half_rows), jnp.float32),
        jnp.zeros((heads_local, half_rows, HD), jnp.float32),
    )
    carry = attend_block(carry, queries_heads, suffix_keys, suffix_mask)
    owner_of_query = jnp.sum(
        jnp.where(
            query_group[:, None] == jnp.arange(groups_count, dtype=jnp.int32)[None, :],
            prefix_owner[None, :],
            0,
        ),
        axis=1,
    )
    state = carry
    piece = lax.all_gather(prefix_full[None], "seq", axis=0, tiled=True)
    start = jnp.int32(0)
    for offset in range(piece.shape[0]):
        slot_mask = (owner_of_query == start + offset)[:, None]
        state = attend_block(state, queries_heads, piece[offset], slot_mask)
    carry = state
    attended = (carry[2] / carry[1][:, :, None]).astype(jnp.bfloat16)
    attended = jnp.transpose(attended, (1, 0, 2)).reshape(half_rows, heads_local * HD)
    split_out = attended.reshape(half_rows, 2, columns)
    own_out = lax.dynamic_index_in_dim(split_out, lower_bit, 1, keepdims=False)
    send_out = lax.dynamic_index_in_dim(split_out, 1 - lower_bit, 1, keepdims=False)
    got_out = from_partner(send_out, "tensor", 0)
    attended_local = jnp.where(
        lower_bit == 0,
        jnp.concatenate([own_out, got_out], axis=0),
        jnp.concatenate([got_out, own_out], axis=0),
    )
    attn_sum = lax.psum_scatter(
        jnp.dot(attended_local, w_out, preferred_element_type=jnp.float32).astype(jnp.bfloat16),
        "tensor",
        scatter_dimension=0,
        tiled=True,
    ).astype(jnp.float32)
    mixed_rows = (tokens.astype(jnp.float32) + attn_sum).astype(jnp.bfloat16)
    expert_in = rms_scale(mixed_rows.astype(jnp.float32), mlp_gain).astype(jnp.bfloat16)
    exp_local = EXP_DEV
    experts_all = exp_local * tensor_size
    own_expert = seq_index // (seq_size // exp_local)
    capacity = max(2, 2 * tok_dev * TOP // experts_all)
    flat_ids = expert_ids.reshape(-1)
    onehot = (flat_ids[:, None] == jnp.arange(experts_all, dtype=jnp.int32)[None, :]).astype(
        jnp.int32
    )
    before = jnp.cumsum(onehot, axis=0) - onehot
    slot = flat_ids * capacity + jnp.sum(before * onehot, axis=1)
    slot_match = (
        slot.reshape(tok_dev, TOP)[:, :, None]
        == jnp.arange(experts_all * capacity, dtype=jnp.int32)[None, None, :]
    )
    dispatch_table = jnp.transpose(jnp.any(slot_match, axis=1)).astype(jnp.bfloat16)
    combine_table = jnp.sum(jnp.where(slot_match, gate_weights[:, :, None], 0.0), axis=1)
    buffer = jnp.dot(dispatch_table, expert_in, preferred_element_type=jnp.float32).astype(
        jnp.bfloat16
    )
    buffer = buffer.reshape(tensor_size, exp_local, capacity, width)
    received = lax.all_to_all(buffer, "tensor", split_axis=0, concat_axis=0, tiled=True)
    gate_local = w_gate[0]
    up_local = w_up[0]
    down_local = w_down[0]
    keep_expert = (jnp.arange(exp_local, dtype=jnp.int32) == own_expert)[None, None, :, None, None]
    chosen = lax.dynamic_index_in_dim(
        lax.all_gather(received[None], "seq", axis=0, tiled=True), own_expert, 2, keepdims=False
    )
    gated = jnp.einsum("srcd,df->srcf", chosen, gate_local, preferred_element_type=jnp.float32)
    upward = jnp.einsum("srcd,df->srcf", chosen, up_local, preferred_element_type=jnp.float32)
    activity = (jax.nn.silu(gated) * upward).astype(jnp.bfloat16)
    result = jnp.einsum("srcf,fd->srcd", activity, down_local, preferred_element_type=jnp.float32)
    partials = jnp.where(keep_expert, result[:, :, None], 0.0)
    summed = lax.psum_scatter(
        partials.astype(jnp.bfloat16), "seq", scatter_dimension=0, tiled=True
    ).astype(jnp.float32)
    returned = lax.all_to_all(
        summed[0].astype(jnp.bfloat16), "tensor", split_axis=0, concat_axis=0, tiled=True
    ).astype(jnp.float32)
    moe_sum = jnp.dot(
        combine_table,
        returned.reshape(experts_all * capacity, width),
        preferred_element_type=jnp.float32,
        precision=lax.Precision.HIGHEST,
    )
    output = (mixed_rows.astype(jnp.float32) + moe_sum).astype(jnp.bfloat16)
    return (output, new_keys, new_values)


def solution(mesh):
    return jax.shard_map(
        local,
        mesh=mesh,
        in_specs=(
            P(("seq", "tensor"), None),
            P(),
            P(None, None, "tensor"),
            P("tensor"),
            P("tensor"),
            P("tensor", None),
            P("seq", None, "tensor"),
            P("seq", None, "tensor"),
            P(),
            P(),
            P(),
            P(),
            P(("seq", "tensor"), None),
            P(("seq", "tensor"), None),
            P(("tensor", "seq"), None, None),
            P(("tensor", "seq"), None, None),
            P(("tensor", "seq"), None, None),
        ),
        out_specs=(P(("seq", "tensor"), None), P("seq", "tensor"), P("seq", "tensor")),
        check_vma=False,
    )
```

profile of v0, /device:TPU:7, one launch (start us, length us, event | category | flops | bytes accessed | tf_op | source)
XLA Modules:
  0.0 611.7 jit_solution(2443688240489283355)
XLA Ops:
  8.9 1.5 fusion.100
  11.7 73.7 %all-gather.6.cloned.1.call-done = bf16[256,2048]{1,0:T(8,128)(2,1)} async-done(((bf16[8,2048]{1,0:T(8,128)(2,1)}), bf16[256,2048]{1,0:T(8,128)(2,1)}) %all-gather.6.cloned.1.call-update) | async-done | bytes 1048592 | tf_op jit(solution)/shard_map/all_gather | solution.py:82
  85.5 2.0 fusion.142
  88.5 58.0 %all-reduce.1 = (f32[256]{0:T(256)S(1)}, f32[256]{0:T(256)S(1)}) all-reduce(f32[256]{0:T(256)S(1)} %get-tuple-element.4, f32[256]{0:T(256)S(1)} %get-tuple-element.3), channel_id=1, replica_groups=mesh['seq'=8,'tensor'=32] {'tensor'}, use_global_device_ids=true, to_apply=%region_4.0 | all-reduce | flops 512 | bytes 4096 | tf_op jit(solution)/shard_map/psum | solution.py:88
  147.8 9.0 %collective-permute-done.1 = bf16[2304,2,64]{0,2,1:T(8,128)(2,1)S(1)} collective-permute-done((bf16[2304,2,64]{0,2,1:T(8,128)(2,1)S(1)}, bf16[2304,2,64]{0,2,1:T(8,128)(2,1)S(1)}, u32[]{:S(2)}, u32[]{:S(2)}) %collective-permute-start.1) | collective-permute-done | bytes 589856 | tf_op jit(solution)/shard_map/ppermute | solution.py:14
  157.1 1.2 slice.155
  158.8 1.3 collective-permute-start.2
  160.4 2.5 collective-permute-done
  162.9 19.3 %collective-permute-done.2 = bf16[256,2,128]{0,2,1:T(8,128)(2,1)S(1)} collective-permute-done((bf16[256,2,128]{0,2,1:T(8,128)(2,1)S(1)}, bf16[256,2,128]{0,2,1:T(8,128)(2,1)S(1)}, u32[]{:S(2)}, u32[]{:S(2)}) %collective-permute-start.2) | collective-permute-done | bytes 131104 | tf_op jit(solution)/shard_map/ppermute | solution.py:20
  182.5 43.9 %all-gather.8.cloned.1.call-done = bf16[16384,2,128]{0,2,1:T(8,128)(2,1)} async-done(((bf16[2048,2,128]{0,2,1:T(8,128)(2,1)}), bf16[16384,2,128]{0,2,1:T(8,128)(2,1)}) %all-gather.8.cloned.1.call-update) | async-done | bytes 8388624 | tf_op jit(solution)/shard_map/all_gather | solution.py:165
  226.4 1.6 fusion.133
  228.0 1.8 fusion.134
  229.9 1.5 fusion.135
  231.3 1.5 fusion.136
  232.8 1.5 fusion.137
  234.2 1.5 fusion.138
  243.0 1.4 collective-permute-start.3
  244.4 1.3 collective-permute-done.3
  245.7 1.4 convolution_convert_fusion
  247.8 213.9 %reduce-scatter.3.cloned.1.call-done = bf16[8,2048]{1,0:T(8,128)(2,1)} async-done(((bf16[256,2048]{1,0:T(8,128)(2,1)}), bf16[8,2048]{1,0:T(8,128)(2,1)}) %reduce-scatter.3.cloned.1.call-update) | async-done | bytes 32784 | tf_op jit(solution)/shard_map/reduce_scatter | solution.py:182
  462.6 1.1 convolution_convert_fusion.1
  464.1 19.3 %all_to_all.10 = bf16[32,2,2,2048]{3,2,1,0:T(2,128)(2,1)} all-to-all(bf16[32,2,2,2048]{3,2,1,0:T(2,128)(2,1)S(1)} %reshape.872), channel_id=1, replica_groups=mesh['seq'=8,'tensor'=32] {'tensor'}, dimensions={0} | all-to-all | bytes 1048576 | tf_op jit(solution)/shard_map/all_to_all | solution.py:210
  483.5 35.6 %all-gather.10.cloned.1.call-done = bf16[256,2,2,2048]{3,2,1,0:T(2,128)(2,1)} async-done(((bf16[32,2,2,2048]{3,2,1,0:T(2,128)(2,1)}), bf16[256,2,2,2048]{3,2,1,0:T(2,128)(2,1)}) %all-gather.10.cloned.1.call-update) | async-done | bytes 4194320 | tf_op jit(solution)/shard_map/all_gather | solution.py:216
  519.1 3.7 constant_dynamic-slice_fusion
  522.8 1.3 copy-done.2
  524.1 2.8 fusion.10
  526.9 4.3 fusion.14
  531.2 3.0 select_convert_fusion
  534.2 40.7 %reduce-scatter.5.cloned.1.call-done = bf16[1,32,2,2,2048]{4,1,3,2,0:T(8,128)(2,1)} async-done(((bf16[8,32,2,2,2048]{4,1,3,2,0:T(8,128)(2,1)}), bf16[1,32,2,2,2048]{4,1,3,2,0:T(8,128)(2,1)}) %reduce-scatter.5.cloned.1.call-update) | async-done | bytes 524304 | tf_op jit(solution)/shard_map/reduce_scatter | solution.py:223
  574.9 2.4 copy.40
  577.3 9.4 %all-to-all-start.1 = ((bf16[32,2,2,2048]{3,2,1,0:T(2,128)(2,1)}), bf16[32,2,2,2048]{3,2,1,0:T(2,128)(2,1)S(1)}, u32[]{:S(2)}, u32[]{:S(2)}) async-start(bf16[32,2,2,2048]{3,2,1,0:T(2,128)(2,1)} %copy.40), calls=%async_computation.3 | async-start | bytes 1048576 | tf_op jit(solution)/shard_map/all_to_all | solution.py:226
  586.8 17.2 %all-to-all-done.1 = bf16[32,2,2,2048]{3,2,1,0:T(2,128)(2,1)S(1)} async-done(((bf16[32,2,2,2048]{3,2,1,0:T(2,128)(2,1)}), bf16[32,2,2,2048]{3,2,1,0:T(2,128)(2,1)S(1)}, u32[]{:S(2)}, u32[]{:S(2)}) %all-to-all-start.1) | async-done | bytes 524320 | tf_op jit(solution)/shard_map/all_to_all | solution.py:226
  (103 shorter events, 17.0 us)
Async XLA Ops:
  7.2 519.8 %copy-start = (bf16[1,256,2048]{2,1,0:T(8,128)(2,1)S(1)}, bf16[1,256,2048]{2,1,0:T(8,128)(2,1)}, u32[]{:S(2)}) copy-start(bf16[1,256,2048]{2,1,0:T(8,128)(2,1)} %param.33) | copy-start | bytes 3145732
  7.2 78.3 %all-gather.6.cloned.1.call-start = ((), (), s32[]{:S(2)}) async-start(), calls=%async_computation.4 | async-start | bytes 1081344 | tf_op jit(solution)/shard_map/all_gather | solution.py:82
  10.4 216.1 %all-gather.8.cloned.1.call-start = ((), (), s32[]{:S(2)}) async-start(), calls=%async_computation.7 | async-start | bytes 9437184 | tf_op jit(solution)/shard_map/all_gather | solution.py:165
  87.4 70.9 %copy-start.8 = (s32[2048]{0:T(1024)S(1)}, s32[2048]{0:T(1024)}, u32[]{:S(2)}) copy-start(s32[2048]{0:T(1024)} %param.25) | copy-start | bytes 24580
  87.4 70.9 %copy-start.12 = (s32[32]{0:T(128)S(1)}, s32[32]{0:T(128)}, u32[]{:S(2)}) copy-start(s32[32]{0:T(128)} %param.26) | copy-start | bytes 388
  87.5 71.2 %copy-start.13 = (s32[4]{0:T(128)S(1)}, s32[4]{0:T(128)}, u32[]{:S(2)}) copy-start(s32[4]{0:T(128)} %param.27) | copy-start | bytes 52
  87.5 71.3 %copy-start.7 = (bf16[256,64]{0,1:T(8,128)(2,1)}, bf16[256,64]{0,1:T(8,128)(2,1)S(1)}, u32[]{:S(2)}) copy-start(bf16[256,64]{0,1:T(8,128)(2,1)S(1)} %slice.219) | copy-start | bytes 98308
  146.6 35.9 %copy-start.6 = (bf16[256,64]{0,1:T(8,128)(2,1)}, bf16[256,64]{0,1:T(8,128)(2,1)S(1)}, u32[]{:S(2)}) copy-start(bf16[256,64]{0,1:T(8,128)(2,1)S(1)} %get-tuple-element.25) | copy-start | bytes 98308
  147.7 9.2 %collective-permute-start.1 = (bf16[2304,2,64]{0,2,1:T(8,128)(2,1)S(1)}, bf16[2304,2,64]{0,2,1:T(8,128)(2,1)S(1)}, u32[]{:S(2)}, u32[]{:S(2)}) collective-permute-start(bf16[2304,2,64]{0,2,1:T(8,128)(2,1)S(1)} %pad_maximum_fusion), channel_id=1, source_target_pairs={{0,1},{1,0},{2,3},{3,2},{4,5},{5,4},{6,7},{7,6},{8,9},{9,8},{10,11... | collective-permute-start | bytes 1769480 | tf_op jit(solution)/shard_map/ppermute | solution.py:14
  158.3 303.4 %reduce-scatter.3.cloned.1.call-start = ((), (), s32[]{:S(2)}) async-start(), calls=%async_computation.5 | async-start | bytes 1081344 | tf_op jit(solution)/shard_map/reduce_scatter | solution.py:182
  158.8 23.4 %collective-permute-start.2 = (bf16[256,2,128]{0,2,1:T(8,128)(2,1)S(1)}, bf16[256,2,128]{0,2,1:T(8,128)(2,1)S(1)}, u32[]{:S(2)}, u32[]{:S(2)}) collective-permute-start(bf16[256,2,128]{0,2,1:T(8,128)(2,1)S(1)} %slice.152), channel_id=1, source_target_pairs={{0,32},{32,64},{64,96},{96,128},{128,160},{160,192},{192,224},{1,3... | collective-permute-start | bytes 393224 | tf_op jit(solution)/shard_map/ppermute | solution.py:20
  160.2 2.7 collective-permute-start
  226.4 9.3 %copy-start.1 = (bf16[16384,2,128]{0,2,1:T(8,128)(2,1)S(1)}, bf16[16384,2,128]{0,2,1:T(8,128)(2,1)}, u32[]{:S(2)}) copy-start(bf16[16384,2,128]{0,2,1:T(8,128)(2,1)} %all-gather.8.cloned.1.call-done) | copy-start | bytes 25165828
  241.3 4.3 copy-start.5
  241.7 5.5 copy-start.9
  241.8 6.0 copy-start.10
  241.8 220.0 %copy-start.3 = (bf16[8,2048]{1,0:T(8,128)(2,1)S(1)}, bf16[8,2048]{1,0:T(8,128)(2,1)}, u32[]{:S(2)}) copy-start(bf16[8,2048]{1,0:T(8,128)(2,1)} %param.17) | copy-start | bytes 98308
  243.0 2.7 collective-permute-start.3
  247.1 272.0 %all-gather.10.cloned.1.call-start = ((), (), s32[]{:S(2)}) async-start(), calls=%async_computation.8 | async-start | bytes 4718592 | tf_op jit(solution)/shard_map/all_gather | solution.py:216
  483.4 91.5 %reduce-scatter.5.cloned.1.call-start = ((), (), s32[]{:S(2)}) async-start(), calls=%async_computation.6 | async-start | bytes 4718592 | tf_op jit(solution)/shard_map/reduce_scatter | solution.py:223
  522.8 1.4 copy-start.2
  534.2 52.5 %copy-start.11 = (f32[8,8]{1,0:T(8,128)S(1)}, f32[8,8]{1,0:T(8,128)}, u32[]{:S(2)}) copy-start(f32[8,8]{1,0:T(8,128)} %param.30) | copy-start | bytes 772
  534.2 70.0 %copy-start.4 = (bf16[8,2048]{1,0:T(8,128)(2,1)S(1)}, bf16[8,2048]{1,0:T(8,128)(2,1)}, u32[]{:S(2)}) copy-start(bf16[8,2048]{1,0:T(8,128)(2,1)} %reduce-scatter.3.cloned.1.call-done) | copy-start | bytes 98308
  577.3 26.7 %all-to-all-start.1 = ((bf16[32,2,2,2048]{3,2,1,0:T(2,128)(2,1)}), bf16[32,2,2,2048]{3,2,1,0:T(2,128)(2,1)S(1)}, u32[]{:S(2)}, u32[]{:S(2)}) async-start(bf16[32,2,2,2048]{3,2,1,0:T(2,128)(2,1)} %copy.40), calls=%async_computation.3 | async-start | bytes 1048576 | tf_op jit(solution)/shard_map/all_to_all | solution.py:226
Sparse Core Ops, SparseCore 0:
  11.1 74.2 all-gather.5
  158.4 67.9 all-gather.7
  247.3 214.4 reduce-scatter.2
  483.5 35.5 all-gather.9
  534.3 40.5 reduce-scatter.4
where the time goes:
time: 613 us; the launch traced here: 612 us
  waiting for transfers between devices  457 us (75%)
  blocking collectives  77.3 us (13%)
  matrix products  26.4 us (4%)
  other arithmetic  14.4 us (2%)
  between operations  14.3 us (2%)
  starting transfers between devices  12.5 us (2%)
  local copies, waits for them, and re-layouts  9.66 us (2%)
    reduce_scatter x1, waiting for transfers between devices, local(): lax.psum_scatter(jnp.dot(attended_local, w_out, preferred_element_type=jn...  214 us
    all_gather x1, waiting for transfers between devices, local(): lax.all_gather(normed, 'tensor', axis=0, tiled=True)  73.7 us
    psum x1, blocking collectives, local(): lax.psum((jnp.sum(query_part * query_part, axis=-1), jnp.sum(key_part * k...  58 us
    all_gather x1, waiting for transfers between devices, local(): piece = lax.all_gather(prefix_full[None], 'seq', axis=0, tiled=True)  43.9 us
    reduce_scatter x1, waiting for transfers between devices, local(): lax.psum_scatter(partials.astype(jnp.bfloat16), 'seq', scatter_dimension=...  40.7 us
    all_gather x1, waiting for transfers between devices, local(): lax.all_gather(received[None], 'seq', axis=0, tiled=True)  35.6 us
    ppermute x1, waiting for transfers between devices, passed_along(): return lax.ppermute(value, axis, pairs)  19.3 us
    all_to_all x1, blocking collectives, local(): lax.all_to_all(buffer, 'tensor', split_axis=0, concat_axis=0, tiled=True)  19.3 us
  transfers between devices with their start and end apart: 10, of which 10 were waited for; matrix products, arithmetic and copies ran while one was open for 0% of the time, Pallas kernels for 0%

commit v1 on v0

--- a/solution.py
+++ b/solution.py
@@ -18,6 +18,13 @@
     devices = lax.axis_size(axis)
     pairs = [(i, i + by) for i in range(devices) if 0 <= i + by < devices]
     return lax.ppermute(value, axis, pairs)
+
+
+def gather_by_exchange(value, axis):
+    devices = lax.axis_size(axis)
+    copies = jnp.broadcast_to(value[None], (devices,) + value.shape)
+    got = lax.all_to_all(copies, axis, 0, 0, tiled=True)
+    return got
 
 
 def rms_scale(values, gain):
@@ -79,15 +86,16 @@
     normed = rms_scale(tokens.astype(jnp.float32), attn_gain).astype(jnp.bfloat16)
     w_flat = w_qkv.reshape(width, 3 * columns)
     projected = jnp.dot(
-        lax.all_gather(normed, "tensor", axis=0, tiled=True),
+        gather_by_exchange(normed, "tensor").reshape(tok_seq, width),
         w_flat,
         preferred_element_type=jnp.float32,
     )
     query_part = projected[:, :columns]
     key_part = projected[:, columns : 2 * columns]
-    squares = lax.psum(
-        (jnp.sum(query_part * query_part, axis=-1), jnp.sum(key_part * key_part, axis=-1)), "tensor"
-    )
+    partial_squares = jnp.stack(
+        [jnp.sum(query_part * query_part, axis=-1), jnp.sum(key_part * key_part, axis=-1)]
+    )
+    squares = jnp.sum(gather_by_exchange(partial_squares, "tensor"), axis=0)
     query_rows = (
         query_part * lax.rsqrt(squares[0] / width + 1e-05)[:, None] * q_gain.astype(jnp.float32)
     ).astype(jnp.bfloat16)
@@ -179,12 +187,11 @@
         jnp.concatenate([own_out, got_out], axis=0),
         jnp.concatenate([got_out, own_out], axis=0),
     )
-    attn_sum = lax.psum_scatter(
-        jnp.dot(attended_local, w_out, preferred_element_type=jnp.float32).astype(jnp.bfloat16),
-        "tensor",
-        scatter_dimension=0,
-        tiled=True,
-    ).astype(jnp.float32)
+    attn_partial = jnp.dot(attended_local, w_out, preferred_element_type=jnp.float32)
+    attn_partial = attn_partial.astype(jnp.bfloat16).reshape(tensor_size, tok_dev, width)
+    attn_sum = jnp.sum(
+        lax.all_to_all(attn_partial, "tensor", 0, 0, tiled=True).astype(jnp.float32), axis=0
+    )
     mixed_rows = (tokens.astype(jnp.float32) + attn_sum).astype(jnp.bfloat16)
     expert_in = rms_scale(mixed_rows.astype(jnp.float32), mlp_gain).astype(jnp.bfloat16)
     exp_local = EXP_DEV

time: 613 us -> 333 us (0.54)
  waiting for transfers between devices: 457 us -> 184 us
  blocking collectives: 77.3 us -> 58.4 us
  starting transfers between devices: 12.5 us -> 29.1 us
    reduce_scatter x1 -> x0, waiting for transfers between devices: 214 us -> none  [local(): lax.psum_scatter(jnp.dot(attended_local, w_out, preferred_element_type=jn...]
    all_gather x1 -> x0, waiting for transfers between devices: 73.7 us -> none  [local(): lax.all_gather(normed, 'tensor', axis=0, tiled=True)]
    psum x1 -> x0, blocking collectives: 58 us -> none  [local(): lax.psum((jnp.sum(query_part * query_part, axis=-1), jnp.sum(key_part * k...]
    all_to_all x0 -> x1, blocking collectives: none -> 37.2 us  [gather_by_exchange(): got = lax.all_to_all(copies, axis, 0, 0, tiled=True)]
    all_to_all x0 -> x2, waiting for transfers between devices: none -> 33.8 us  [the longest x1 25.1 us: local(): lax.all_to_all(attn_partial, 'tensor', 0, 0, tiled=True).astype(jnp.float32)]
    ppermute x1, waiting for transfers between devices: 19.3 us -> 2.66 us  [passed_along(): return lax.ppermute(value, axis, pairs)]
    all_to_all x0 -> x2, starting transfers between devices: none -> 16.3 us  [the longest x1 9.74 us: local(): lax.all_to_all(attn_partial, 'tensor', 0, 0, tiled=True).astype(jnp.float32)]
where the time goes in v1:
time: 333 us; the launch traced here: 332 us
  waiting for transfers between devices  184 us (55%)
  blocking collectives  58.4 us (18%)
  starting transfers between devices  29.1 us (9%)
  matrix products  25.3 us (8%)
  between operations  14.3 us (4%)
  local copies, waits for them, and re-layouts  10.4 us (3%)
  other arithmetic  10.1 us (3%)
    all_gather x1, waiting for transfers between devices, local(): piece = lax.all_gather(prefix_full[None], 'seq', axis=0, tiled=True)  41.7 us
    reduce_scatter x1, waiting for transfers between devices, local(): lax.psum_scatter(partials.astype(jnp.bfloat16), 'seq', scatter_dimension=...  40.7 us
    all_to_all x1, blocking collectives, gather_by_exchange(): got = lax.all_to_all(copies, axis, 0, 0, tiled=True)  37.2 us
    all_gather x1, waiting for transfers between devices, local(): lax.all_gather(received[None], 'seq', axis=0, tiled=True)  33.2 us
    all_to_all x1, waiting for transfers between devices, local(): lax.all_to_all(attn_partial, 'tensor', 0, 0, tiled=True).astype(jnp.float32)  25.1 us
    all_to_all x1, blocking collectives, local(): lax.all_to_all(buffer, 'tensor', split_axis=0, concat_axis=0, tiled=True)  21.2 us
    all_to_all x1, waiting for transfers between devices, local(): lax.all_to_all(summed[0].astype(jnp.bfloat16), 'tensor', split_axis=0, co...  17.2 us
    ppermute x3, waiting for transfers between devices, from_partner(): return lax.ppermute(value, axis, pairs)  15 us
  transfers between devices with their start and end apart: 10, of which 10 were waited for; matrix products, arithmetic and copies ran while one was open for 0% of the time, Pallas kernels for 0%

profile of v1, /device:TPU:7, one launch (start us, length us, event | category | flops | bytes accessed | tf_op | source)
XLA Modules:
  0.0 331.9 jit_solution(13519340740135800317)
XLA Ops:
  9.9 37.2 %all_to_all.25 = bf16[32,8,2048]{2,1,0:T(8,128)(2,1)S(1)} all-to-all(bf16[32,8,2048]{2,1,0:T(8,128)(2,1)S(1)} %broadcast_in_dim.222), channel_id=1, replica_groups=mesh['seq'=8,'tensor'=32] {'tensor'}, dimensions={0} | all-to-all | bytes 2097152 | tf_op jit(solution)/shard_map/all_to_all | solution.py:26
  47.1 1.6 fusion.30
  49.4 6.5 %all-to-all-start.1 = ((f32[32,2,256]{2,1,0:T(2,128)}), f32[32,2,256]{2,1,0:T(2,128)S(1)}, u32[]{:S(2)}, u32[]{:S(2)}) async-start(f32[32,2,256]{2,1,0:T(2,128)} %broadcast_in_dim.223), calls=%async_computation.1 | async-start | bytes 131072 | tf_op jit(solution)/shard_map/all_to_all | solution.py:26
  56.1 8.7 %all-to-all-done.1 = f32[32,2,256]{2,1,0:T(2,128)S(1)} async-done(((f32[32,2,256]{2,1,0:T(2,128)}), f32[32,2,256]{2,1,0:T(2,128)S(1)}, u32[]{:S(2)}, u32[]{:S(2)}) %all-to-all-start.1) | async-done | bytes 65568 | tf_op jit(solution)/shard_map/all_to_all | solution.py:26
  65.4 11.5 %collective-permute-done.1 = bf16[2304,2,64]{0,2,1:T(8,128)(2,1)S(1)} collective-permute-done((bf16[2304,2,64]{0,2,1:T(8,128)(2,1)S(1)}, bf16[2304,2,64]{0,2,1:T(8,128)(2,1)S(1)}, u32[]{:S(2)}, u32[]{:S(2)}) %collective-permute-start.1) | collective-permute-done | bytes 589856 | tf_op jit(solution)/shard_map/ppermute | solution.py:14
  77.1 1.2 slice.165
  78.8 1.3 collective-permute-start.2
  80.6 2.3 collective-permute-done
  82.9 2.7 collective-permute-done.2
  85.9 41.7 %all-gather.5.cloned.1.call-done = bf16[16384,2,128]{0,2,1:T(8,128)(2,1)} async-done(((bf16[2048,2,128]{0,2,1:T(8,128)(2,1)}), bf16[16384,2,128]{0,2,1:T(8,128)(2,1)}) %all-gather.5.cloned.1.call-update) | async-done | bytes 8388624 | tf_op jit(solution)/shard_map/all_gather | solution.py:173
  127.6 1.6 fusion.140
  129.2 1.8 fusion.141
  131.0 1.5 fusion.142
  132.5 1.5 fusion.143
  133.9 1.5 fusion.144
  135.4 1.5 fusion.145
  144.1 1.4 collective-permute-start.3
  145.6 1.2 collective-permute-done.3
  146.8 1.4 fusion
  148.3 9.7 %all-to-all-start.2 = ((bf16[32,8,2048]{2,1,0:T(8,128)(2,1)}), bf16[32,8,2048]{2,1,0:T(8,128)(2,1)S(1)}, u32[]{:S(2)}, u32[]{:S(2)}) async-start(bf16[32,8,2048]{2,1,0:T(8,128)(2,1)} %fusion), calls=%async_computation.2 | async-start | bytes 2097152 | tf_op jit(solution)/shard_map/all_to_all | solution.py:193
  158.7 25.1 %all-to-all-done.2 = bf16[32,8,2048]{2,1,0:T(8,128)(2,1)S(1)} async-done(((bf16[32,8,2048]{2,1,0:T(8,128)(2,1)}), bf16[32,8,2048]{2,1,0:T(8,128)(2,1)S(1)}, u32[]{:S(2)}, u32[]{:S(2)}) %all-to-all-start.2) | async-done | bytes 1048608 | tf_op jit(solution)/shard_map/all_to_all | solution.py:193
  184.8 21.2 %all_to_all.26 = bf16[32,2,2,2048]{3,2,1,0:T(2,128)(2,1)} all-to-all(bf16[32,2,2,2048]{3,2,1,0:T(2,128)(2,1)S(1)} %reshape.904), channel_id=1, replica_groups=mesh['seq'=8,'tensor'=32] {'tensor'}, dimensions={0} | all-to-all | bytes 1048576 | tf_op jit(solution)/shard_map/all_to_all | solution.py:217
  206.2 33.2 %all-gather.7.cloned.1.call-done = bf16[256,2,2,2048]{3,2,1,0:T(2,128)(2,1)} async-done(((bf16[32,2,2,2048]{3,2,1,0:T(2,128)(2,1)}), bf16[256,2,2,2048]{3,2,1,0:T(2,128)(2,1)}) %all-gather.7.cloned.1.call-update) | async-done | bytes 4194320 | tf_op jit(solution)/shard_map/all_gather | solution.py:223
  239.4 3.7 %constant_dynamic-slice_fusion = bf16[8,32,1,2,2048]{4,3,2,1,0:T(2,128)(2,1)S(1)} fusion(bf16[8,32,2,2,2048]{4,3,2,1,0:T(2,128)(2,1)} %bitcast.149, s32[]{:T(128)S(6)} %select_n.189), kind=kLoop, calls=%fused_computation.191 | loop fusion | bytes 4194308 | tf_op jit(solution)/shard_map/jit(dynamic_index_in_dim)/dynamic_slice | solution.py:222
  243.1 1.3 copy-done.2
  244.4 2.8 fusion.11
  247.2 4.3 %fusion.15 = bf16[8,32,2,2048]{3,1,2,0:T(8,128)(2,1)S(1)} fusion(bf16[8,32,1,2,2048]{4,3,2,1,0:T(2,128)(2,1)} %copy-done.2, bf16[1,256,2048]{2,1,0:T(8,128)(2,1)S(1)} %copy-done, bf16[1,2048,256]{2,1,0:T(8,128)(2,1)} %param.32, f32[8,32,2,256]{3,1,2,0:T(8,128)} %fusion.11), kind=kOutput, calls=%fused_computation.31 | convolution fusion | flops 1074528256 | bytes 6815744 | tf_op jit(solution)/shard_map/srcf,fd->srcd/dot_general | solution.py:228
  251.5 3.0 select_convert_fusion
  254.5 40.7 %reduce-scatter.2.cloned.1.call-done = bf16[1,32,2,2,2048]{4,1,3,2,0:T(8,128)(2,1)} async-done(((bf16[8,32,2,2,2048]{4,1,3,2,0:T(8,128)(2,1)}), bf16[1,32,2,2,2048]{4,1,3,2,0:T(8,128)(2,1)}) %reduce-scatter.2.cloned.1.call-update) | async-done | bytes 524304 | tf_op jit(solution)/shard_map/reduce_scatter | solution.py:230
  295.2 2.4 copy.45
  297.6 9.4 %all-to-all-start.4 = ((bf16[32,2,2,2048]{3,2,1,0:T(2,128)(2,1)}), bf16[32,2,2,2048]{3,2,1,0:T(2,128)(2,1)S(1)}, u32[]{:S(2)}, u32[]{:S(2)}) async-start(bf16[32,2,2,2048]{3,2,1,0:T(2,128)(2,1)} %copy.45), calls=%async_computation.5 | async-start | bytes 1048576 | tf_op jit(solution)/shard_map/all_to_all | solution.py:233
  307.1 17.2 %all-to-all-done.4 = bf16[32,2,2,2048]{3,2,1,0:T(2,128)(2,1)S(1)} async-done(((bf16[32,2,2,2048]{3,2,1,0:T(2,128)(2,1)}), bf16[32,2,2,2048]{3,2,1,0:T(2,128)(2,1)S(1)}, u32[]{:S(2)}, u32[]{:S(2)}) %all-to-all-start.4) | async-done | bytes 524320 | tf_op jit(solution)/shard_map/all_to_all | solution.py:233
  (111 shorter events, 15.5 us)
Async XLA Ops:
  7.2 240.0 %copy-start = (bf16[1,256,2048]{2,1,0:T(8,128)(2,1)S(1)}, bf16[1,256,2048]{2,1,0:T(8,128)(2,1)}, u32[]{:S(2)}) copy-start(bf16[1,256,2048]{2,1,0:T(8,128)(2,1)} %param.33) | copy-start | bytes 3145732
  7.2 48.8 %copy-start.14 = (bf16[64]{0:T(256)(128)(2,1)S(1)}, bf16[64]{0:T(256)(128)(2,1)}, u32[]{:S(2)}) copy-start(bf16[64]{0:T(256)(128)(2,1)} %param.20) | copy-start | bytes 388
  7.2 48.8 %copy-start.15 = (bf16[64]{0:T(256)(128)(2,1)S(1)}, bf16[64]{0:T(256)(128)(2,1)}, u32[]{:S(2)}) copy-start(bf16[64]{0:T(256)(128)(2,1)} %param.21) | copy-start | bytes 388
  7.2 57.7 %copy-start.5 = (bf16[1,2048,64]{1,2,0:T(8,128)(2,1)S(1)}, bf16[1,2048,64]{1,2,0:T(8,128)(2,1)}, u32[]{:S(2)}) copy-start(bf16[1,2048,64]{1,2,0:T(8,128)(2,1)} %param.23) | copy-start | bytes 786436
  7.2 57.7 %copy-start.6 = (bf16[1,2048,64]{1,2,0:T(8,128)(2,1)S(1)}, bf16[1,2048,64]{1,2,0:T(8,128)(2,1)}, u32[]{:S(2)}) copy-start(bf16[1,2048,64]{1,2,0:T(8,128)(2,1)} %param.24) | copy-start | bytes 786436
  49.4 29.0 %copy-start.9 = (s32[2048]{0:T(1024)S(1)}, s32[2048]{0:T(1024)}, u32[]{:S(2)}) copy-start(s32[2048]{0:T(1024)} %param.25) | copy-start | bytes 24580
  49.4 29.0 %copy-start.13 = (s32[32]{0:T(128)S(1)}, s32[32]{0:T(128)}, u32[]{:S(2)}) copy-start(s32[32]{0:T(128)} %param.26) | copy-start | bytes 388
  49.4 15.3 %all-to-all-start.1 = ((f32[32,2,256]{2,1,0:T(2,128)}), f32[32,2,256]{2,1,0:T(2,128)S(1)}, u32[]{:S(2)}, u32[]{:S(2)}) async-start(f32[32,2,256]{2,1,0:T(2,128)} %broadcast_in_dim.223), calls=%async_computation.1 | async-start | bytes 131072 | tf_op jit(solution)/shard_map/all_to_all | solution.py:26
  55.9 22.8 %copy-start.16 = (s32[4]{0:T(128)S(1)}, s32[4]{0:T(128)}, u32[]{:S(2)}) copy-start(s32[4]{0:T(128)} %param.27) | copy-start | bytes 52
  55.9 71.7 %all-gather.5.cloned.1.call-start = ((), (), s32[]{:S(2)}) async-start(), calls=%async_computation.7 | async-start | bytes 9437184 | tf_op jit(solution)/shard_map/all_gather | solution.py:173
  56.0 22.8 %copy-start.8 = (bf16[256,64]{0,1:T(8,128)(2,1)}, bf16[256,64]{0,1:T(8,128)(2,1)S(1)}, u32[]{:S(2)}) copy-start(bf16[256,64]{0,1:T(8,128)(2,1)S(1)} %slice.239) | copy-start | bytes 98308
  64.9 15.3 %copy-start.7 = (bf16[256,64]{0,1:T(8,128)(2,1)}, bf16[256,64]{0,1:T(8,128)(2,1)S(1)}, u32[]{:S(2)}) copy-start(bf16[256,64]{0,1:T(8,128)(2,1)S(1)} %get-tuple-element.25) | copy-start | bytes 98308
  65.1 11.8 %collective-permute-start.1 = (bf16[2304,2,64]{0,2,1:T(8,128)(2,1)S(1)}, bf16[2304,2,64]{0,2,1:T(8,128)(2,1)S(1)}, u32[]{:S(2)}, u32[]{:S(2)}) collective-permute-start(bf16[2304,2,64]{0,2,1:T(8,128)(2,1)S(1)} %pad_maximum_fusion), channel_id=1, source_target_pairs={{0,1},{1,0},{2,3},{3,2},{4,5},{5,4},{6,7},{7,6},{8,9},{9,8},{10,11... | collective-permute-start | bytes 1769480 | tf_op jit(solution)/shard_map/ppermute | solution.py:14
  78.8 6.7 %collective-permute-start.2 = (bf16[256,2,128]{0,2,1:T(8,128)(2,1)S(1)}, bf16[256,2,128]{0,2,1:T(8,128)(2,1)S(1)}, u32[]{:S(2)}, u32[]{:S(2)}) collective-permute-start(bf16[256,2,128]{0,2,1:T(8,128)(2,1)S(1)} %slice.162), channel_id=1, source_target_pairs={{0,32},{32,64},{64,96},{96,128},{128,160},{160,192},{192,224},{1,3... | collective-permute-start | bytes 393224 | tf_op jit(solution)/shard_map/ppermute | solution.py:20
  80.2 2.7 collective-permute-start
  127.6 9.3 %copy-start.1 = (bf16[16384,2,128]{0,2,1:T(8,128)(2,1)S(1)}, bf16[16384,2,128]{0,2,1:T(8,128)(2,1)}, u32[]{:S(2)}) copy-start(bf16[16384,2,128]{0,2,1:T(8,128)(2,1)} %all-gather.5.cloned.1.call-done) | copy-start | bytes 25165828
  142.5 4.3 %copy-start.4 = (bf16[64,2048]{1,0:T(8,128)(2,1)S(1)}, bf16[64,2048]{1,0:T(8,128)(2,1)}, u32[]{:S(2)}) copy-start(bf16[64,2048]{1,0:T(8,128)(2,1)} %param.22) | copy-start | bytes 786436
  143.3 14.8 %copy-start.10 = (s32[8,8]{1,0:T(8,128)S(1)}, s32[8,8]{1,0:T(8,128)}, u32[]{:S(2)}) copy-start(s32[8,8]{1,0:T(8,128)} %param.29) | copy-start | bytes 772
  143.3 15.3 %copy-start.11 = (bf16[2048]{0:T(1024)(128)(2,1)S(1)}, bf16[2048]{0:T(1024)(128)(2,1)}, u32[]{:S(2)}) copy-start(bf16[2048]{0:T(1024)(128)(2,1)} %param.28) | copy-start | bytes 12292
  143.3 40.7 %copy-start.3 = (bf16[8,2048]{1,0:T(8,128)(2,1)S(1)}, bf16[8,2048]{1,0:T(8,128)(2,1)}, u32[]{:S(2)}) copy-start(bf16[8,2048]{1,0:T(8,128)(2,1)} %param.17) | copy-start | bytes 98308
  144.1 2.7 collective-permute-start.3
  148.3 35.6 %all-to-all-start.2 = ((bf16[32,8,2048]{2,1,0:T(8,128)(2,1)}), bf16[32,8,2048]{2,1,0:T(8,128)(2,1)S(1)}, u32[]{:S(2)}, u32[]{:S(2)}) async-start(bf16[32,8,2048]{2,1,0:T(8,128)(2,1)} %fusion), calls=%async_computation.2 | async-start | bytes 2097152 | tf_op jit(solution)/shard_map/all_to_all | solution.py:193
  158.0 81.3 %all-gather.7.cloned.1.call-start = ((), (), s32[]{:S(2)}) async-start(), calls=%async_computation.8 | async-start | bytes 4718592 | tf_op jit(solution)/shard_map/all_gather | solution.py:223
  206.1 89.1 %reduce-scatter.2.cloned.1.call-start = ((), (), s32[]{:S(2)}) async-start(), calls=%async_computation.6 | async-start | bytes 4718592 | tf_op jit(solution)/shard_map/reduce_scatter | solution.py:230
  243.1 1.4 copy-start.2
  254.5 52.5 %copy-start.12 = (f32[8,8]{1,0:T(8,128)S(1)}, f32[8,8]{1,0:T(8,128)}, u32[]{:S(2)}) copy-start(f32[8,8]{1,0:T(8,128)} %param.30) | copy-start | bytes 772
  297.6 26.7 %all-to-all-start.4 = ((bf16[32,2,2,2048]{3,2,1,0:T(2,128)(2,1)}), bf16[32,2,2,2048]{3,2,1,0:T(2,128)(2,1)S(1)}, u32[]{:S(2)}, u32[]{:S(2)}) async-start(bf16[32,2,2,2048]{3,2,1,0:T(2,128)(2,1)} %copy.45), calls=%async_computation.5 | async-start | bytes 1048576 | tf_op jit(solution)/shard_map/all_to_all | solution.py:233
Sparse Core Ops, SparseCore 0:
  78.5 49.0 all-gather.4
  206.2 33.1 all-gather.6
  254.6 40.5 reduce-scatter.1

commit v2 on v1

--- a/solution.py
+++ b/solution.py
@@ -83,6 +83,15 @@
     width = tokens.shape[1]
     tok_seq = tok_dev * tensor_size
     columns = w_qkv.shape[2]
+    lower_bit = tensor_index % 2
+    prefix_own = jnp.stack([prefix_keys[0], prefix_values[0]], axis=1)
+    prefix_partner = from_partner(prefix_own, "tensor", 0)
+    prefix_full = jnp.where(
+        lower_bit == 0,
+        jnp.concatenate([prefix_own, prefix_partner], axis=-1),
+        jnp.concatenate([prefix_partner, prefix_own], axis=-1),
+    )
+    piece = lax.all_gather(prefix_full[None], "seq", axis=0, tiled=True)
     normed = rms_scale(tokens.astype(jnp.float32), attn_gain).astype(jnp.bfloat16)
     w_flat = w_qkv.reshape(width, 3 * columns)
     projected = jnp.dot(
@@ -103,17 +112,10 @@
         key_part * lax.rsqrt(squares[1] / width + 1e-05)[:, None] * k_gain.astype(jnp.float32)
     ).astype(jnp.bfloat16)
     new_values = projected[:, 2 * columns :].astype(jnp.bfloat16)
-    stacked = jnp.stack(
-        [
-            jnp.concatenate([new_keys, prefix_keys[0]], axis=0),
-            jnp.concatenate([new_values, prefix_values[0]], axis=0),
-        ],
-        axis=1,
-    )
+    stacked = jnp.stack([new_keys, new_values], axis=1)
     half_rows = tok_seq // 2
-    lower_bit = tensor_index % 2
     partner = from_partner(stacked, "tensor", 0)
-    full = jnp.where(
+    suffix_full = jnp.where(
         lower_bit == 0,
         jnp.concatenate([stacked, partner], axis=-1),
         jnp.concatenate([partner, stacked], axis=-1),
@@ -129,8 +131,6 @@
     )
     query_offset = lower_bit * half_rows
     heads_local = 1
-    suffix_full = full[:tok_seq]
-    prefix_full = full[tok_seq:]
     queries_heads = query_full.reshape(half_rows, heads_local, HD)
     groups_count = prefix_owner.shape[0]
     request_count = request_group.shape[0]
@@ -170,7 +170,6 @@
         axis=1,
     )
     state = carry
-    piece = lax.all_gather(prefix_full[None], "seq", axis=0, tiled=True)
     start = jnp.int32(0)
     for offset in range(piece.shape[0]):
         slot_mask = (owner_of_query == start + offset)[:, None]

time: 333 us -> 287 us (0.86)
  blocking collectives: 58.4 us -> 20.3 us
  waiting for transfers between devices: 184 us -> 175 us
  matrix products: 25.3 us -> 16.6 us
  starting transfers between devices: 29.1 us -> 35.4 us
  local copies, waits for them, and re-layouts: 10.4 us -> 16 us
    all_gather x1, waiting for transfers between devices: 41.7 us -> 0.02 us  [local(): piece = lax.all_gather(prefix_full[None], 'seq', axis=0, tiled=True)]
    all_to_all x1 -> x0, blocking collectives: 37.2 us -> none  [gather_by_exchange(): got = lax.all_to_all(copies, axis, 0, 0, tiled=True)]
    all_to_all x1 -> x2, waiting for transfers between devices: 8.7 us -> 34.2 us  [gather_by_exchange(): got = lax.all_to_all(copies, axis, 0, 0, tiled=True)]
    all_to_all x1 -> x2, starting transfers between devices: 6.51 us -> 17.8 us  [gather_by_exchange(): got = lax.all_to_all(copies, axis, 0, 0, tiled=True)]
    dot_general x9, matrix products: 10.4 us -> 3.64 us  [attend_block(): jnp.einsum('qhd,khd->hqk', queries_heads, key_block, preferred_element_ty...]
    all_gather x1, waiting for transfers between devices: 33.2 us -> 39.7 us  [local(): lax.all_gather(received[None], 'seq', axis=0, tiled=True)]
    all_to_all x1, starting transfers between devices: 9.74 us -> 3.93 us  [local(): lax.all_to_all(attn_partial, 'tensor', 0, 0, tiled=True).astype(jnp.float32)]
    ppermute x3 -> x4, waiting for transfers between devices: 15 us -> 18.8 us  [from_partner(): return lax.ppermute(value, axis, pairs)]
  transfers between devices with their start and end apart: 10 -> 12, of which waited for: 10 -> 11; matrix products, arithmetic and copies ran while one was open for 0% -> 2% of each run, Pallas kernels for 0% -> 0%
where the time goes in v2:
time: 287 us; the launch traced here: 286 us
  waiting for transfers between devices  175 us (61%)
  starting transfers between devices  35.4 us (12%)
  blocking collectives  20.3 us (7%)
  matrix products  16.6 us (6%)
  local copies, waits for them, and re-layouts  16 us (6%)
  between operations  14.3 us (5%)
  other arithmetic  8.9 us (3%)
    reduce_scatter x1, waiting for transfers between devices, local(): lax.psum_scatter(partials.astype(jnp.bfloat16), 'seq', scatter_dimension=...  40.7 us
    all_gather x1, waiting for transfers between devices, local(): lax.all_gather(received[None], 'seq', axis=0, tiled=True)  39.7 us
    all_to_all x2, waiting for transfers between devices, gather_by_exchange(): got = lax.all_to_all(copies, axis, 0, 0, tiled=True)  34.2 us
    all_to_all x1, waiting for transfers between devices, local(): lax.all_to_all(attn_partial, 'tensor', 0, 0, tiled=True).astype(jnp.float32)  21.6 us
    all_to_all x1, blocking collectives, local(): lax.all_to_all(buffer, 'tensor', split_axis=0, concat_axis=0, tiled=True)  20.3 us
    ppermute x4, waiting for transfers between devices, from_partner(): return lax.ppermute(value, axis, pairs)  18.8 us
    all_to_all x2, starting transfers between devices, gather_by_exchange(): got = lax.all_to_all(copies, axis, 0, 0, tiled=True)  17.8 us
    all_to_all x1, waiting for transfers between devices, local(): lax.all_to_all(summed[0].astype(jnp.bfloat16), 'tensor', split_axis=0, co...  16.6 us
  transfers between devices with their start and end apart: 12, of which 11 were waited for; matrix products, arithmetic and copies ran while one was open for 2% of the time, Pallas kernels for 0%

profile of v2, /device:TPU:7, one launch (start us, length us, event | category | flops | bytes accessed | tf_op | source)
XLA Modules:
  0.0 286.1 jit_solution(7223962524962361193)
XLA Ops:
  7.2 1.2 fusion.137
  8.4 1.4 collective-permute-start.3
  9.8 11.5 %collective-permute-done.3 = bf16[2048,2,64]{0,2,1:T(8,128)(2,1)S(1)} collective-permute-done((bf16[2048,2,64]{0,2,1:T(8,128)(2,1)S(1)}, bf16[2048,2,64]{0,2,1:T(8,128)(2,1)S(1)}, u32[]{:S(2)}, u32[]{:S(2)}) %collective-permute-start.3) | collective-permute-done | bytes 524320 | tf_op jit(solution)/shard_map/ppermute | solution.py:14
  21.6 1.4 copy.50
  23.3 1.1 broadcast_in_dim.220
  24.4 11.2 %all-to-all-start = ((bf16[32,8,2048]{2,1,0:T(8,128)(2,1)}), bf16[32,8,2048]{2,1,0:T(8,128)(2,1)S(1)}, u32[]{:S(2)}, u32[]{:S(2)}) async-start(bf16[32,8,2048]{2,1,0:T(8,128)(2,1)} %broadcast_in_dim.220), calls=%async_computation | async-start | bytes 2097152 | tf_op jit(solution)/shard_map/all_to_all | solution.py:26
  36.0 25.3 %all-to-all-done = bf16[32,8,2048]{2,1,0:T(8,128)(2,1)S(1)} async-done(((bf16[32,8,2048]{2,1,0:T(8,128)(2,1)}), bf16[32,8,2048]{2,1,0:T(8,128)(2,1)S(1)}, u32[]{:S(2)}, u32[]{:S(2)}) %all-to-all-start) | async-done | bytes 1048608 | tf_op jit(solution)/shard_map/all_to_all | solution.py:26
  61.9 0.6 broadcast_in_dim.221
  62.5 6.6 %all-to-all-start.1 = ((f32[32,2,256]{2,1,0:T(2,128)}), f32[32,2,256]{2,1,0:T(2,128)S(1)}, u32[]{:S(2)}, u32[]{:S(2)}) async-start(f32[32,2,256]{2,1,0:T(2,128)} %broadcast_in_dim.221), calls=%async_computation.1 | async-start | bytes 131072 | tf_op jit(solution)/shard_map/all_to_all | solution.py:26
  69.2 8.9 %all-to-all-done.1 = f32[32,2,256]{2,1,0:T(2,128)S(1)} async-done(((f32[32,2,256]{2,1,0:T(2,128)}), f32[32,2,256]{2,1,0:T(2,128)S(1)}, u32[]{:S(2)}, u32[]{:S(2)}) %all-to-all-start.1) | async-done | bytes 65568 | tf_op jit(solution)/shard_map/all_to_all | solution.py:26
  78.7 2.7 collective-permute-done.1
  81.4 1.3 collective-permute-start.2
  83.5 2.2 collective-permute-done
  85.7 2.9 %collective-permute-done.2 = bf16[256,2,128]{0,2,1:T(8,128)(2,1)S(1)} collective-permute-done((bf16[256,2,128]{0,2,1:T(8,128)(2,1)S(1)}, bf16[256,2,128]{0,2,1:T(8,128)(2,1)S(1)}, u32[]{:S(2)}, u32[]{:S(2)}) %collective-permute-start.2) | collective-permute-done | bytes 131104 | tf_op jit(solution)/shard_map/ppermute | solution.py:20
  89.0 3.7 %slice_bitcast_fusion.7 = (bf16[2048,2,128]{2,0,1:T(8,128)(2,1)S(1)}, bf16[2048,2,128]{2,0,1:T(8,128)(2,1)S(1)}, bf16[2048,2,128]{2,0,1:T(8,128)(2,1)S(1)}, bf16...) fusion(bf16[8,2048,2,128]{3,1,2,0:T(8,128)(2,1)} %all-gather.4., ...), kind=kLoop, calls=%fused_computation.57 | loop fusion | bytes 16777216 | tf_op jit(solution)/shard_map/squeeze | solution.py:176
  103.2 2.3 collective-permute-done.4
  105.5 1.4 fusion
  107.0 3.9 %all-to-all-start.2 = ((bf16[32,8,2048]{2,1,0:T(8,128)(2,1)}), bf16[32,8,2048]{2,1,0:T(8,128)(2,1)S(1)}, u32[]{:S(2)}, u32[]{:S(2)}) async-start(bf16[32,8,2048]{2,1,0:T(8,128)(2,1)} %fusion), calls=%async_computation.2 | async-start | bytes 2097152 | tf_op jit(solution)/shard_map/all_to_all | solution.py:192
  111.6 21.6 %all-to-all-done.2 = bf16[32,8,2048]{2,1,0:T(8,128)(2,1)S(1)} async-done(((bf16[32,8,2048]{2,1,0:T(8,128)(2,1)}), bf16[32,8,2048]{2,1,0:T(8,128)(2,1)S(1)}, u32[]{:S(2)}, u32[]{:S(2)}) %all-to-all-start.2) | async-done | bytes 1048608 | tf_op jit(solution)/shard_map/all_to_all | solution.py:192
  134.3 20.3 %all_to_all.25 = bf16[32,2,2,2048]{3,2,1,0:T(2,128)(2,1)} all-to-all(bf16[32,2,2,2048]{3,2,1,0:T(2,128)(2,1)S(1)} %reshape.959), channel_id=1, replica_groups=mesh['seq'=8,'tensor'=32] {'tensor'}, dimensions={0} | all-to-all | bytes 1048576 | tf_op jit(solution)/shard_map/all_to_all | solution.py:216
  154.9 39.7 %all-gather.6.cloned.1.call-done = bf16[256,2,2,2048]{3,2,1,0:T(2,128)(2,1)} async-done(((bf16[32,2,2,2048]{3,2,1,0:T(2,128)(2,1)}), bf16[256,2,2,2048]{3,2,1,0:T(2,128)(2,1)}) %all-gather.6.cloned.1.call-update) | async-done | bytes 4194320 | tf_op jit(solution)/shard_map/all_gather | solution.py:222
  194.7 3.8 %constant_dynamic-slice_fusion = bf16[8,32,1,2,2048]{4,3,2,1,0:T(2,128)(2,1)S(1)} fusion(bf16[8,32,2,2,2048]{4,3,2,1,0:T(2,128)(2,1)} %bitcast.158, s32[]{:T(128)S(6)} %select_n.206), kind=kLoop, calls=%fused_computation.199 | loop fusion | bytes 4194308 | tf_op jit(solution)/shard_map/jit(dynamic_index_in_dim)/dynamic_slice | solution.py:221
  198.5 1.3 copy-done.1
  199.8 1.6 fusion.11
  201.4 4.3 %fusion.15 = bf16[8,32,2,2048]{3,1,2,0:T(8,128)(2,1)S(1)} fusion(bf16[8,32,1,2,2048]{4,3,2,1,0:T(2,128)(2,1)} %copy-done.1, bf16[1,256,2048]{2,1,0:T(8,128)(2,1)S(1)} %copy-done, bf16[1,2048,256]{2,1,0:T(8,128)(2,1)} %param.32, f32[8,32,2,256]{3,1,2,0:T(8,128)} %fusion.11), kind=kOutput, calls=%fused_computation.30 | convolution fusion | flops 1074528256 | bytes 6815744 | tf_op jit(solution)/shard_map/srcf,fd->srcd/dot_general | solution.py:227
  205.7 3.0 %select_convert_fusion = bf16[8,32,2,2,2048]{4,1,3,2,0:T(8,128)(2,1)} fusion(bf16[8,32,2,2048]{3,1,2,0:T(8,128)(2,1)S(1)} %fusion.15, pred[2]{0:T(512)(128)(4,1)S(1)} %iota_compare_fusion.4), kind=kLoop, calls=%fused_computation | loop fusion | flops 2097152 | bytes 6291458 | tf_op jit(solution)/shard_map/convert_element_type | solution.py:230
  208.7 40.7 %reduce-scatter.2.cloned.1.call-done = bf16[1,32,2,2,2048]{4,1,3,2,0:T(8,128)(2,1)} async-done(((bf16[8,32,2,2,2048]{4,1,3,2,0:T(8,128)(2,1)}), bf16[1,32,2,2,2048]{4,1,3,2,0:T(8,128)(2,1)}) %reduce-scatter.2.cloned.1.call-update) | async-done | bytes 524304 | tf_op jit(solution)/shard_map/reduce_scatter | solution.py:229
  249.4 2.4 copy.52
  251.7 9.4 %all-to-all-start.4 = ((bf16[32,2,2,2048]{3,2,1,0:T(2,128)(2,1)}), bf16[32,2,2,2048]{3,2,1,0:T(2,128)(2,1)S(1)}, u32[]{:S(2)}, u32[]{:S(2)}) async-start(bf16[32,2,2,2048]{3,2,1,0:T(2,128)(2,1)} %copy.52), calls=%async_computation.5 | async-start | bytes 1048576 | tf_op jit(solution)/shard_map/all_to_all | solution.py:232
  261.3 0.6 slice.221
  261.9 16.6 %all-to-all-done.4 = bf16[32,2,2,2048]{3,2,1,0:T(2,128)(2,1)S(1)} async-done(((bf16[32,2,2,2048]{3,2,1,0:T(2,128)(2,1)}), bf16[32,2,2,2048]{3,2,1,0:T(2,128)(2,1)S(1)}, u32[]{:S(2)}, u32[]{:S(2)}) %all-to-all-start.4) | async-done | bytes 524320 | tf_op jit(solution)/shard_map/all_to_all | solution.py:232
  278.6 0.9 fusion.9
  (114 shorter events, 15.8 us)
Async XLA Ops:
  7.2 194.2 %copy-start = (bf16[1,256,2048]{2,1,0:T(8,128)(2,1)S(1)}, bf16[1,256,2048]{2,1,0:T(8,128)(2,1)}, u32[]{:S(2)}) copy-start(bf16[1,256,2048]{2,1,0:T(8,128)(2,1)} %param.33) | copy-start | bytes 3145732
  7.2 81.8 %all-gather.4.cloned.1.call-start = ((), (), s32[]{:S(2)}) async-start(), calls=%async_computation.6 | async-start | bytes 9437184 | tf_op jit(solution)/shard_map/all_gather | solution.py:94
  8.4 12.9 %collective-permute-start.3 = (bf16[2048,2,64]{0,2,1:T(8,128)(2,1)S(1)}, bf16[2048,2,64]{0,2,1:T(8,128)(2,1)S(1)}, u32[]{:S(2)}, u32[]{:S(2)}) collective-permute-start(bf16[2048,2,64]{0,2,1:T(8,128)(2,1)S(1)} %get-tuple-element.33), channel_id=1, source_target_pairs={{0,1},{1,0},{2,3},{3,2},{4,5},{5,4},{6,7},{7,6},{8,9},{9,8},{10,11... | collective-permute-start | bytes 1572872 | tf_op jit(solution)/shard_map/ppermute | solution.py:14
  21.6 1.5 copy-start.8
  21.6 1.5 copy-start.3
  23.0 12.7 %copy-start.13 = (bf16[64]{0:T(256)(128)(2,1)S(1)}, bf16[64]{0:T(256)(128)(2,1)}, u32[]{:S(2)}) copy-start(bf16[64]{0:T(256)(128)(2,1)} %param.20) | copy-start | bytes 388
  23.0 12.7 %copy-start.14 = (bf16[64]{0:T(256)(128)(2,1)S(1)}, bf16[64]{0:T(256)(128)(2,1)}, u32[]{:S(2)}) copy-start(bf16[64]{0:T(256)(128)(2,1)} %param.21) | copy-start | bytes 388
  23.0 12.7 %copy-start.6 = (s32[2048]{0:T(1024)S(1)}, s32[2048]{0:T(1024)}, u32[]{:S(2)}) copy-start(s32[2048]{0:T(1024)} %param.25) | copy-start | bytes 24580
  23.0 12.7 %copy-start.11 = (s32[32]{0:T(128)S(1)}, s32[32]{0:T(128)}, u32[]{:S(2)}) copy-start(s32[32]{0:T(128)} %param.26) | copy-start | bytes 388
  23.0 12.9 %copy-start.15 = (s32[4]{0:T(128)S(1)}, s32[4]{0:T(128)}, u32[]{:S(2)}) copy-start(s32[4]{0:T(128)} %param.27) | copy-start | bytes 52
  23.0 38.3 %copy-start.2 = (bf16[2048,3,64]{0,2,1:T(8,128)(2,1)S(1)}, bf16[2048,3,64]{0,2,1:T(8,128)(2,1)}, u32[]{:S(2)}) copy-start(bf16[2048,3,64]{0,2,1:T(8,128)(2,1)} %param.19) | copy-start | bytes 2359300
  24.4 37.0 %all-to-all-start = ((bf16[32,8,2048]{2,1,0:T(8,128)(2,1)}), bf16[32,8,2048]{2,1,0:T(8,128)(2,1)S(1)}, u32[]{:S(2)}, u32[]{:S(2)}) async-start(bf16[32,8,2048]{2,1,0:T(8,128)(2,1)} %broadcast_in_dim.220), calls=%async_computation | async-start | bytes 2097152 | tf_op jit(solution)/shard_map/all_to_all | solution.py:26
  62.5 15.5 %all-to-all-start.1 = ((f32[32,2,256]{2,1,0:T(2,128)}), f32[32,2,256]{2,1,0:T(2,128)S(1)}, u32[]{:S(2)}, u32[]{:S(2)}) async-start(f32[32,2,256]{2,1,0:T(2,128)} %broadcast_in_dim.221), calls=%async_computation.1 | async-start | bytes 131072 | tf_op jit(solution)/shard_map/all_to_all | solution.py:26
  78.2 14.5 %copy-start.4 = (bf16[256,64]{0,1:T(8,128)(2,1)}, bf16[256,64]{0,1:T(8,128)(2,1)S(1)}, u32[]{:S(2)}) copy-start(bf16[256,64]{0,1:T(8,128)(2,1)S(1)} %get-tuple-element.35) | copy-start | bytes 98308
  78.2 3.2 %collective-permute-start.1 = (bf16[256,2,64]{0,2,1:T(8,128)(2,1)S(1)}, bf16[256,2,64]{0,2,1:T(8,128)(2,1)S(1)}, u32[]{:S(2)}, u32[]{:S(2)}) collective-permute-start(bf16[256,2,64]{0,2,1:T(8,128)(2,1)S(1)} %pad_maximum_fusion.2), channel_id=1, source_target_pairs={{0,1},{1,0},{2,3},{3,2},{4,5},{5,4},{6,7},{7,6},{8,9},{9,8},{10,11... | collective-permute-start | bytes 196616 | tf_op jit(solution)/shard_map/ppermute | solution.py:14
  81.4 7.2 %collective-permute-start.2 = (bf16[256,2,128]{0,2,1:T(8,128)(2,1)S(1)}, bf16[256,2,128]{0,2,1:T(8,128)(2,1)S(1)}, u32[]{:S(2)}, u32[]{:S(2)}) collective-permute-start(bf16[256,2,128]{0,2,1:T(8,128)(2,1)S(1)} %maximum_select_fusion.1), channel_id=1, source_target_pairs={{0,32},{32,64},{64,96},{96,128},{128,160},{160,192},{192,224},{1,3... | collective-permute-start | bytes 393224 | tf_op jit(solution)/shard_map/ppermute | solution.py:20
  82.8 2.9 collective-permute-start
  101.9 3.6 %copy-start.5 = (bf16[64,2048]{1,0:T(8,128)(2,1)S(1)}, bf16[64,2048]{1,0:T(8,128)(2,1)}, u32[]{:S(2)}) copy-start(bf16[64,2048]{1,0:T(8,128)(2,1)} %param.22) | copy-start | bytes 786436
  102.8 8.2 %copy-start.7 = (s32[8,8]{1,0:T(8,128)S(1)}, s32[8,8]{1,0:T(8,128)}, u32[]{:S(2)}) copy-start(s32[8,8]{1,0:T(8,128)} %param.29) | copy-start | bytes 772
  102.8 8.2 %copy-start.9 = (bf16[2048]{0:T(1024)(128)(2,1)S(1)}, bf16[2048]{0:T(1024)(128)(2,1)}, u32[]{:S(2)}) copy-start(bf16[2048]{0:T(1024)(128)(2,1)} %param.28) | copy-start | bytes 12292
  102.9 2.7 collective-permute-start.4
  107.0 26.3 %all-to-all-start.2 = ((bf16[32,8,2048]{2,1,0:T(8,128)(2,1)}), bf16[32,8,2048]{2,1,0:T(8,128)(2,1)S(1)}, u32[]{:S(2)}, u32[]{:S(2)}) async-start(bf16[32,8,2048]{2,1,0:T(8,128)(2,1)} %fusion), calls=%async_computation.2 | async-start | bytes 2097152 | tf_op jit(solution)/shard_map/all_to_all | solution.py:192
  110.9 83.7 %all-gather.6.cloned.1.call-start = ((), (), s32[]{:S(2)}) async-start(), calls=%async_computation.8 | async-start | bytes 4718592 | tf_op jit(solution)/shard_map/all_gather | solution.py:222
  154.6 94.8 %reduce-scatter.2.cloned.1.call-start = ((), (), s32[]{:S(2)}) async-start(), calls=%async_computation.7 | async-start | bytes 4718592 | tf_op jit(solution)/shard_map/reduce_scatter | solution.py:229
  194.7 5.1 %copy-start.12 = (bf16[1,2048,256]{2,1,0:T(8,128)(2,1)S(1)}, bf16[1,2048,256]{2,1,0:T(8,128)(2,1)}, u32[]{:S(2)}) copy-start(bf16[1,2048,256]{2,1,0:T(8,128)(2,1)} %param.31) | copy-start | bytes 3145732
  198.4 1.4 copy-start.1
  208.7 52.5 %copy-start.10 = (f32[8,8]{1,0:T(8,128)S(1)}, f32[8,8]{1,0:T(8,128)}, u32[]{:S(2)}) copy-start(f32[8,8]{1,0:T(8,128)} %param.30) | copy-start | bytes 772
  251.7 26.7 %all-to-all-start.4 = ((bf16[32,2,2,2048]{3,2,1,0:T(2,128)(2,1)}), bf16[32,2,2,2048]{3,2,1,0:T(2,128)(2,1)S(1)}, u32[]{:S(2)}, u32[]{:S(2)}) async-start(bf16[32,2,2,2048]{3,2,1,0:T(2,128)(2,1)} %copy.52), calls=%async_computation.5 | async-start | bytes 1048576 | tf_op jit(solution)/shard_map/all_to_all | solution.py:232
Sparse Core Ops, SparseCore 0:
  23.2 54.5 all-gather.3
  154.7 39.8 all-gather.5
  208.8 40.5 reduce-scatter.1

commit v3 on v2

--- a/solution.py
+++ b/solution.py
@@ -217,20 +217,20 @@
     gate_local = w_gate[0]
     up_local = w_up[0]
     down_local = w_down[0]
-    keep_expert = (jnp.arange(exp_local, dtype=jnp.int32) == own_expert)[None, None, :, None, None]
-    chosen = lax.dynamic_index_in_dim(
-        lax.all_gather(received[None], "seq", axis=0, tiled=True), own_expert, 2, keepdims=False
-    )
+    holders = seq_size // exp_local
+    per_expert = jnp.transpose(received, (1, 0, 2, 3))
+    chosen = lax.all_to_all(jnp.repeat(per_expert, holders, axis=0), "seq", 0, 0, tiled=True)
     gated = jnp.einsum("srcd,df->srcf", chosen, gate_local, preferred_element_type=jnp.float32)
     upward = jnp.einsum("srcd,df->srcf", chosen, up_local, preferred_element_type=jnp.float32)
     activity = (jax.nn.silu(gated) * upward).astype(jnp.bfloat16)
     result = jnp.einsum("srcf,fd->srcd", activity, down_local, preferred_element_type=jnp.float32)
-    partials = jnp.where(keep_expert, result[:, :, None], 0.0)
-    summed = lax.psum_scatter(
-        partials.astype(jnp.bfloat16), "seq", scatter_dimension=0, tiled=True
-    ).astype(jnp.float32)
+    back = lax.all_to_all(result.astype(jnp.bfloat16), "seq", 0, 0, tiled=True)
+    summed = jnp.sum(
+        back.astype(jnp.float32).reshape((exp_local, holders) + back.shape[1:]), axis=1
+    )
+    summed = jnp.transpose(summed, (1, 0, 2, 3))
     returned = lax.all_to_all(
-        summed[0].astype(jnp.bfloat16), "tensor", split_axis=0, concat_axis=0, tiled=True
+        summed.astype(jnp.bfloat16), "tensor", split_axis=0, concat_axis=0, tiled=True
     ).astype(jnp.float32)
     moe_sum = jnp.dot(
         combine_table,

time: 287 us -> 266 us (0.927); the launches traced: 286 us -> 262 us
  waiting for transfers between devices: 175 us -> 92.3 us
  blocking collectives: 20.3 us -> 91.2 us
  local copies, waits for them, and re-layouts: 16 us -> 10.3 us
  starting transfers between devices: 35.4 us -> 30 us
    all_to_all x0 -> x2, blocking collectives: none -> 71 us  [the longest x1 40.3 us: local(): lax.all_to_all(jnp.repeat(per_expert, holders, axis=0), 'seq', 0, 0, tile...]
    reduce_scatter x1 -> x0, waiting for transfers between devices: 40.7 us -> none  [local(): lax.psum_scatter(partials.astype(jnp.bfloat16), 'seq', scatter_dimension=...]
    all_gather x1 -> x0, waiting for transfers between devices: 39.7 us -> none  [local(): lax.all_gather(received[None], 'seq', axis=0, tiled=True)]
    all_to_all x1, starting transfers between devices: 9.4 us -> 4.26 us  [local(): lax.all_to_all(summed.astype(jnp.bfloat16), 'tensor', split_axis=0, conca...]
    dynamic_slice x1 -> x0, local copies, waits for them, and re-layouts: 3.77 us -> none  [local(): lax.dynamic_index_in_dim(lax.all_gather(received[None], 'seq', axis=0, ti...]
    convert_element_type x1 -> x0, other arithmetic: 2.97 us -> none  [local(): partials.astype(jnp.bfloat16)]
  transfers between devices with their start and end apart: 12 -> 10, of which waited for: 11 -> 9; matrix products, arithmetic and copies ran while one was open for 2% -> 2% of each run, Pallas kernels for 0% -> 0%
where the time goes in v3:
time: 266 us; the launch traced here: 262 us
  waiting for transfers between devices  92.3 us (35%)
  blocking collectives  91.2 us (34%)
  starting transfers between devices  30 us (11%)
  matrix products  17.2 us (6%)
  between operations  14.5 us (5%)
  local copies, waits for them, and re-layouts  10.3 us (4%)
  other arithmetic  6.3 us (2%)
    all_to_all x1, blocking collectives, local(): lax.all_to_all(jnp.repeat(per_expert, holders, axis=0), 'seq', 0, 0, tile...  40.3 us
    all_to_all x2, waiting for transfers between devices, gather_by_exchange(): got = lax.all_to_all(copies, axis, 0, 0, tiled=True)  34.2 us
    all_to_all x1, blocking collectives, local(): back = lax.all_to_all(result.astype(jnp.bfloat16), 'seq', 0, 0, tiled=True)  30.7 us
    all_to_all x1, waiting for transfers between devices, local(): lax.all_to_all(attn_partial, 'tensor', 0, 0, tiled=True).astype(jnp.float32)  21.7 us
    all_to_all x1, blocking collectives, local(): lax.all_to_all(buffer, 'tensor', split_axis=0, concat_axis=0, tiled=True)  20.2 us
    ppermute x4, waiting for transfers between devices, from_partner(): return lax.ppermute(value, axis, pairs)  18.8 us
    all_to_all x2, starting transfers between devices, gather_by_exchange(): got = lax.all_to_all(copies, axis, 0, 0, tiled=True)  17.8 us
    all_to_all x1, waiting for transfers between devices, local(): lax.all_to_all(summed.astype(jnp.bfloat16), 'tensor', split_axis=0, conca...  14.6 us
  transfers between devices with their start and end apart: 10, of which 9 were waited for; matrix products, arithmetic and copies ran while one was open for 2% of the time, Pallas kernels for 0%

profile of v3, /device:TPU:7, one launch (start us, length us, event | category | flops | bytes accessed | tf_op | source)
XLA Modules:
  0.0 261.9 jit_solution(5647444806106926141)
XLA Ops:
  7.2 1.2 fusion.134
  8.4 1.4 collective-permute-start.3
  9.8 11.5 %collective-permute-done.3 = bf16[2048,2,64]{0,2,1:T(8,128)(2,1)S(1)} collective-permute-done((bf16[2048,2,64]{0,2,1:T(8,128)(2,1)S(1)}, bf16[2048,2,64]{0,2,1:T(8,128)(2,1)S(1)}, u32[]{:S(2)}, u32[]{:S(2)}) %collective-permute-start.3) | collective-permute-done | bytes 524320 | tf_op jit(solution)/shard_map/ppermute | solution.py:14
  21.6 1.4 copy.43
  23.3 1.1 broadcast_in_dim.198
  24.4 11.2 %all-to-all-start = ((bf16[32,8,2048]{2,1,0:T(8,128)(2,1)}), bf16[32,8,2048]{2,1,0:T(8,128)(2,1)S(1)}, u32[]{:S(2)}, u32[]{:S(2)}) async-start(bf16[32,8,2048]{2,1,0:T(8,128)(2,1)} %broadcast_in_dim.198), calls=%async_computation | async-start | bytes 2097152 | tf_op jit(solution)/shard_map/all_to_all | solution.py:26
  36.0 25.3 %all-to-all-done = bf16[32,8,2048]{2,1,0:T(8,128)(2,1)S(1)} async-done(((bf16[32,8,2048]{2,1,0:T(8,128)(2,1)}), bf16[32,8,2048]{2,1,0:T(8,128)(2,1)S(1)}, u32[]{:S(2)}, u32[]{:S(2)}) %all-to-all-start) | async-done | bytes 1048608 | tf_op jit(solution)/shard_map/all_to_all | solution.py:26
  61.3 0.5 fusion.27
  61.9 0.6 broadcast_in_dim.199
  62.5 6.6 %all-to-all-start.1 = ((f32[32,2,256]{2,1,0:T(2,128)}), f32[32,2,256]{2,1,0:T(2,128)S(1)}, u32[]{:S(2)}, u32[]{:S(2)}) async-start(f32[32,2,256]{2,1,0:T(2,128)} %broadcast_in_dim.199), calls=%async_computation.1 | async-start | bytes 131072 | tf_op jit(solution)/shard_map/all_to_all | solution.py:26
  69.2 8.9 %all-to-all-done.1 = f32[32,2,256]{2,1,0:T(2,128)S(1)} async-done(((f32[32,2,256]{2,1,0:T(2,128)}), f32[32,2,256]{2,1,0:T(2,128)S(1)}, u32[]{:S(2)}, u32[]{:S(2)}) %all-to-all-start.1) | async-done | bytes 65568 | tf_op jit(solution)/shard_map/all_to_all | solution.py:26
  78.7 2.7 %collective-permute-done.1 = bf16[256,2,64]{0,2,1:T(8,128)(2,1)S(1)} collective-permute-done((bf16[256,2,64]{0,2,1:T(8,128)(2,1)S(1)}, bf16[256,2,64]{0,2,1:T(8,128)(2,1)S(1)}, u32[]{:S(2)}, u32[]{:S(2)}) %collective-permute-start.1) | collective-permute-done | bytes 65568 | tf_op jit(solution)/shard_map/ppermute | solution.py:14
  81.4 1.3 collective-permute-start.2
  82.8 0.6 collective-permute-start
  83.5 2.2 collective-permute-done
  85.7 2.9 %collective-permute-done.2 = bf16[256,2,128]{0,2,1:T(8,128)(2,1)S(1)} collective-permute-done((bf16[256,2,128]{0,2,1:T(8,128)(2,1)S(1)}, bf16[256,2,128]{0,2,1:T(8,128)(2,1)S(1)}, u32[]{:S(2)}, u32[]{:S(2)}) %collective-permute-start.2) | collective-permute-done | bytes 131104 | tf_op jit(solution)/shard_map/ppermute | solution.py:20
  89.0 3.7 %slice_bitcast_fusion.7 = (bf16[2048,2,128]{2,0,1:T(8,128)(2,1)S(1)}, bf16[2048,2,128]{2,0,1:T(8,128)(2,1)S(1)}, bf16[2048,2,128]{2,0,1:T(8,128)(2,1)S(1)}, bf16...) fusion(bf16[8,2048,2,128]{3,1,2,0:T(8,128)(2,1)} %all-gather.2., ...), kind=kLoop, calls=%fused_computation.54 | loop fusion | bytes 16777216 | tf_op jit(solution)/shard_map/squeeze | solution.py:176
  99.2 0.4 fusion.19
  103.2 2.3 collective-permute-done.4
  105.5 1.4 fusion
  107.0 3.9 %all-to-all-start.2 = ((bf16[32,8,2048]{2,1,0:T(8,128)(2,1)}), bf16[32,8,2048]{2,1,0:T(8,128)(2,1)S(1)}, u32[]{:S(2)}, u32[]{:S(2)}) async-start(bf16[32,8,2048]{2,1,0:T(8,128)(2,1)} %fusion), calls=%async_computation.2 | async-start | bytes 2097152 | tf_op jit(solution)/shard_map/all_to_all | solution.py:192
  111.6 21.7 %all-to-all-done.2 = bf16[32,8,2048]{2,1,0:T(8,128)(2,1)S(1)} async-done(((bf16[32,8,2048]{2,1,0:T(8,128)(2,1)}), bf16[32,8,2048]{2,1,0:T(8,128)(2,1)S(1)}, u32[]{:S(2)}, u32[]{:S(2)}) %all-to-all-start.2) | async-done | bytes 1048608 | tf_op jit(solution)/shard_map/all_to_all | solution.py:192
  134.3 20.2 %all_to_all.35 = bf16[32,2,2,2048]{3,2,1,0:T(2,128)(2,1)S(1)} all-to-all(bf16[32,2,2,2048]{3,2,1,0:T(2,128)(2,1)S(1)} %reshape.962), channel_id=1, replica_groups=mesh['seq'=8,'tensor'=32] {'tensor'}, dimensions={0} | all-to-all | bytes 1048576 | tf_op jit(solution)/shard_map/all_to_all | solution.py:216
  155.0 40.3 %all_to_all.36 = bf16[8,32,2,2048]{3,1,2,0:T(8,128)(2,1)S(1)} all-to-all(bf16[8,32,2,2048]{3,1,2,0:T(8,128)(2,1)S(1)} %bitcast.153), channel_id=1, replica_groups=mesh['seq'=8,'tensor'=32] {'seq'}, dimensions={0} | all-to-all | bytes 4194304 | tf_op jit(solution)/shard_map/all_to_all | solution.py:222
  195.3 1.5 fusion.25
  196.8 5.0 %convolution_convert_fusion = bf16[8,32,2,2048]{3,1,2,0:T(8,128)(2,1)} fusion(bf16[8,32,2,2048]{3,1,2,0:T(8,128)(2,1)S(1)} %all_to_all.36, bf16[1,256,2048]{2,1,0:T(8,128)(2,1)S(1)} %copy-done, bf16[1,2048,256]{2,1,0:T(8,128)(2,1)} %param.32, f32[8,32,2,256]{3,1,2,0:T(8,128)} %fusion.25), kind=kOutput, calls=%fused_computation | convolution fusion | flops 1075576832 | bytes 6815744 | tf_op jit(solution)/shard_map/srcf,fd->srcd/dot_general | solution.py:226
  201.9 30.7 %all_to_all.37 = bf16[8,32,2,2048]{3,1,2,0:T(8,128)(2,1)S(1)} all-to-all(bf16[8,32,2,2048]{3,1,2,0:T(8,128)(2,1)} %convolution_convert_fusion), channel_id=1, replica_groups=mesh['seq'=8,'tensor'=32] {'seq'}, dimensions={0} | all-to-all | bytes 4194304 | tf_op jit(solution)/shard_map/all_to_all | solution.py:227
  233.0 1.3 copy.45
  234.3 4.3 %all-to-all-start.6 = ((bf16[32,2,2,2048]{3,2,1,0:T(2,128)(2,1)}), bf16[32,2,2,2048]{3,2,1,0:T(2,128)(2,1)S(1)}, u32[]{:S(2)}, u32[]{:S(2)}) async-start(bf16[32,2,2,2048]{3,2,1,0:T(2,128)(2,1)} %copy.45), calls=%async_computation.6 | async-start | bytes 1048576 | tf_op jit(solution)/shard_map/all_to_all | solution.py:232
  238.7 0.6 slice.221
  239.3 14.6 %all-to-all-done.6 = bf16[32,2,2,2048]{3,2,1,0:T(2,128)(2,1)S(1)} async-done(((bf16[32,2,2,2048]{3,2,1,0:T(2,128)(2,1)}), bf16[32,2,2,2048]{3,2,1,0:T(2,128)(2,1)S(1)}, u32[]{:S(2)}, u32[]{:S(2)}) %all-to-all-start.6) | async-done | bytes 524320 | tf_op jit(solution)/shard_map/all_to_all | solution.py:232
  254.1 0.9 fusion.9
  (108 shorter events, 14.9 us)
Async XLA Ops:
  7.2 189.7 %copy-start = (bf16[1,256,2048]{2,1,0:T(8,128)(2,1)S(1)}, bf16[1,256,2048]{2,1,0:T(8,128)(2,1)}, u32[]{:S(2)}) copy-start(bf16[1,256,2048]{2,1,0:T(8,128)(2,1)} %param.33) | copy-start | bytes 3145732
  7.2 81.8 %all-gather.2.cloned.1.call-start = ((), (), s32[]{:S(2)}) async-start(), calls=%async_computation.7 | async-start | bytes 9437184 | tf_op jit(solution)/shard_map/all_gather | solution.py:94
  8.4 12.9 %collective-permute-start.3 = (bf16[2048,2,64]{0,2,1:T(8,128)(2,1)S(1)}, bf16[2048,2,64]{0,2,1:T(8,128)(2,1)S(1)}, u32[]{:S(2)}, u32[]{:S(2)}) collective-permute-start(bf16[2048,2,64]{0,2,1:T(8,128)(2,1)S(1)} %get-tuple-element.33), channel_id=1, source_target_pairs={{0,1},{1,0},{2,3},{3,2},{4,5},{5,4},{6,7},{7,6},{8,9},{9,8},{10,11... | collective-permute-start | bytes 1572872 | tf_op jit(solution)/shard_map/ppermute | solution.py:14
  21.6 1.5 copy-start.7
  21.6 1.5 copy-start.2
  23.0 12.7 %copy-start.12 = (bf16[64]{0:T(256)(128)(2,1)S(1)}, bf16[64]{0:T(256)(128)(2,1)}, u32[]{:S(2)}) copy-start(bf16[64]{0:T(256)(128)(2,1)} %param.20) | copy-start | bytes 388
  23.0 12.7 %copy-start.13 = (bf16[64]{0:T(256)(128)(2,1)S(1)}, bf16[64]{0:T(256)(128)(2,1)}, u32[]{:S(2)}) copy-start(bf16[64]{0:T(256)(128)(2,1)} %param.21) | copy-start | bytes 388
  23.0 12.7 %copy-start.5 = (s32[2048]{0:T(1024)S(1)}, s32[2048]{0:T(1024)}, u32[]{:S(2)}) copy-start(s32[2048]{0:T(1024)} %param.25) | copy-start | bytes 24580
  23.0 12.7 %copy-start.10 = (s32[32]{0:T(128)S(1)}, s32[32]{0:T(128)}, u32[]{:S(2)}) copy-start(s32[32]{0:T(128)} %param.26) | copy-start | bytes 388
  23.0 12.9 %copy-start.14 = (s32[4]{0:T(128)S(1)}, s32[4]{0:T(128)}, u32[]{:S(2)}) copy-start(s32[4]{0:T(128)} %param.27) | copy-start | bytes 52
  23.0 38.3 %copy-start.1 = (bf16[2048,3,64]{0,2,1:T(8,128)(2,1)S(1)}, bf16[2048,3,64]{0,2,1:T(8,128)(2,1)}, u32[]{:S(2)}) copy-start(bf16[2048,3,64]{0,2,1:T(8,128)(2,1)} %param.19) | copy-start | bytes 2359300
  24.4 37.0 %all-to-all-start = ((bf16[32,8,2048]{2,1,0:T(8,128)(2,1)}), bf16[32,8,2048]{2,1,0:T(8,128)(2,1)S(1)}, u32[]{:S(2)}, u32[]{:S(2)}) async-start(bf16[32,8,2048]{2,1,0:T(8,128)(2,1)} %broadcast_in_dim.198), calls=%async_computation | async-start | bytes 2097152 | tf_op jit(solution)/shard_map/all_to_all | solution.py:26
  62.5 15.5 %all-to-all-start.1 = ((f32[32,2,256]{2,1,0:T(2,128)}), f32[32,2,256]{2,1,0:T(2,128)S(1)}, u32[]{:S(2)}, u32[]{:S(2)}) async-start(f32[32,2,256]{2,1,0:T(2,128)} %broadcast_in_dim.199), calls=%async_computation.1 | async-start | bytes 131072 | tf_op jit(solution)/shard_map/all_to_all | solution.py:26
  78.2 14.5 %copy-start.3 = (bf16[256,64]{0,1:T(8,128)(2,1)}, bf16[256,64]{0,1:T(8,128)(2,1)S(1)}, u32[]{:S(2)}) copy-start(bf16[256,64]{0,1:T(8,128)(2,1)S(1)} %get-tuple-element.35) | copy-start | bytes 98308
  78.2 3.2 %collective-permute-start.1 = (bf16[256,2,64]{0,2,1:T(8,128)(2,1)S(1)}, bf16[256,2,64]{0,2,1:T(8,128)(2,1)S(1)}, u32[]{:S(2)}, u32[]{:S(2)}) collective-permute-start(bf16[256,2,64]{0,2,1:T(8,128)(2,1)S(1)} %pad_maximum_fusion.2), channel_id=1, source_target_pairs={{0,1},{1,0},{2,3},{3,2},{4,5},{5,4},{6,7},{7,6},{8,9},{9,8},{10,11... | collective-permute-start | bytes 196616 | tf_op jit(solution)/shard_map/ppermute | solution.py:14
  81.4 7.2 %collective-permute-start.2 = (bf16[256,2,128]{0,2,1:T(8,128)(2,1)S(1)}, bf16[256,2,128]{0,2,1:T(8,128)(2,1)S(1)}, u32[]{:S(2)}, u32[]{:S(2)}) collective-permute-start(bf16[256,2,128]{0,2,1:T(8,128)(2,1)S(1)} %maximum_select_fusion.1), channel_id=1, source_target_pairs={{0,32},{32,64},{64,96},{96,128},{128,160},{160,192},{192,224},{1,3... | collective-permute-start | bytes 393224 | tf_op jit(solution)/shard_map/ppermute | solution.py:20
  82.8 2.9 %collective-permute-start = (bf16[128,64]{0,1:T(8,128)(2,1)S(1)}, bf16[128,64]{0,1:T(8,128)(2,1)S(1)}, u32[]{:S(2)}, u32[]{:S(2)}) collective-permute-start(bf16[128,64]{0,1:T(8,128)(2,1)S(1)} %bitcast.172), channel_id=1, source_target_pairs={{0,1},{1,0},{2,3},{3,2},{4,5},{5,4},{6,7},{7,6},{8,9},{9,8},{10,11... | collective-permute-start | bytes 49160 | tf_op jit(solution)/shard_map/ppermute | solution.py:14
  101.9 3.6 %copy-start.4 = (bf16[64,2048]{1,0:T(8,128)(2,1)S(1)}, bf16[64,2048]{1,0:T(8,128)(2,1)}, u32[]{:S(2)}) copy-start(bf16[64,2048]{1,0:T(8,128)(2,1)} %param.22) | copy-start | bytes 786436
  102.8 8.1 %copy-start.6 = (s32[8,8]{1,0:T(8,128)S(1)}, s32[8,8]{1,0:T(8,128)}, u32[]{:S(2)}) copy-start(s32[8,8]{1,0:T(8,128)} %param.29) | copy-start | bytes 772
  102.8 8.2 %copy-start.8 = (bf16[2048]{0:T(1024)(128)(2,1)S(1)}, bf16[2048]{0:T(1024)(128)(2,1)}, u32[]{:S(2)}) copy-start(bf16[2048]{0:T(1024)(128)(2,1)} %param.28) | copy-start | bytes 12292
  102.9 2.7 %collective-permute-start.4 = (bf16[128,64]{0,1:T(8,128)(2,1)S(1)}, bf16[128,64]{0,1:T(8,128)(2,1)S(1)}, u32[]{:S(2)}, u32[]{:S(2)}) collective-permute-start(bf16[128,64]{0,1:T(8,128)(2,1)S(1)} %get-tuple-element.37), channel_id=1, source_target_pairs={{0,1},{1,0},{2,3},{3,2},{4,5},{5,4},{6,7},{7,6},{8,9},{9,8},{10,11... | collective-permute-start | bytes 49160 | tf_op jit(solution)/shard_map/ppermute | solution.py:14
  107.0 26.3 %all-to-all-start.2 = ((bf16[32,8,2048]{2,1,0:T(8,128)(2,1)}), bf16[32,8,2048]{2,1,0:T(8,128)(2,1)S(1)}, u32[]{:S(2)}, u32[]{:S(2)}) async-start(bf16[32,8,2048]{2,1,0:T(8,128)(2,1)} %fusion), calls=%async_computation.2 | async-start | bytes 2097152 | tf_op jit(solution)/shard_map/all_to_all | solution.py:192
  155.0 40.3 %copy-start.11 = (bf16[1,2048,256]{2,1,0:T(8,128)(2,1)S(1)}, bf16[1,2048,256]{2,1,0:T(8,128)(2,1)}, u32[]{:S(2)}) copy-start(bf16[1,2048,256]{2,1,0:T(8,128)(2,1)} %param.31) | copy-start | bytes 3145732
  232.6 6.0 %copy-start.9 = (f32[8,8]{1,0:T(8,128)S(1)}, f32[8,8]{1,0:T(8,128)}, u32[]{:S(2)}) copy-start(f32[8,8]{1,0:T(8,128)} %param.30) | copy-start | bytes 772
  234.3 19.6 %all-to-all-start.6 = ((bf16[32,2,2,2048]{3,2,1,0:T(2,128)(2,1)}), bf16[32,2,2,2048]{3,2,1,0:T(2,128)(2,1)S(1)}, u32[]{:S(2)}, u32[]{:S(2)}) async-start(bf16[32,2,2,2048]{3,2,1,0:T(2,128)(2,1)} %copy.45), calls=%async_computation.6 | async-start | bytes 1048576 | tf_op jit(solution)/shard_map/all_to_all | solution.py:232
Sparse Core Ops, SparseCore 0:
  23.2 54.5 all-gather.1

commit v4 on v3

v4 whole, which is shorter than its diff:
```python
import jax
import jax.numpy as jnp
from jax import lax
from jax.sharding import Mesh
from jax.sharding import PartitionSpec as P

HD = 128
TOP = 8
EXP_DEV = 2
HEADS_AXES = ("tz", "tyh")
TENSOR = ("tz", "tyh", "tyl")


def passed_along(value, axis, by):
    devices = lax.axis_size(axis)
    pairs = [(i, i + by) for i in range(devices) if 0 <= i + by < devices]
    return lax.ppermute(value, axis, pairs)


def from_partner(value):
    return lax.ppermute(value, "tyl", [(0, 1), (1, 0)])


def gather_by_exchange(value, axis):
    devices = lax.axis_size(axis)
    copies = jnp.broadcast_to(value[None], (devices,) + value.shape)
    return lax.all_to_all(copies, axis, 0, 0, tiled=True)


def rms_scale(values, gain):
    mean_square = jnp.mean(values * values, axis=-1, keepdims=True)
    return values * lax.rsqrt(mean_square + 1e-05) * gain.astype(jnp.float32)


def attend_block(carry, queries_heads, block, mask):
    largest, total, accum = carry
    heads_local = queries_heads.shape[1]
    count = block.shape[0]
    key_block = block[:, 0].reshape(count, heads_local, HD)
    value_block = block[:, 1].reshape(count, heads_local, HD)
    scores = jnp.einsum(
        "qhd,khd->hqk", queries_heads, key_block, preferred_element_type=jnp.float32
    ) * HD ** (-0.5)
    scores = jnp.where(mask[None], scores, -1e30)
    new_largest = jnp.maximum(largest, jnp.max(scores, axis=-1))
    weights = jnp.where(mask[None], jnp.exp(scores - new_largest[:, :, None]), 0.0)
    factor = jnp.exp(largest - new_largest)
    total = total * factor + jnp.sum(weights, axis=-1)
    update = jnp.einsum(
        "hqk,khd->hqd",
        weights.astype(jnp.bfloat16),
        value_block,
        preferred_element_type=jnp.float32,
    )
    accum = accum * factor[:, :, None] + update
    return (new_largest, total, accum)


def local(
    tokens,
    attn_gain,
    w_qkv,
    q_gain,
    k_gain,
    w_out,
    prefix_keys,
    prefix_values,
    segments,
    request_group,
    prefix_owner,
    mlp_gain,
    expert_ids,
    gate_weights,
    w_gate,
    w_up,
    w_down,
):
    tensor_size = lax.axis_size(TENSOR)
    heads_count = lax.axis_size(HEADS_AXES)
    seq_size = lax.axis_size("seq")
    seq_index = lax.axis_index("seq")
    parity = lax.axis_index("tyl")
    tok_dev = tokens.shape[0]
    width = tokens.shape[1]
    tok_seq = tok_dev * tensor_size
    columns = w_qkv.shape[2]
    rows_half = tok_dev * heads_count

    def join(own, other, axis):
        return jnp.where(
            parity == 0,
            jnp.concatenate([own, other], axis=axis),
            jnp.concatenate([other, own], axis=axis),
        )

    prefix_own = jnp.stack([prefix_keys[0], prefix_values[0]], axis=1)
    piece = lax.all_gather(prefix_own[None], ("seq", "tyl"), axis=0, tiled=True)
    piece = piece.reshape((seq_size, 2) + prefix_own.shape)
    piece = jnp.transpose(piece, (0, 2, 3, 1, 4)).reshape(
        (seq_size,) + prefix_own.shape[:2] + (2 * columns,)
    )
    w_head = join(w_qkv, from_partner(w_qkv), 2)
    out_head = join(w_out, from_partner(w_out), 0)
    gain_pair = jnp.stack([q_gain, k_gain])
    gains = join(gain_pair, from_partner(gain_pair), 1).astype(jnp.float32)

    normed = rms_scale(tokens.astype(jnp.float32), attn_gain).astype(jnp.bfloat16)
    rows = gather_by_exchange(normed, HEADS_AXES).reshape(rows_half, width)
    projected = jnp.dot(
        rows, w_head.reshape(width, 3 * 2 * columns), preferred_element_type=jnp.float32
    ).reshape(rows_half, 3, 2 * columns)
    query_part = projected[:, 0]
    key_part = projected[:, 1]
    partial_squares = jnp.stack(
        [jnp.sum(query_part * query_part, axis=-1), jnp.sum(key_part * key_part, axis=-1)]
    )
    squares = jnp.sum(gather_by_exchange(partial_squares, HEADS_AXES), axis=0)
    queries = (
        query_part * lax.rsqrt(squares[0] / width + 1e-05)[:, None] * gains[0]
    ).astype(jnp.bfloat16)
    keys = (key_part * lax.rsqrt(squares[1] / width + 1e-05)[:, None] * gains[1]).astype(
        jnp.bfloat16
    )
    values = projected[:, 2].astype(jnp.bfloat16)
    own_kv = jnp.stack([keys, values], axis=1)
    other_kv = from_partner(own_kv)
    kv_shape = (heads_count, 1, tok_dev, 2, 2 * columns)
    suffix_full = join(own_kv.reshape(kv_shape), other_kv.reshape(kv_shape), 1).reshape(
        tok_seq, 2, 2 * columns
    )
    own_cols = jnp.where(parity == 0, suffix_full[..., :columns], suffix_full[..., columns:])
    new_keys = own_cols[:, 0]
    new_values = own_cols[:, 1]

    groups_count = prefix_owner.shape[0]
    request_count = request_group.shape[0]
    token_group = jnp.sum(
        jnp.where(
            segments[:, None] == jnp.arange(request_count, dtype=jnp.int32)[None, :],
            request_group[None, :],
            0,
        ),
        axis=1,
    )
    base_row = seq_index * tok_seq
    seq_segments = lax.dynamic_slice_in_dim(segments, base_row, tok_seq, 0)
    seq_groups = lax.dynamic_slice_in_dim(token_group, base_row, tok_seq, 0)

    def own_rows(values_of_seq):
        halves = values_of_seq.reshape(heads_count, 2, tok_dev)
        return jnp.where(parity == 0, halves[:, 0], halves[:, 1]).reshape(rows_half)

    query_seg = own_rows(seq_segments)
    query_group = own_rows(seq_groups)
    query_pos = own_rows(base_row + jnp.arange(tok_seq, dtype=jnp.int32))
    padded_seg = jnp.concatenate([jnp.full((tok_seq,), -1, jnp.int32), segments], axis=0)
    key_seg = lax.dynamic_slice_in_dim(padded_seg, base_row, 2 * tok_seq, 0)
    key_pos = base_row - tok_seq + jnp.arange(2 * tok_seq, dtype=jnp.int32)
    previous = passed_along(suffix_full, "seq", 1)
    suffix_keys = jnp.concatenate([previous, suffix_full], axis=0)
    suffix_mask = (key_seg[None, :] == query_seg[:, None]) & (
        key_pos[None, :] <= query_pos[:, None]
    )
    heads_local = 1
    queries_heads = queries.reshape(rows_half, heads_local, HD)
    carry = (
        jnp.full((heads_local, rows_half), -1e30, jnp.float32),
        jnp.zeros((heads_local, rows_half), jnp.float32),
        jnp.zeros((heads_local, rows_half, HD), jnp.float32),
    )
    carry = attend_block(carry, queries_heads, suffix_keys, suffix_mask)
    owner_of_query = jnp.sum(
        jnp.where(
            query_group[:, None] == jnp.arange(groups_count, dtype=jnp.int32)[None, :],
            prefix_owner[None, :],
            0,
        ),
        axis=1,
    )
    for slot in range(seq_size):
        slot_mask = (owner_of_query == slot)[:, None]
        carry = attend_block(carry, queries_heads, piece[slot], slot_mask)
    attended = (carry[2] / carry[1][:, :, None]).astype(jnp.bfloat16)
    attended = jnp.transpose(attended, (1, 0, 2)).reshape(rows_half, heads_local * HD)
    attn_partial = jnp.dot(attended, out_head, preferred_element_type=jnp.float32)
    attn_partial = attn_partial.astype(jnp.bfloat16).reshape(heads_count, tok_dev, width)
    attn_sum = jnp.sum(
        lax.all_to_all(attn_partial, HEADS_AXES, 0, 0, tiled=True).astype(jnp.float32), axis=0
    )
    mixed_rows = (tokens.astype(jnp.float32) + attn_sum).astype(jnp.bfloat16)
    expert_in = rms_scale(mixed_rows.astype(jnp.float32), mlp_gain).astype(jnp.bfloat16)
    exp_local = EXP_DEV
    experts_all = exp_local * tensor_size
    own_expert = seq_index // (seq_size // exp_local)
    capacity = max(2, 2 * tok_dev * TOP // experts_all)
    flat_ids = expert_ids.reshape(-1)
    onehot = (flat_ids[:, None] == jnp.arange(experts_all, dtype=jnp.int32)[None, :]).astype(
        jnp.int32
    )
    before = jnp.cumsum(onehot, axis=0) - onehot
    slot = flat_ids * capacity + jnp.sum(before * onehot, axis=1)
    slot_match = (
        slot.reshape(tok_dev, TOP)[:, :, None]
        == jnp.arange(experts_all * capacity, dtype=jnp.int32)[None, None, :]
    )
    dispatch_table = jnp.transpose(jnp.any(slot_match, axis=1)).astype(jnp.bfloat16)
    combine_table = jnp.sum(jnp.where(slot_match, gate_weights[:, :, None], 0.0), axis=1)
    buffer = jnp.dot(dispatch_table, expert_in, preferred_element_type=jnp.float32).astype(
        jnp.bfloat16
    )
    buffer = buffer.reshape(tensor_size, exp_local, capacity, width)
    received = lax.all_to_all(buffer, TENSOR, split_axis=0, concat_axis=0, tiled=True)
    gate_local = w_gate[0]
    up_local = w_up[0]
    down_local = w_down[0]
    holders = seq_size // exp_local
    per_expert = jnp.transpose(received, (1, 0, 2, 3))
    chosen = lax.all_to_all(jnp.repeat(per_expert, holders, axis=0), "seq", 0, 0, tiled=True)
    gated = jnp.einsum("srcd,df->srcf", chosen, gate_local, preferred_element_type=jnp.float32)
    upward = jnp.einsum("srcd,df->srcf", chosen, up_local, preferred_element_type=jnp.float32)
    activity = (jax.nn.silu(gated) * upward).astype(jnp.bfloat16)
    result = jnp.einsum("srcf,fd->srcd", activity, down_local, preferred_element_type=jnp.float32)
    back = lax.all_to_all(result.astype(jnp.bfloat16), "seq", 0, 0, tiled=True)
    summed = jnp.sum(
        back.astype(jnp.float32).reshape((exp_local, holders) + back.shape[1:]), axis=1
    )
    summed = jnp.transpose(summed, (1, 0, 2, 3))
    returned = lax.all_to_all(
        summed.astype(jnp.bfloat16), TENSOR, split_axis=0, concat_axis=0, tiled=True
    ).astype(jnp.float32)
    moe_sum = jnp.dot(
        combine_table,
        returned.reshape(experts_all * capacity, width),
        preferred_element_type=jnp.float32,
        precision=lax.Precision.HIGHEST,
    )
    output = (mixed_rows.astype(jnp.float32) + moe_sum).astype(jnp.bfloat16)
    return (output, new_keys, new_values)


def solution(mesh):
    seq_size, tensor_size = mesh.devices.shape
    tz = tensor_size // 4
    grid = Mesh(mesh.devices.reshape(seq_size, tz, 2, 2), ("seq",) + TENSOR)
    rows = ("seq",) + TENSOR
    return jax.shard_map(
        local,
        mesh=grid,
        in_specs=(
            P(rows, None),
            P(),
            P(None, None, TENSOR),
            P(TENSOR),
            P(TENSOR),
            P(TENSOR, None),
            P("seq", None, TENSOR),
            P("seq", None, TENSOR),
            P(),
            P(),
            P(),
            P(),
            P(rows, None),
            P(rows, None),
            P(TENSOR + ("seq",), None, None),
            P(TENSOR + ("seq",), None, None),
            P(TENSOR + ("seq",), None, None),
        ),
        out_specs=(P(rows, None), P("seq", TENSOR), P("seq", TENSOR)),
        check_vma=False,
    )
```

time: 266 us -> 291 us (1.094)
  local copies, waits for them, and re-layouts: 10.3 us -> 34.6 us
  blocking collectives: 91.2 us -> 81.4 us
  starting transfers between devices: 30 us -> 38.3 us
  waiting for transfers between devices: 92.3 us -> 88.7 us
  other arithmetic: 6.3 us -> 9.38 us
    all_to_all x4, waiting for transfers between devices: 70.5 us -> 40.5 us  [the longest x1 17.9 us: local(): lax.all_to_all(attn_partial, HEADS_AXES, 0, 0, tiled=True)]
    reshape x1 -> x3, local copies, waits for them, and re-layouts: 0.01 us -> 14.7 us  [the longest x1 14.5 us: local(): piece = piece.reshape((seq_size, 2) + prefix_own.shape)]
    ppermute x4, waiting for transfers between devices: 18.8 us -> 32.4 us  [from_partner(): return lax.ppermute(value, 'tyl', [(0, 1), (1, 0)])]
    slice x1 -> x11, local copies, waits for them, and re-layouts: 0.62 us -> 13.9 us  [the longest x9 13.9 us: local(): carry = attend_block(carry, queries_heads, piece[slot], slot_mask)]
    all_to_all x1, blocking collectives: 40.3 us -> 31.2 us  [local(): lax.all_to_all(jnp.repeat(per_expert, holders, axis=0), 'seq', 0, 0, tile...]
    all_gather x1, waiting for transfers between devices: 0.02 us -> 9 us  [local(): piece = lax.all_gather(prefix_own[None], ('seq', 'tyl'), axis=0, tiled=True)]
    all_to_all x4, starting transfers between devices: 26 us -> 33.3 us  [the longest x2 19.3 us: gather_by_exchange(): return lax.all_to_all(copies, axis, 0, 0, tiled=True)]
    ppermute x1, waiting for transfers between devices: 2.95 us -> 6.8 us  [passed_along(): return lax.ppermute(value, axis, pairs)]
  transfers between devices with their start and end apart: 10 -> 10, of which waited for: 9 -> 7; matrix products, arithmetic and copies ran while one was open for 2% -> 17% of each run, Pallas kernels for 0% -> 0%
where the time goes in v4:
time: 291 us; the launch traced here: 286 us
  waiting for transfers between devices  88.7 us (30%)
  blocking collectives  81.4 us (28%)
  starting transfers between devices  38.3 us (13%)
  local copies, waits for them, and re-layouts  34.6 us (12%)
  matrix products  19.3 us (7%)
  between operations  14.5 us (5%)
  other arithmetic  9.38 us (3%)
    ppermute x4, waiting for transfers between devices, from_partner(): return lax.ppermute(value, 'tyl', [(0, 1), (1, 0)])  32.4 us
    all_to_all x1, blocking collectives, local(): lax.all_to_all(jnp.repeat(per_expert, holders, axis=0), 'seq', 0, 0, tile...  31.2 us
    all_to_all x1, blocking collectives, local(): back = lax.all_to_all(result.astype(jnp.bfloat16), 'seq', 0, 0, tiled=True)  30.7 us
    all_to_all x1, blocking collectives, local(): lax.all_to_all(buffer, TENSOR, split_axis=0, concat_axis=0, tiled=True)  19.5 us
    all_to_all x2, starting transfers between devices, gather_by_exchange(): return lax.all_to_all(copies, axis, 0, 0, tiled=True)  19.3 us
    all_to_all x1, waiting for transfers between devices, local(): lax.all_to_all(attn_partial, HEADS_AXES, 0, 0, tiled=True)  17.9 us
    reshape x1, local copies, waits for them, and re-layouts, local(): piece = piece.reshape((seq_size, 2) + prefix_own.shape)  14.5 us
    slice x9, local copies, waits for them, and re-layouts, local(): carry = attend_block(carry, queries_heads, piece[slot], slot_mask)  13.9 us
  transfers between devices with their start and end apart: 10, of which 7 were waited for; matrix products, arithmetic and copies ran while one was open for 17% of the time, Pallas kernels for 0%

profile of v4, /device:TPU:7, one launch (start us, length us, event | category | flops | bytes accessed | tf_op | source)
XLA Modules:
  0.0 286.3 jit_solution(17284734955352048107)
XLA Ops:
  7.3 2.0 pad_maximum_fusion
  10.0 0.9 fusion.116
  10.9 0.8 fusion.118
  11.7 0.9 broadcast_in_dim.195
  12.6 10.9 %all-to-all-start = ((bf16[16,8,2048]{2,1,0:T(8,128)(2,1)}), bf16[16,8,2048]{2,1,0:T(8,128)(2,1)S(1)}, u32[]{:S(2)}, u32[]{:S(2)}) async-start(bf16[16,8,2048]{2,1,0:T(8,128)(2,1)} %broadcast_in_dim.195), calls=%async_computation | async-start | bytes 1048576 | tf_op jit(solution)/shard_map/all_to_all | solution.py:27
  24.0 1.2 collective-permute-start.1
  26.3 29.5 %collective-permute-done.1 = bf16[2,64]{1,0:T(2,128)(2,1)S(1)} collective-permute-done((bf16[2,64]{1,0:T(2,128)(2,1)S(1)}, bf16[2,64]{1,0:T(2,128)(2,1)S(1)}, u32[]{:S(2)}, u32[]{:S(2)}) %collective-permute-start.1) | collective-permute-done | bytes 288 | tf_op jit(solution)/shard_map/ppermute | solution.py:21
  56.0 2.0 fusion.11
  58.8 8.4 %all-to-all-start.1 = ((f32[16,2,128]{2,1,0:T(2,128)}), f32[16,2,128]{2,1,0:T(2,128)S(1)}, u32[]{:S(2)}, u32[]{:S(2)}) async-start(f32[16,2,128]{2,1,0:T(2,128)} %broadcast_in_dim.196), calls=%async_computation.1 | async-start | bytes 32768 | tf_op jit(solution)/shard_map/all_to_all | solution.py:27
  67.2 8.9 %all-to-all-done.1 = f32[16,2,128]{2,1,0:T(2,128)S(1)} async-done(((f32[16,2,128]{2,1,0:T(2,128)}), f32[16,2,128]{2,1,0:T(2,128)S(1)}, u32[]{:S(2)}, u32[]{:S(2)}) %all-to-all-start.1) | async-done | bytes 16416 | tf_op jit(solution)/shard_map/all_to_all | solution.py:27
  76.2 1.5 collective-permute-start.2
  77.7 2.9 %collective-permute-done.2 = bf16[128,2,128]{2,0,1:T(8,128)(2,1)S(1)} collective-permute-done((bf16[128,2,128]{2,0,1:T(8,128)(2,1)S(1)}, bf16[128,2,128]{2,0,1:T(8,128)(2,1)S(1)}, u32[]{:S(2)}, u32[]{:S(2)}) %collective-permute-start.2) | collective-permute-done | bytes 65568 | tf_op jit(solution)/shard_map/ppermute | solution.py:21
  80.6 1.5 collective-permute-start.3
  82.4 6.8 %collective-permute-done.3 = bf16[256,2,128]{2,0,1:T(8,128)(2,1)S(1)} collective-permute-done((bf16[256,2,128]{2,0,1:T(8,128)(2,1)S(1)}, bf16[256,2,128]{2,0,1:T(8,128)(2,1)S(1)}, u32[]{:S(2)}, u32[]{:S(2)}) %collective-permute-start.3) | collective-permute-done | bytes 131104 | tf_op jit(solution)/shard_map/ppermute | solution.py:17
  89.2 0.9 fusion.162
  90.2 9.0 %all-gather.3.cloned.1.call-done = bf16[32768,2,64]{0,2,1:T(8,128)(2,1)} async-done(((bf16[2048,2,64]{0,2,1:T(8,128)(2,1)}), bf16[32768,2,64]{0,2,1:T(8,128)(2,1)}) %all-gather.3.cloned.1.call-update) | async-done | bytes 8388624 | tf_op jit(solution)/shard_map/all_gather | solution.py:97
  99.2 14.5 %reshape.907 = bf16[8,2,2048,2,64]{2,1,0,4,3:T(2,128)(2,1)} reshape(bf16[32768,2,64]{0,2,1:T(8,128)(2,1)} %all-gather.3.cloned.1.call-done) | data formatting | bytes 16777216 | tf_op jit(solution)/shard_map/reshape | solution.py:98
  113.7 11.1 %fusion.153 = (bf16[1,2048,2,2,64]{1,3,0,4,2:T(2,128)(2,1)S(1)}, bf16[1,2048,2,2,64]{1,3,0,4,2:T(2,128)(2,1)S(1)}, bf16[1,2048,2,2,64]{1,3,0,4,2:T(2,128)(2,1)S(...) fusion(bf16[8,2048,2,2,64]{1,3,0,4,2:T(2,128)(2,1)} %bitcast.187), kind=kLoop, calls=%fused_computation.247 | loop fusion | bytes 16777216 | tf_op jit(solution)/shard_map/slice | solution.py:182
  136.5 2.7 fusion.8
  139.2 9.6 %all-to-all-start.2 = ((bf16[16,8,2048]{2,1,0:T(8,128)(2,1)}), bf16[16,8,2048]{2,1,0:T(8,128)(2,1)S(1)}, u32[]{:S(2)}, u32[]{:S(2)}) async-start(bf16[16,8,2048]{2,1,0:T(8,128)(2,1)} %fusion.8), calls=%async_computation.2 | async-start | bytes 1048576 | tf_op jit(solution)/shard_map/all_to_all | solution.py:188
  149.4 17.9 %all-to-all-done.2 = bf16[16,8,2048]{2,1,0:T(8,128)(2,1)S(1)} async-done(((bf16[16,8,2048]{2,1,0:T(8,128)(2,1)}), bf16[16,8,2048]{2,1,0:T(8,128)(2,1)S(1)}, u32[]{:S(2)}, u32[]{:S(2)}) %all-to-all-start.2) | async-done | bytes 524320 | tf_op jit(solution)/shard_map/all_to_all | solution.py:188
  168.3 19.5 %all_to_all.35 = bf16[32,2,2,2048]{3,2,1,0:T(2,128)(2,1)S(1)} all-to-all(bf16[32,2,2,2048]{3,2,1,0:T(2,128)(2,1)S(1)} %reshape.925), channel_id=1, replica_groups=mesh['seq'=8,'tz'=8,'tyh'=2,'tyl'=2] {'tz','tyh','tyl'}, dimensions={0} | all-to-all | bytes 1048576 | tf_op jit(solution)/shard_map/all_to_all | solution.py:212
  188.3 31.2 %all_to_all.36 = bf16[8,32,2,2048]{3,1,2,0:T(8,128)(2,1)S(1)} all-to-all(bf16[8,32,2,2048]{3,1,2,0:T(8,128)(2,1)S(1)} %bitcast.188), channel_id=1, replica_groups=mesh['seq'=8,'tz'=8,'tyh'=2,'tyl'=2] {'seq'}, dimensions={0} | all-to-all | bytes 4194304 | tf_op jit(solution)/shard_map/all_to_all | solution.py:218
  219.6 1.5 fusion.34
  221.1 5.0 %convolution_convert_fusion = bf16[8,32,2,2048]{3,1,2,0:T(8,128)(2,1)} fusion(bf16[8,32,2,2048]{3,1,2,0:T(8,128)(2,1)S(1)} %all_to_all.36, bf16[1,256,2048]{2,1,0:T(8,128)(2,1)S(1)} %copy-done, bf16[1,2048,256]{2,1,0:T(8,128)(2,1)} %param.32, f32[8,32,2,256]{3,1,2,0:T(8,128)} %fusion.34), kind=kOutput, calls=%fused_computation | convolution fusion | flops 1075576832 | bytes 6815744 | tf_op jit(solution)/shard_map/srcf,fd->srcd/dot_general | solution.py:222
  226.1 30.7 %all_to_all.37 = bf16[8,32,2,2048]{3,1,2,0:T(8,128)(2,1)S(1)} all-to-all(bf16[8,32,2,2048]{3,1,2,0:T(8,128)(2,1)} %convolution_convert_fusion), channel_id=1, replica_groups=mesh['seq'=8,'tz'=8,'tyh'=2,'tyl'=2] {'seq'}, dimensions={0} | all-to-all | bytes 4194304 | tf_op jit(solution)/shard_map/all_to_all | solution.py:223
  257.2 1.3 copy.202
  258.6 4.4 %all-to-all-start.6 = ((bf16[32,2,2,2048]{3,2,1,0:T(2,128)(2,1)}), bf16[32,2,2,2048]{3,2,1,0:T(2,128)(2,1)S(1)}, u32[]{:S(2)}, u32[]{:S(2)}) async-start(bf16[32,2,2,2048]{3,2,1,0:T(2,128)(2,1)} %copy.202), calls=%async_computation.6 | async-start | bytes 1048576 | tf_op jit(solution)/shard_map/all_to_all | solution.py:228
  263.2 0.7 copy.203
  263.9 0.7 copy.204
  264.6 13.7 %all-to-all-done.6 = bf16[32,2,2,2048]{3,2,1,0:T(2,128)(2,1)S(1)} async-done(((bf16[32,2,2,2048]{3,2,1,0:T(2,128)(2,1)}), bf16[32,2,2,2048]{3,2,1,0:T(2,128)(2,1)S(1)}, u32[]{:S(2)}, u32[]{:S(2)}) %all-to-all-start.6) | async-done | bytes 524320 | tf_op jit(solution)/shard_map/all_to_all | solution.py:228
  278.5 0.9 fusion.9
  (117 shorter events, 18.2 us)
Async XLA Ops:
  7.2 213.9 %copy-start = (bf16[1,256,2048]{2,1,0:T(8,128)(2,1)S(1)}, bf16[1,256,2048]{2,1,0:T(8,128)(2,1)}, u32[]{:S(2)}) copy-start(bf16[1,256,2048]{2,1,0:T(8,128)(2,1)} %param.33) | copy-start | bytes 3145732
  7.2 16.3 %copy-start.11 = (bf16[2048,3,64]{0,2,1:T(8,128)(2,1)S(1)}, bf16[2048,3,64]{0,2,1:T(8,128)(2,1)}, u32[]{:S(2)}) copy-start(bf16[2048,3,64]{0,2,1:T(8,128)(2,1)} %param.19) | copy-start | bytes 2359300
  7.2 16.8 %copy-start.9 = (bf16[64]{0:T(256)(128)(2,1)S(1)}, bf16[64]{0:T(256)(128)(2,1)}, u32[]{:S(2)}) copy-start(bf16[64]{0:T(256)(128)(2,1)} %param.20) | copy-start | bytes 388
  7.2 16.8 %copy-start.8 = (bf16[64]{0:T(256)(128)(2,1)S(1)}, bf16[64]{0:T(256)(128)(2,1)}, u32[]{:S(2)}) copy-start(bf16[64]{0:T(256)(128)(2,1)} %param.21) | copy-start | bytes 388
  7.2 18.4 %copy-start.3 = (s32[2048]{0:T(1024)S(1)}, s32[2048]{0:T(1024)}, u32[]{:S(2)}) copy-start(s32[2048]{0:T(1024)} %param.25) | copy-start | bytes 24580
  7.2 18.4 %copy-start.7 = (s32[32]{0:T(128)S(1)}, s32[32]{0:T(128)}, u32[]{:S(2)}) copy-start(s32[32]{0:T(128)} %param.26) | copy-start | bytes 388
  7.2 18.8 %copy-start.12 = (s32[4]{0:T(128)S(1)}, s32[4]{0:T(128)}, u32[]{:S(2)}) copy-start(s32[4]{0:T(128)} %param.27) | copy-start | bytes 52
  7.2 91.9 %all-gather.3.cloned.1.call-start = ((), (), s32[]{:S(2)}) async-start(), calls=%async_computation.7 | async-start | bytes 8912896 | tf_op jit(solution)/shard_map/all_gather | solution.py:97
  12.6 43.4 %all-to-all-start = ((bf16[16,8,2048]{2,1,0:T(8,128)(2,1)}), bf16[16,8,2048]{2,1,0:T(8,128)(2,1)S(1)}, u32[]{:S(2)}, u32[]{:S(2)}) async-start(bf16[16,8,2048]{2,1,0:T(8,128)(2,1)} %broadcast_in_dim.195), calls=%async_computation | async-start | bytes 1048576 | tf_op jit(solution)/shard_map/all_to_all | solution.py:27
  23.5 32.4 %collective-permute-start = (bf16[2048,3,64]{0,2,1:T(8,128)(2,1)S(1)}, bf16[2048,3,64]{0,2,1:T(8,128)(2,1)}, u32[]{:S(2)}, u32[]{:S(2)}) collective-permute-start(bf16[2048,3,64]{0,2,1:T(8,128)(2,1)S(1)} %copy-done.11), channel_id=1, source_target_pairs={{0,1},{1,0},{2,3},{3,2},{4,5},{5,4},{6,7},{7,6},{8,9},{9,8},{10,11... | collective-permute-start | bytes 2359304 | tf_op jit(solution)/shard_map/ppermute | solution.py:21
  24.0 31.8 %collective-permute-start.1 = (bf16[2,64]{1,0:T(2,128)(2,1)S(1)}, bf16[2,64]{1,0:T(2,128)(2,1)S(1)}, u32[]{:S(2)}, u32[]{:S(2)}) collective-permute-start(bf16[2,64]{1,0:T(2,128)(2,1)S(1)} %pad_maximum_fusion.4), channel_id=1, source_target_pairs={{0,1},{1,0},{2,3},{3,2},{4,5},{5,4},{6,7},{7,6},{8,9},{9,8},{10,11... | collective-permute-start | bytes 776 | tf_op jit(solution)/shard_map/ppermute | solution.py:21
  25.2 111.3 %collective-permute-start.4 = (bf16[64,2048]{1,0:T(8,128)(2,1)}, bf16[64,2048]{1,0:T(8,128)(2,1)}, u32[]{:S(2)}, u32[]{:S(2)}) collective-permute-start(bf16[64,2048]{1,0:T(8,128)(2,1)} %param.22), channel_id=1, source_target_pairs={{0,1},{1,0},{2,3},{3,2},{4,5},{5,4},{6,7},{7,6},{8,9},{9,8},{10,11... | collective-permute-start | bytes 786440 | tf_op jit(solution)/shard_map/ppermute | solution.py:21
  58.8 17.3 %all-to-all-start.1 = ((f32[16,2,128]{2,1,0:T(2,128)}), f32[16,2,128]{2,1,0:T(2,128)S(1)}, u32[]{:S(2)}, u32[]{:S(2)}) async-start(f32[16,2,128]{2,1,0:T(2,128)} %broadcast_in_dim.196), calls=%async_computation.1 | async-start | bytes 32768 | tf_op jit(solution)/shard_map/all_to_all | solution.py:27
  76.2 4.4 %collective-permute-start.2 = (bf16[128,2,128]{2,0,1:T(8,128)(2,1)S(1)}, bf16[128,2,128]{2,0,1:T(8,128)(2,1)S(1)}, u32[]{:S(2)}, u32[]{:S(2)}) collective-permute-start(bf16[128,2,128]{2,0,1:T(8,128)(2,1)S(1)} %pad_maximum_fusion.2), channel_id=1, source_target_pairs={{0,1},{1,0},{2,3},{3,2},{4,5},{5,4},{6,7},{7,6},{8,9},{9,8},{10,11... | collective-permute-start | bytes 196616 | tf_op jit(solution)/shard_map/ppermute | solution.py:21
  80.6 8.6 %collective-permute-start.3 = (bf16[256,2,128]{2,0,1:T(8,128)(2,1)S(1)}, bf16[256,2,128]{2,0,1:T(8,128)(2,1)S(1)}, u32[]{:S(2)}, u32[]{:S(2)}) collective-permute-start(bf16[256,2,128]{2,0,1:T(8,128)(2,1)S(1)} %bitcast.207), channel_id=1, source_target_pairs={{0,32},{32,64},{64,96},{96,128},{128,160},{160,192},{192,224},{1,3... | collective-permute-start | bytes 393224 | tf_op jit(solution)/shard_map/ppermute | solution.py:17
  129.5 1.2 copy-start.2
  136.5 12.3 %copy-start.4 = (s32[8,8]{1,0:T(8,128)S(1)}, s32[8,8]{1,0:T(8,128)}, u32[]{:S(2)}) copy-start(s32[8,8]{1,0:T(8,128)} %param.29) | copy-start | bytes 772
  136.5 12.8 %copy-start.5 = (bf16[2048]{0:T(1024)(128)(2,1)S(1)}, bf16[2048]{0:T(1024)(128)(2,1)}, u32[]{:S(2)}) copy-start(bf16[2048]{0:T(1024)(128)(2,1)} %param.28) | copy-start | bytes 12292
  136.5 30.9 %copy-start.1 = (bf16[8,2048]{1,0:T(8,128)(2,1)S(1)}, bf16[8,2048]{1,0:T(8,128)(2,1)}, u32[]{:S(2)}) copy-start(bf16[8,2048]{1,0:T(8,128)(2,1)} %param.17) | copy-start | bytes 98308
  139.2 28.1 %all-to-all-start.2 = ((bf16[16,8,2048]{2,1,0:T(8,128)(2,1)}), bf16[16,8,2048]{2,1,0:T(8,128)(2,1)S(1)}, u32[]{:S(2)}, u32[]{:S(2)}) async-start(bf16[16,8,2048]{2,1,0:T(8,128)(2,1)} %fusion.8), calls=%async_computation.2 | async-start | bytes 1048576 | tf_op jit(solution)/shard_map/all_to_all | solution.py:188
  188.3 31.2 %copy-start.10 = (bf16[1,2048,256]{2,1,0:T(8,128)(2,1)S(1)}, bf16[1,2048,256]{2,1,0:T(8,128)(2,1)}, u32[]{:S(2)}) copy-start(bf16[1,2048,256]{2,1,0:T(8,128)(2,1)} %param.31) | copy-start | bytes 3145732
  256.8 6.2 %copy-start.6 = (f32[8,8]{1,0:T(8,128)S(1)}, f32[8,8]{1,0:T(8,128)}, u32[]{:S(2)}) copy-start(f32[8,8]{1,0:T(8,128)} %param.30) | copy-start | bytes 772
  258.6 19.8 %all-to-all-start.6 = ((bf16[32,2,2,2048]{3,2,1,0:T(2,128)(2,1)}), bf16[32,2,2,2048]{3,2,1,0:T(2,128)(2,1)S(1)}, u32[]{:S(2)}, u32[]{:S(2)}) async-start(bf16[32,2,2,2048]{3,2,1,0:T(2,128)(2,1)} %copy.202), calls=%async_computation.6 | async-start | bytes 1048576 | tf_op jit(solution)/shard_map/all_to_all | solution.py:228
Sparse Core Ops, SparseCore 0:
  9.9 89.2 all-gather.2

commit v5 on v3

--- a/solution.py
+++ b/solution.py
@@ -92,42 +92,53 @@
         jnp.concatenate([prefix_partner, prefix_own], axis=-1),
     )
     piece = lax.all_gather(prefix_full[None], "seq", axis=0, tiled=True)
+    gains_in = from_partner(jnp.stack([q_gain, k_gain]), "tensor", 0)
     normed = rms_scale(tokens.astype(jnp.float32), attn_gain).astype(jnp.bfloat16)
     w_flat = w_qkv.reshape(width, 3 * columns)
+    rows = gather_by_exchange(normed, "tensor").reshape(tok_seq, width)
     projected = jnp.dot(
-        gather_by_exchange(normed, "tensor").reshape(tok_seq, width),
+        rows,
         w_flat,
         preferred_element_type=jnp.float32,
     )
     query_part = projected[:, :columns]
     key_part = projected[:, columns : 2 * columns]
+    value_part = projected[:, 2 * columns :]
     partial_squares = jnp.stack(
         [jnp.sum(query_part * query_part, axis=-1), jnp.sum(key_part * key_part, axis=-1)]
     )
+    half_rows = tok_seq // 2
+    query_halves = query_part.reshape(2, half_rows, columns)
+    own_half = lax.dynamic_index_in_dim(query_halves, lower_bit, 0, keepdims=False)
+    send_half = lax.dynamic_index_in_dim(query_halves, 1 - lower_bit, 0, keepdims=False)
+    raw_out = jnp.concatenate([send_half, key_part, value_part], axis=0)
+    raw_out, partial_squares = lax.optimization_barrier((raw_out, partial_squares))
+    raw_in = from_partner(raw_out, "tensor", 0)
+    got_half = raw_in[:half_rows]
+    got_keys = raw_in[half_rows : half_rows + tok_seq]
+    got_values = raw_in[half_rows + tok_seq :]
     squares = jnp.sum(gather_by_exchange(partial_squares, "tensor"), axis=0)
-    query_rows = (
-        query_part * lax.rsqrt(squares[0] / width + 1e-05)[:, None] * q_gain.astype(jnp.float32)
-    ).astype(jnp.bfloat16)
-    new_keys = (
-        key_part * lax.rsqrt(squares[1] / width + 1e-05)[:, None] * k_gain.astype(jnp.float32)
-    ).astype(jnp.bfloat16)
-    new_values = projected[:, 2 * columns :].astype(jnp.bfloat16)
+    query_scale = lax.rsqrt(squares[0] / width + 1e-05)[:, None]
+    key_scale = lax.rsqrt(squares[1] / width + 1e-05)[:, None]
+    own_scale = lax.dynamic_index_in_dim(
+        query_scale.reshape(2, half_rows, 1), lower_bit, 0, keepdims=False
+    )
+    own_query = (own_half * own_scale * q_gain.astype(jnp.float32)).astype(jnp.bfloat16)
+    got_query = (got_half * own_scale * gains_in[0].astype(jnp.float32)).astype(jnp.bfloat16)
+    new_keys = (key_part * key_scale * k_gain.astype(jnp.float32)).astype(jnp.bfloat16)
+    new_values = value_part.astype(jnp.bfloat16)
+    partner_keys = (got_keys * key_scale * gains_in[1].astype(jnp.float32)).astype(jnp.bfloat16)
     stacked = jnp.stack([new_keys, new_values], axis=1)
-    half_rows = tok_seq // 2
-    partner = from_partner(stacked, "tensor", 0)
+    partner = jnp.stack([partner_keys, got_values.astype(jnp.bfloat16)], axis=1)
     suffix_full = jnp.where(
         lower_bit == 0,
         jnp.concatenate([stacked, partner], axis=-1),
         jnp.concatenate([partner, stacked], axis=-1),
     )
-    query_halves = query_rows.reshape(2, half_rows, columns)
-    own_half = lax.dynamic_index_in_dim(query_halves, lower_bit, 0, keepdims=False)
-    send_half = lax.dynamic_index_in_dim(query_halves, 1 - lower_bit, 0, keepdims=False)
-    got_half = from_partner(send_half, "tensor", 0)
     query_full = jnp.where(
         lower_bit == 0,
-        jnp.concatenate([own_half, got_half], axis=-1),
-        jnp.concatenate([got_half, own_half], axis=-1),
+        jnp.concatenate([own_query, got_query], axis=-1),
+        jnp.concatenate([got_query, own_query], axis=-1),
     )
     query_offset = lower_bit * half_rows
     heads_local = 1
@@ -195,7 +206,6 @@
     expert_in = rms_scale(mixed_rows.astype(jnp.float32), mlp_gain).astype(jnp.bfloat16)
     exp_local = EXP_DEV
     experts_all = exp_local * tensor_size
-    own_expert = seq_index // (seq_size // exp_local)
     capacity = max(2, 2 * tok_dev * TOP // experts_all)
     flat_ids = expert_ids.reshape(-1)
     onehot = (flat_ids[:, None] == jnp.arange(experts_all, dtype=jnp.int32)[None, :]).astype(

time: 266 us -> 261 us (0.981)
  waiting for transfers between devices: 92.3 us -> 85.7 us
  starting transfers between devices: 30 us -> 32.8 us
    all_to_all x2, waiting for transfers between devices: 34.2 us -> 30.2 us  [gather_by_exchange(): got = lax.all_to_all(copies, axis, 0, 0, tiled=True)]
    ppermute x4, waiting for transfers between devices: 18.8 us -> 15.1 us  [from_partner(): return lax.ppermute(value, axis, pairs)]
  transfers between devices with their start and end apart: 10 -> 10, of which waited for: 9 -> 8; matrix products, arithmetic and copies ran while one was open for 2% -> 2% of each run, Pallas kernels for 0% -> 0%
where the time goes in v5:
time: 261 us; the launch traced here: 257 us
  blocking collectives  89.8 us (34%)
  waiting for transfers between devices  85.7 us (33%)
  starting transfers between devices  32.8 us (13%)
  matrix products  17.2 us (7%)
  between operations  14.5 us (6%)
  local copies, waits for them, and re-layouts  10.4 us (4%)
  other arithmetic  6.41 us (2%)
    all_to_all x1, blocking collectives, local(): lax.all_to_all(jnp.repeat(per_expert, holders, axis=0), 'seq', 0, 0, tile...  38.6 us
    all_to_all x1, blocking collectives, local(): back = lax.all_to_all(result.astype(jnp.bfloat16), 'seq', 0, 0, tiled=True)  30.7 us
    all_to_all x2, waiting for transfers between devices, gather_by_exchange(): got = lax.all_to_all(copies, axis, 0, 0, tiled=True)  30.2 us
    all_to_all x1, waiting for transfers between devices, local(): lax.all_to_all(attn_partial, 'tensor', 0, 0, tiled=True).astype(jnp.float32)  21.3 us
    all_to_all x1, blocking collectives, local(): lax.all_to_all(buffer, 'tensor', split_axis=0, concat_axis=0, tiled=True)  20.6 us
    all_to_all x2, starting transfers between devices, gather_by_exchange(): got = lax.all_to_all(copies, axis, 0, 0, tiled=True)  17.8 us
    ppermute x4, waiting for transfers between devices, from_partner(): return lax.ppermute(value, axis, pairs)  15.1 us
    all_to_all x1, waiting for transfers between devices, local(): lax.all_to_all(summed.astype(jnp.bfloat16), 'tensor', split_axis=0, conca...  14.6 us
  transfers between devices with their start and end apart: 10, of which 8 were waited for; matrix products, arithmetic and copies ran while one was open for 2% of the time, Pallas kernels for 0%

profile of v5, /device:TPU:7, one launch (start us, length us, event | category | flops | bytes accessed | tf_op | source)
XLA Modules:
  0.0 256.9 jit_solution(7860175124105188072)
XLA Ops:
  7.2 1.2 fusion.142
  8.4 1.4 collective-permute-start.3
  9.8 11.5 %collective-permute-done.3 = bf16[2048,2,64]{0,2,1:T(8,128)(2,1)S(1)} collective-permute-done((bf16[2048,2,64]{0,2,1:T(8,128)(2,1)S(1)}, bf16[2048,2,64]{0,2,1:T(8,128)(2,1)S(1)}, u32[]{:S(2)}, u32[]{:S(2)}) %collective-permute-start.3) | collective-permute-done | bytes 524320 | tf_op jit(solution)/shard_map/ppermute | solution.py:14
  21.6 1.4 copy.47
  23.3 1.1 broadcast_in_dim.199
  24.4 11.2 %all-to-all-start = ((bf16[32,8,2048]{2,1,0:T(8,128)(2,1)}), bf16[32,8,2048]{2,1,0:T(8,128)(2,1)S(1)}, u32[]{:S(2)}, u32[]{:S(2)}) async-start(bf16[32,8,2048]{2,1,0:T(8,128)(2,1)} %broadcast_in_dim.199), calls=%async_computation | async-start | bytes 2097152 | tf_op jit(solution)/shard_map/all_to_all | solution.py:26
  35.6 1.3 collective-permute-start.1
  37.4 1.2 collective-permute-done.1
  38.7 22.7 %all-to-all-done = bf16[32,8,2048]{2,1,0:T(8,128)(2,1)S(1)} async-done(((bf16[32,8,2048]{2,1,0:T(8,128)(2,1)}), bf16[32,8,2048]{2,1,0:T(8,128)(2,1)S(1)}, u32[]{:S(2)}, u32[]{:S(2)}) %all-to-all-start) | async-done | bytes 1048608 | tf_op jit(solution)/shard_map/all_to_all | solution.py:26
  61.3 0.5 fusion.27
  62.0 0.6 broadcast_in_dim.200
  62.7 6.6 %all-to-all-start.1 = ((f32[32,2,256]{2,1,0:T(2,128)}), f32[32,2,256]{2,1,0:T(2,128)S(1)}, u32[]{:S(2)}, u32[]{:S(2)}) async-start(f32[32,2,256]{2,1,0:T(2,128)} %broadcast_in_dim.200), calls=%async_computation.1 | async-start | bytes 131072 | tf_op jit(solution)/shard_map/all_to_all | solution.py:26
  69.3 1.3 collective-permute-start
  70.6 7.6 %all-to-all-done.1 = f32[32,2,256]{2,1,0:T(2,128)S(1)} async-done(((f32[32,2,256]{2,1,0:T(2,128)}), f32[32,2,256]{2,1,0:T(2,128)S(1)}, u32[]{:S(2)}, u32[]{:S(2)}) %all-to-all-start.1) | async-done | bytes 65568 | tf_op jit(solution)/shard_map/all_to_all | solution.py:26
  78.4 1.5 collective-permute-start.2
  80.0 4.5 %collective-permute-done.2 = bf16[256,2,128]{0,2,1:T(8,128)(2,1)S(1)} collective-permute-done((bf16[256,2,128]{0,2,1:T(8,128)(2,1)S(1)}, bf16[256,2,128]{0,2,1:T(8,128)(2,1)S(1)}, u32[]{:S(2)}, u32[]{:S(2)}) %collective-permute-start.2) | collective-permute-done | bytes 131104 | tf_op jit(solution)/shard_map/ppermute | solution.py:20
  84.8 3.7 %slice_bitcast_fusion.7 = (bf16[2048,2,128]{2,0,1:T(8,128)(2,1)S(1)}, bf16[2048,2,128]{2,0,1:T(8,128)(2,1)S(1)}, bf16[2048,2,128]{2,0,1:T(8,128)(2,1)S(1)}, bf16...) fusion(bf16[8,2048,2,128]{3,1,2,0:T(8,128)(2,1)} %all-gather.2., ...), kind=kLoop, calls=%fused_computation.54 | loop fusion | bytes 16777216 | tf_op jit(solution)/shard_map/squeeze | solution.py:187
  95.5 0.4 fusion.18
  99.0 2.3 collective-permute-done.4
  101.3 1.4 fusion
  102.8 4.9 %all-to-all-start.2 = ((bf16[32,8,2048]{2,1,0:T(8,128)(2,1)}), bf16[32,8,2048]{2,1,0:T(8,128)(2,1)S(1)}, u32[]{:S(2)}, u32[]{:S(2)}) async-start(bf16[32,8,2048]{2,1,0:T(8,128)(2,1)} %fusion), calls=%async_computation.2 | async-start | bytes 2097152 | tf_op jit(solution)/shard_map/all_to_all | solution.py:203
  108.3 21.3 %all-to-all-done.2 = bf16[32,8,2048]{2,1,0:T(8,128)(2,1)S(1)} async-done(((bf16[32,8,2048]{2,1,0:T(8,128)(2,1)}), bf16[32,8,2048]{2,1,0:T(8,128)(2,1)S(1)}, u32[]{:S(2)}, u32[]{:S(2)}) %all-to-all-start.2) | async-done | bytes 1048608 | tf_op jit(solution)/shard_map/all_to_all | solution.py:203
  130.6 20.6 %all_to_all.35 = bf16[32,2,2,2048]{3,2,1,0:T(2,128)(2,1)S(1)} all-to-all(bf16[32,2,2,2048]{3,2,1,0:T(2,128)(2,1)S(1)} %reshape.970), channel_id=1, replica_groups=mesh['seq'=8,'tensor'=32] {'tensor'}, dimensions={0} | all-to-all | bytes 1048576 | tf_op jit(solution)/shard_map/all_to_all | solution.py:226
  151.7 38.6 %all_to_all.36 = bf16[8,32,2,2048]{3,1,2,0:T(8,128)(2,1)S(1)} all-to-all(bf16[8,32,2,2048]{3,1,2,0:T(8,128)(2,1)S(1)} %bitcast.170), channel_id=1, replica_groups=mesh['seq'=8,'tensor'=32] {'seq'}, dimensions={0} | all-to-all | bytes 4194304 | tf_op jit(solution)/shard_map/all_to_all | solution.py:232
  190.3 1.5 fusion.25
  191.8 5.0 %convolution_convert_fusion = bf16[8,32,2,2048]{3,1,2,0:T(8,128)(2,1)} fusion(bf16[8,32,2,2048]{3,1,2,0:T(8,128)(2,1)S(1)} %all_to_all.36, bf16[1,256,2048]{2,1,0:T(8,128)(2,1)S(1)} %copy-done, bf16[1,2048,256]{2,1,0:T(8,128)(2,1)} %param.32, f32[8,32,2,256]{3,1,2,0:T(8,128)} %fusion.25), kind=kOutput, calls=%fused_computation | convolution fusion | flops 1075576832 | bytes 6815744 | tf_op jit(solution)/shard_map/srcf,fd->srcd/dot_general | solution.py:236
  196.8 30.7 %all_to_all.37 = bf16[8,32,2,2048]{3,1,2,0:T(8,128)(2,1)S(1)} all-to-all(bf16[8,32,2,2048]{3,1,2,0:T(8,128)(2,1)} %convolution_convert_fusion), channel_id=1, replica_groups=mesh['seq'=8,'tensor'=32] {'seq'}, dimensions={0} | all-to-all | bytes 4194304 | tf_op jit(solution)/shard_map/all_to_all | solution.py:237
  227.9 1.3 copy.49
  229.3 4.3 %all-to-all-start.6 = ((bf16[32,2,2,2048]{3,2,1,0:T(2,128)(2,1)}), bf16[32,2,2,2048]{3,2,1,0:T(2,128)(2,1)S(1)}, u32[]{:S(2)}, u32[]{:S(2)}) async-start(bf16[32,2,2,2048]{3,2,1,0:T(2,128)(2,1)} %copy.49), calls=%async_computation.6 | async-start | bytes 1048576 | tf_op jit(solution)/shard_map/all_to_all | solution.py:242
  233.7 0.6 slice.262
  234.3 14.6 %all-to-all-done.6 = bf16[32,2,2,2048]{3,2,1,0:T(2,128)(2,1)S(1)} async-done(((bf16[32,2,2,2048]{3,2,1,0:T(2,128)(2,1)}), bf16[32,2,2,2048]{3,2,1,0:T(2,128)(2,1)S(1)}, u32[]{:S(2)}, u32[]{:S(2)}) %all-to-all-start.6) | async-done | bytes 524320 | tf_op jit(solution)/shard_map/all_to_all | solution.py:242
  249.1 0.9 fusion.9
  (111 shorter events, 14.6 us)
Async XLA Ops:
  7.2 184.6 %copy-start = (bf16[1,256,2048]{2,1,0:T(8,128)(2,1)S(1)}, bf16[1,256,2048]{2,1,0:T(8,128)(2,1)}, u32[]{:S(2)}) copy-start(bf16[1,256,2048]{2,1,0:T(8,128)(2,1)} %param.33) | copy-start | bytes 3145732
  7.2 77.6 %all-gather.2.cloned.1.call-start = ((), (), s32[]{:S(2)}) async-start(), calls=%async_computation.7 | async-start | bytes 9437184 | tf_op jit(solution)/shard_map/all_gather | solution.py:94
  8.4 12.9 %collective-permute-start.3 = (bf16[2048,2,64]{0,2,1:T(8,128)(2,1)S(1)}, bf16[2048,2,64]{0,2,1:T(8,128)(2,1)S(1)}, u32[]{:S(2)}, u32[]{:S(2)}) collective-permute-start(bf16[2048,2,64]{0,2,1:T(8,128)(2,1)S(1)} %get-tuple-element.37), channel_id=1, source_target_pairs={{0,1},{1,0},{2,3},{3,2},{4,5},{5,4},{6,7},{7,6},{8,9},{9,8},{10,11... | collective-permute-start | bytes 1572872 | tf_op jit(solution)/shard_map/ppermute | solution.py:14
  21.6 1.5 copy-start.7
  21.6 1.5 copy-start.2
  23.0 12.6 %copy-start.12 = (bf16[64]{0:T(256)(128)(2,1)S(1)}, bf16[64]{0:T(256)(128)(2,1)}, u32[]{:S(2)}) copy-start(bf16[64]{0:T(256)(128)(2,1)} %param.20) | copy-start | bytes 388
  23.0 12.6 %copy-start.13 = (bf16[64]{0:T(256)(128)(2,1)S(1)}, bf16[64]{0:T(256)(128)(2,1)}, u32[]{:S(2)}) copy-start(bf16[64]{0:T(256)(128)(2,1)} %param.21) | copy-start | bytes 388
  23.0 14.0 %copy-start.5 = (s32[2048]{0:T(1024)S(1)}, s32[2048]{0:T(1024)}, u32[]{:S(2)}) copy-start(s32[2048]{0:T(1024)} %param.25) | copy-start | bytes 24580
  23.0 14.1 %copy-start.10 = (s32[32]{0:T(128)S(1)}, s32[32]{0:T(128)}, u32[]{:S(2)}) copy-start(s32[32]{0:T(128)} %param.26) | copy-start | bytes 388
  23.0 14.3 %copy-start.14 = (s32[4]{0:T(128)S(1)}, s32[4]{0:T(128)}, u32[]{:S(2)}) copy-start(s32[4]{0:T(128)} %param.27) | copy-start | bytes 52
  23.0 38.3 %copy-start.1 = (bf16[2048,3,64]{0,2,1:T(8,128)(2,1)S(1)}, bf16[2048,3,64]{0,2,1:T(8,128)(2,1)}, u32[]{:S(2)}) copy-start(bf16[2048,3,64]{0,2,1:T(8,128)(2,1)} %param.19) | copy-start | bytes 2359300
  24.4 37.0 %all-to-all-start = ((bf16[32,8,2048]{2,1,0:T(8,128)(2,1)}), bf16[32,8,2048]{2,1,0:T(8,128)(2,1)S(1)}, u32[]{:S(2)}, u32[]{:S(2)}) async-start(bf16[32,8,2048]{2,1,0:T(8,128)(2,1)} %broadcast_in_dim.199), calls=%async_computation | async-start | bytes 2097152 | tf_op jit(solution)/shard_map/all_to_all | solution.py:26
  35.6 3.0 %collective-permute-start.1 = (bf16[2,64]{1,0:T(2,128)(2,1)S(1)}, bf16[2,64]{1,0:T(2,128)(2,1)S(1)}, u32[]{:S(2)}, u32[]{:S(2)}) collective-permute-start(bf16[2,64]{1,0:T(2,128)(2,1)S(1)} %pad_maximum_fusion.4), channel_id=1, source_target_pairs={{0,1},{1,0},{2,3},{3,2},{4,5},{5,4},{6,7},{7,6},{8,9},{9,8},{10,11... | collective-permute-start | bytes 776 | tf_op jit(solution)/shard_map/ppermute | solution.py:14
  62.7 15.5 %all-to-all-start.1 = ((f32[32,2,256]{2,1,0:T(2,128)}), f32[32,2,256]{2,1,0:T(2,128)S(1)}, u32[]{:S(2)}, u32[]{:S(2)}) async-start(f32[32,2,256]{2,1,0:T(2,128)} %broadcast_in_dim.200), calls=%async_computation.1 | async-start | bytes 131072 | tf_op jit(solution)/shard_map/all_to_all | solution.py:26
  69.3 9.0 %collective-permute-start = (f32[640,64]{0,1:T(8,128)S(1)}, f32[640,64]{0,1:T(8,128)S(1)}, u32[]{:S(2)}, u32[]{:S(2)}) collective-permute-start(f32[640,64]{0,1:T(8,128)S(1)} %pad_maximum_fusion.1), channel_id=1, source_target_pairs={{0,1},{1,0},{2,3},{3,2},{4,5},{5,4},{6,7},{7,6},{8,9},{9,8},{10,11... | collective-permute-start | bytes 491528 | tf_op jit(solution)/shard_map/ppermute | solution.py:14
  78.4 10.1 %copy-start.4 = (bf16[256,64]{0,1:T(8,128)(2,1)}, bf16[256,64]{0,1:T(8,128)(2,1)S(1)}, u32[]{:S(2)}) copy-start(bf16[256,64]{0,1:T(8,128)(2,1)S(1)} %get-tuple-element.47) | copy-start | bytes 98308
  78.4 6.0 %collective-permute-start.2 = (bf16[256,2,128]{0,2,1:T(8,128)(2,1)S(1)}, bf16[256,2,128]{0,2,1:T(8,128)(2,1)S(1)}, u32[]{:S(2)}, u32[]{:S(2)}) collective-permute-start(bf16[256,2,128]{0,2,1:T(8,128)(2,1)S(1)} %maximum_select_fusion.1), channel_id=1, source_target_pairs={{0,32},{32,64},{64,96},{96,128},{128,160},{160,192},{192,224},{1,3... | collective-permute-start | bytes 393224 | tf_op jit(solution)/shard_map/ppermute | solution.py:20
  97.7 3.6 %copy-start.3 = (bf16[64,2048]{1,0:T(8,128)(2,1)S(1)}, bf16[64,2048]{1,0:T(8,128)(2,1)}, u32[]{:S(2)}) copy-start(bf16[64,2048]{1,0:T(8,128)(2,1)} %param.22) | copy-start | bytes 786436
  98.6 9.0 %copy-start.6 = (s32[8,8]{1,0:T(8,128)S(1)}, s32[8,8]{1,0:T(8,128)}, u32[]{:S(2)}) copy-start(s32[8,8]{1,0:T(8,128)} %param.29) | copy-start | bytes 772
  98.6 9.1 %copy-start.8 = (bf16[2048]{0:T(1024)(128)(2,1)S(1)}, bf16[2048]{0:T(1024)(128)(2,1)}, u32[]{:S(2)}) copy-start(bf16[2048]{0:T(1024)(128)(2,1)} %param.28) | copy-start | bytes 12292
  98.7 2.7 %collective-permute-start.4 = (bf16[128,64]{0,1:T(8,128)(2,1)S(1)}, bf16[128,64]{0,1:T(8,128)(2,1)S(1)}, u32[]{:S(2)}, u32[]{:S(2)}) collective-permute-start(bf16[128,64]{0,1:T(8,128)(2,1)S(1)} %get-tuple-element.44), channel_id=1, source_target_pairs={{0,1},{1,0},{2,3},{3,2},{4,5},{5,4},{6,7},{7,6},{8,9},{9,8},{10,11... | collective-permute-start | bytes 49160 | tf_op jit(solution)/shard_map/ppermute | solution.py:14
  102.8 26.8 %all-to-all-start.2 = ((bf16[32,8,2048]{2,1,0:T(8,128)(2,1)}), bf16[32,8,2048]{2,1,0:T(8,128)(2,1)S(1)}, u32[]{:S(2)}, u32[]{:S(2)}) async-start(bf16[32,8,2048]{2,1,0:T(8,128)(2,1)} %fusion), calls=%async_computation.2 | async-start | bytes 2097152 | tf_op jit(solution)/shard_map/all_to_all | solution.py:203
  151.7 38.6 %copy-start.11 = (bf16[1,2048,256]{2,1,0:T(8,128)(2,1)S(1)}, bf16[1,2048,256]{2,1,0:T(8,128)(2,1)}, u32[]{:S(2)}) copy-start(bf16[1,2048,256]{2,1,0:T(8,128)(2,1)} %param.31) | copy-start | bytes 3145732
  227.5 6.0 %copy-start.9 = (f32[8,8]{1,0:T(8,128)S(1)}, f32[8,8]{1,0:T(8,128)}, u32[]{:S(2)}) copy-start(f32[8,8]{1,0:T(8,128)} %param.30) | copy-start | bytes 772
  229.3 19.6 %all-to-all-start.6 = ((bf16[32,2,2,2048]{3,2,1,0:T(2,128)(2,1)}), bf16[32,2,2,2048]{3,2,1,0:T(2,128)(2,1)S(1)}, u32[]{:S(2)}, u32[]{:S(2)}) async-start(bf16[32,2,2,2048]{3,2,1,0:T(2,128)(2,1)} %copy.49), calls=%async_computation.6 | async-start | bytes 1048576 | tf_op jit(solution)/shard_map/all_to_all | solution.py:242
Sparse Core Ops, SparseCore 0:
  23.2 54.4 all-gather.1

commit v6 on v5

--- a/solution.py
+++ b/solution.py
@@ -1,17 +1,17 @@
 import jax
 import jax.numpy as jnp
 from jax import lax
+from jax.sharding import Mesh
 from jax.sharding import PartitionSpec as P
 
 HD = 128
 TOP = 8
 EXP_DEV = 2
-
-
-def from_partner(value, axis, stride):
-    mask = 2**stride
-    pairs = [(source, source ^ mask) for source in range(lax.axis_size(axis))]
-    return lax.ppermute(value, axis, pairs)
+TENSOR = ("th", "tyl")
+
+
+def from_partner(value):
+    return lax.ppermute(value, "tyl", [(0, 1), (1, 0)])
 
 
 def passed_along(value, axis, by):
@@ -52,6 +52,28 @@
         value_block,
         preferred_element_type=jnp.float32,
     )
+    accum = accum * factor[:, :, None] + update
+    return (new_largest, total, accum)
+
+
+def attend_halves(carry, queries_heads, halves, mask):
+    largest, total, accum = carry
+    rows = queries_heads.shape[0]
+    split_queries = queries_heads.reshape(rows, 2, HD // 2)
+    scores = jnp.einsum(
+        "qcd,ckd->qk", split_queries, halves[:, :, 0], preferred_element_type=jnp.float32
+    )[None] * HD ** (-0.5)
+    scores = jnp.where(mask[None], scores, -1e30)
+    new_largest = jnp.maximum(largest, jnp.max(scores, axis=-1))
+    weights = jnp.where(mask[None], jnp.exp(scores - new_largest[:, :, None]), 0.0)
+    factor = jnp.exp(largest - new_largest)
+    total = total * factor + jnp.sum(weights, axis=-1)
+    update = jnp.einsum(
+        "qk,ckd->qcd",
+        weights[0].astype(jnp.bfloat16),
+        halves[:, :, 1],
+        preferred_element_type=jnp.float32,
+    ).reshape(1, rows, HD)
     accum = accum * factor[:, :, None] + update
     return (new_largest, total, accum)
 
@@ -75,27 +97,21 @@
     w_up,
     w_down,
 ):
-    tensor_size = lax.axis_size("tensor")
+    tensor_size = lax.axis_size(TENSOR)
     seq_size = lax.axis_size("seq")
     seq_index = lax.axis_index("seq")
-    tensor_index = lax.axis_index("tensor")
+    tensor_index = lax.axis_index(TENSOR)
     tok_dev = tokens.shape[0]
     width = tokens.shape[1]
     tok_seq = tok_dev * tensor_size
     columns = w_qkv.shape[2]
     lower_bit = tensor_index % 2
     prefix_own = jnp.stack([prefix_keys[0], prefix_values[0]], axis=1)
-    prefix_partner = from_partner(prefix_own, "tensor", 0)
-    prefix_full = jnp.where(
-        lower_bit == 0,
-        jnp.concatenate([prefix_own, prefix_partner], axis=-1),
-        jnp.concatenate([prefix_partner, prefix_own], axis=-1),
-    )
-    piece = lax.all_gather(prefix_full[None], "seq", axis=0, tiled=True)
-    gains_in = from_partner(jnp.stack([q_gain, k_gain]), "tensor", 0)
+    piece = lax.all_gather(prefix_own[None], ("seq", "tyl"), axis=0, tiled=True)
+    gains_in = from_partner(jnp.stack([q_gain, k_gain]))
     normed = rms_scale(tokens.astype(jnp.float32), attn_gain).astype(jnp.bfloat16)
     w_flat = w_qkv.reshape(width, 3 * columns)
-    rows = gather_by_exchange(normed, "tensor").reshape(tok_seq, width)
+    rows = gather_by_exchange(normed, TENSOR).reshape(tok_seq, width)
     projected = jnp.dot(
         rows,
         w_flat,
@@ -113,11 +129,11 @@
     send_half = lax.dynamic_index_in_dim(query_halves, 1 - lower_bit, 0, keepdims=False)
     raw_out = jnp.concatenate([send_half, key_part, value_part], axis=0)
     raw_out, partial_squares = lax.optimization_barrier((raw_out, partial_squares))
-    raw_in = from_partner(raw_out, "tensor", 0)
+    raw_in = from_partner(raw_out)
     got_half = raw_in[:half_rows]
     got_keys = raw_in[half_rows : half_rows + tok_seq]
     got_values = raw_in[half_rows + tok_seq :]
-    squares = jnp.sum(gather_by_exchange(partial_squares, "tensor"), axis=0)
+    squares = jnp.sum(gather_by_exchange(partial_squares, TENSOR), axis=0)
     query_scale = lax.rsqrt(squares[0] / width + 1e-05)[:, None]
     key_scale = lax.rsqrt(squares[1] / width + 1e-05)[:, None]
     own_scale = lax.dynamic_index_in_dim(
@@ -182,16 +198,16 @@
     )
     state = carry
     start = jnp.int32(0)
-    for offset in range(piece.shape[0]):
+    for offset in range(seq_size):
         slot_mask = (owner_of_query == start + offset)[:, None]
-        state = attend_block(state, queries_heads, piece[offset], slot_mask)
+        state = attend_halves(state, queries_heads, piece[2 * offset : 2 * offset + 2], slot_mask)
     carry = state
     attended = (carry[2] / carry[1][:, :, None]).astype(jnp.bfloat16)
     attended = jnp.transpose(attended, (1, 0, 2)).reshape(half_rows, heads_local * HD)
     split_out = attended.reshape(half_rows, 2, columns)
     own_out = lax.dynamic_index_in_dim(split_out, lower_bit, 1, keepdims=False)
     send_out = lax.dynamic_index_in_dim(split_out, 1 - lower_bit, 1, keepdims=False)
-    got_out = from_partner(send_out, "tensor", 0)
+    got_out = from_partner(send_out)
     attended_local = jnp.where(
         lower_bit == 0,
         jnp.concatenate([own_out, got_out], axis=0),
@@ -200,7 +216,7 @@
     attn_partial = jnp.dot(attended_local, w_out, preferred_element_type=jnp.float32)
     attn_partial = attn_partial.astype(jnp.bfloat16).reshape(tensor_size, tok_dev, width)
     attn_sum = jnp.sum(
-        lax.all_to_all(attn_partial, "tensor", 0, 0, tiled=True).astype(jnp.float32), axis=0
+        lax.all_to_all(attn_partial, TENSOR, 0, 0, tiled=True).astype(jnp.float32), axis=0
     )
     mixed_rows = (tokens.astype(jnp.float32) + attn_sum).astype(jnp.bfloat16)
     expert_in = rms_scale(mixed_rows.astype(jnp.float32), mlp_gain).astype(jnp.bfloat16)
@@ -223,7 +239,7 @@
         jnp.bfloat16
     )
     buffer = buffer.reshape(tensor_size, exp_local, capacity, width)
-    received = lax.all_to_all(buffer, "tensor", split_axis=0, concat_axis=0, tiled=True)
+    received = lax.all_to_all(buffer, TENSOR, split_axis=0, concat_axis=0, tiled=True)
     gate_local = w_gate[0]
     up_local = w_up[0]
     down_local = w_down[0]
@@ -240,7 +256,7 @@
     )
     summed = jnp.transpose(summed, (1, 0, 2, 3))
     returned = lax.all_to_all(
-        summed.astype(jnp.bfloat16), "tensor", split_axis=0, concat_axis=0, tiled=True
+        summed.astype(jnp.bfloat16), TENSOR, split_axis=0, concat_axis=0, tiled=True
     ).astype(jnp.float32)
     moe_sum = jnp.dot(
         combine_table,
@@ -253,28 +269,30 @@
 
 
 def solution(mesh):
+    seq_size, tensor_size = mesh.devices.shape
+    grid = Mesh(mesh.devices.reshape(seq_size, tensor_size // 2, 2), ("seq",) + TENSOR)
     return jax.shard_map(
         local,
-        mesh=mesh,
+        mesh=grid,
         in_specs=(
-            P(("seq", "tensor"), None),
-            P(),
-            P(None, None, "tensor"),
-            P("tensor"),
-            P("tensor"),
-            P("tensor", None),
-            P("seq", None, "tensor"),
-            P("seq", None, "tensor"),
-            P(),
-            P(),
-            P(),
-            P(),
-            P(("seq", "tensor"), None),
-            P(("seq", "tensor"), None),
-            P(("tensor", "seq"), None, None),
-            P(("tensor", "seq"), None, None),
-            P(("tensor", "seq"), None, None),
+            P(("seq",) + TENSOR, None),
+            P(),
+            P(None, None, TENSOR),
+            P(TENSOR),
+            P(TENSOR),
+            P(TENSOR, None),
+            P("seq", None, TENSOR),
+            P("seq", None, TENSOR),
+            P(),
+            P(),
+            P(),
+            P(),
+            P(("seq",) + TENSOR, None),
+            P(("seq",) + TENSOR, None),
+            P(TENSOR + ("seq",), None, None),
+            P(TENSOR + ("seq",), None, None),
+            P(TENSOR + ("seq",), None, None),
         ),
-        out_specs=(P(("seq", "tensor"), None), P("seq", "tensor"), P("seq", "tensor")),
+        out_specs=(P(("seq",) + TENSOR, None), P("seq", TENSOR), P("seq", TENSOR)),
         check_vma=False,
     )

time: 261 us -> 291 us (1.11)
  local copies, waits for them, and re-layouts: 10.4 us -> 34.7 us
  blocking collectives: 89.8 us -> 84.3 us
  waiting for transfers between devices: 85.7 us -> 90.8 us
    dot_general x0 -> x9, local copies, waits for them, and re-layouts: none -> 16.5 us  [attend_halves(): jnp.einsum('qk,ckd->qcd', weights[0].astype(jnp.bfloat16), halves[:, :, 1...]
    unnamed x30 -> x29, local copies, waits for them, and re-layouts: 0.09 us -> 13 us
    all_gather x1, waiting for transfers between devices: 0.02 us -> 12 us  [local(): piece = lax.all_gather(prefix_own[None], ('seq', 'tyl'), axis=0, tiled=True)]
    ppermute x4 -> x3, waiting for transfers between devices: 15.1 us -> 4.22 us  [from_partner(): return lax.ppermute(value, 'tyl', [(0, 1), (1, 0)])]
    dot_general x0 -> x16, matrix products: none -> 6.55 us  [the longest x8 3.43 us: attend_halves(): jnp.einsum('qcd,ckd->qk', split_queries, halves[:, :, 0], preferred_eleme...]
    all_to_all x1, blocking collectives: 38.6 us -> 32.3 us  [local(): lax.all_to_all(jnp.repeat(per_expert, holders, axis=0), 'seq', 0, 0, tile...]
    all_to_all x2, starting transfers between devices: 9.15 us -> 13.6 us  [the longest x1 9.33 us: local(): lax.all_to_all(attn_partial, TENSOR, 0, 0, tiled=True).astype(jnp.float32)]
    all_to_all x2, waiting for transfers between devices: 35.9 us -> 40.1 us  [the longest x1 25.5 us: local(): lax.all_to_all(attn_partial, TENSOR, 0, 0, tiled=True).astype(jnp.float32)]
  transfers between devices with their start and end apart: 10 -> 9, of which waited for: 8 -> 8; matrix products, arithmetic and copies ran while one was open for 2% -> 3% of each run, Pallas kernels for 0% -> 0%
where the time goes in v6:
time: 291 us; the launch traced here: 286 us
  waiting for transfers between devices  90.8 us (31%)
  blocking collectives  84.3 us (29%)
  starting transfers between devices  35.6 us (12%)
  local copies, waits for them, and re-layouts  34.7 us (12%)
  matrix products  16.9 us (6%)
  between operations  14.5 us (5%)
  other arithmetic  9.28 us (3%)
    all_to_all x1, blocking collectives, local(): lax.all_to_all(jnp.repeat(per_expert, holders, axis=0), 'seq', 0, 0, tile...  32.3 us
    all_to_all x1, blocking collectives, local(): back = lax.all_to_all(result.astype(jnp.bfloat16), 'seq', 0, 0, tiled=True)  30.7 us
    all_to_all x2, waiting for transfers between devices, gather_by_exchange(): got = lax.all_to_all(copies, axis, 0, 0, tiled=True)  29.9 us
    all_to_all x1, waiting for transfers between devices, local(): lax.all_to_all(attn_partial, TENSOR, 0, 0, tiled=True).astype(jnp.float32)  25.5 us
    all_to_all x1, blocking collectives, local(): lax.all_to_all(buffer, TENSOR, split_axis=0, concat_axis=0, tiled=True)  21.2 us
    all_to_all x2, starting transfers between devices, gather_by_exchange(): got = lax.all_to_all(copies, axis, 0, 0, tiled=True)  17.6 us
    dot_general x9, local copies, waits for them, and re-layouts, attend_halves(): jnp.einsum('qk,ckd->qcd', weights[0].astype(jnp.bfloat16), halves[:, :, 1...  16.5 us
    all_to_all x1, waiting for transfers between devices, local(): lax.all_to_all(summed.astype(jnp.bfloat16), TENSOR, split_axis=0, concat_...  14.6 us
  transfers between devices with their start and end apart: 9, of which 8 were waited for; matrix products, arithmetic and copies ran while one was open for 3% of the time, Pallas kernels for 0%

profile of v6, /device:TPU:7, one launch (start us, length us, event | category | flops | bytes accessed | tf_op | source)
XLA Modules:
  0.0 286.1 jit_solution(1501497104310050189)
XLA Ops:
  7.2 2.0 pad_maximum_fusion
  9.2 0.8 convert_element_type.135
  10.0 0.9 fusion.106
  10.9 0.8 fusion.108
  11.7 1.2 broadcast_in_dim.209
  12.9 11.2 %all-to-all-start = ((bf16[32,8,2048]{2,1,0:T(8,128)(2,1)}), bf16[32,8,2048]{2,1,0:T(8,128)(2,1)S(1)}, u32[]{:S(2)}, u32[]{:S(2)}) async-start(bf16[32,8,2048]{2,1,0:T(8,128)(2,1)} %broadcast_in_dim.209), calls=%async_computation | async-start | bytes 2097152 | tf_op jit(solution)/shard_map/all_to_all | solution.py:26
  24.2 1.3 collective-permute-start.1
  26.0 2.0 collective-permute-done.1
  27.9 22.4 %all-to-all-done = bf16[32,8,2048]{2,1,0:T(8,128)(2,1)S(1)} async-done(((bf16[32,8,2048]{2,1,0:T(8,128)(2,1)}), bf16[32,8,2048]{2,1,0:T(8,128)(2,1)S(1)}, u32[]{:S(2)}, u32[]{:S(2)}) %all-to-all-start) | async-done | bytes 1048608 | tf_op jit(solution)/shard_map/all_to_all | solution.py:26
  51.0 0.7 broadcast_in_dim.210
  51.7 6.4 %all-to-all-start.1 = ((f32[32,2,256]{2,1,0:T(2,128)}), f32[32,2,256]{2,1,0:T(2,128)S(1)}, u32[]{:S(2)}, u32[]{:S(2)}) async-start(f32[32,2,256]{2,1,0:T(2,128)} %broadcast_in_dim.210), calls=%async_computation.1 | async-start | bytes 131072 | tf_op jit(solution)/shard_map/all_to_all | solution.py:26
  58.1 1.3 collective-permute-start
  59.4 7.5 %all-to-all-done.1 = f32[32,2,256]{2,1,0:T(2,128)S(1)} async-done(((f32[32,2,256]{2,1,0:T(2,128)}), f32[32,2,256]{2,1,0:T(2,128)S(1)}, u32[]{:S(2)}, u32[]{:S(2)}) %all-to-all-start.1) | async-done | bytes 65568 | tf_op jit(solution)/shard_map/all_to_all | solution.py:26
  67.2 1.3 collective-permute-start.2
  68.6 4.6 %collective-permute-done.2 = bf16[256,2,128]{0,2,1:T(8,128)(2,1)S(1)} collective-permute-done((bf16[256,2,128]{0,2,1:T(8,128)(2,1)S(1)}, bf16[256,2,128]{0,2,1:T(8,128)(2,1)S(1)}, u32[]{:S(2)}, u32[]{:S(2)}) %collective-permute-start.2) | collective-permute-done | bytes 131104 | tf_op jit(solution)/shard_map/ppermute | solution.py:20
  73.5 12.0 %all-gather.3.cloned.1.call-done = bf16[32768,2,64]{0,2,1:T(8,128)(2,1)} async-done(((bf16[2048,2,64]{0,2,1:T(8,128)(2,1)}), bf16[32768,2,64]{0,2,1:T(8,128)(2,1)}) %all-gather.3.cloned.1.call-update) | async-done | bytes 8388624 | tf_op jit(solution)/shard_map/all_gather | solution.py:110
  85.5 12.9 %copy.152 = bf16[16,8,16,2048]{3,2,1,0:T(8,128)(2,1)} copy(bf16[16,8,16,2048]{3,1,2,0:T(8,128)(2,1)} %bitcast.234) | data formatting | bytes 16777216
  98.4 15.2 %slice_bitcast_fusion = (bf16[2,64,2048]{2,0,1:T(2,128)(2,1)S(1)}, bf16[2,2048,1,64]{1,0,3,2:T(2,128)(2,1)S(1)}, bf16[2,2048,1,64]{1,0,3,2:T(2,128)(2,1)S(1)}, b...) fusion(bf16[16,2048,2,64]{1,0,3,2:T(8,128)(2,1)} %bitcast.232), kind=kLoop, calls=%fused_computation.85 | loop fusion | bytes 16777216 | tf_op jit(solution)/shard_map/qk,ckd->qcd/dot_general | solution.py:71
  125.2 2.3 collective-permute-done.3
  127.5 1.5 fusion
  128.9 9.3 %all-to-all-start.2 = ((bf16[32,8,2048]{2,1,0:T(8,128)(2,1)}), bf16[32,8,2048]{2,1,0:T(8,128)(2,1)S(1)}, u32[]{:S(2)}, u32[]{:S(2)}) async-start(bf16[32,8,2048]{2,1,0:T(8,128)(2,1)} %fusion), calls=%async_computation.2 | async-start | bytes 2097152 | tf_op jit(solution)/shard_map/all_to_all | solution.py:219
  138.9 25.5 %all-to-all-done.2 = bf16[32,8,2048]{2,1,0:T(8,128)(2,1)S(1)} async-done(((bf16[32,8,2048]{2,1,0:T(8,128)(2,1)}), bf16[32,8,2048]{2,1,0:T(8,128)(2,1)S(1)}, u32[]{:S(2)}, u32[]{:S(2)}) %all-to-all-start.2) | async-done | bytes 1048608 | tf_op jit(solution)/shard_map/all_to_all | solution.py:219
  165.4 21.2 %all_to_all.35 = bf16[32,2,2,2048]{3,2,1,0:T(2,128)(2,1)S(1)} all-to-all(bf16[32,2,2,2048]{3,2,1,0:T(2,128)(2,1)S(1)} %reshape.835), channel_id=1, replica_groups=mesh['seq'=8,'th'=16,'tyl'=2] {'th','tyl'}, dimensions={0} | all-to-all | bytes 1048576 | tf_op jit(solution)/shard_map/all_to_all | solution.py:242
  187.2 32.3 %all_to_all.36 = bf16[8,32,2,2048]{3,1,2,0:T(8,128)(2,1)S(1)} all-to-all(bf16[8,32,2,2048]{3,1,2,0:T(8,128)(2,1)S(1)} %bitcast.233), channel_id=1, replica_groups=mesh['seq'=8,'th'=16,'tyl'=2] {'seq'}, dimensions={0} | all-to-all | bytes 4194304 | tf_op jit(solution)/shard_map/all_to_all | solution.py:248
  219.5 1.5 fusion.33
  221.0 5.0 %convolution_convert_fusion = bf16[8,32,2,2048]{3,1,2,0:T(8,128)(2,1)} fusion(bf16[8,32,2,2048]{3,1,2,0:T(8,128)(2,1)S(1)} %all_to_all.36, bf16[1,256,2048]{2,1,0:T(8,128)(2,1)S(1)} %copy-done, bf16[1,2048,256]{2,1,0:T(8,128)(2,1)} %param.32, f32[8,32,2,256]{3,1,2,0:T(8,128)} %fusion.33), kind=kOutput, calls=%fused_computation | convolution fusion | flops 1075576832 | bytes 6815744 | tf_op jit(solution)/shard_map/srcf,fd->srcd/dot_general | solution.py:252
  226.1 30.7 %all_to_all.37 = bf16[8,32,2,2048]{3,1,2,0:T(8,128)(2,1)S(1)} all-to-all(bf16[8,32,2,2048]{3,1,2,0:T(8,128)(2,1)} %convolution_convert_fusion), channel_id=1, replica_groups=mesh['seq'=8,'th'=16,'tyl'=2] {'seq'}, dimensions={0} | all-to-all | bytes 4194304 | tf_op jit(solution)/shard_map/all_to_all | solution.py:253
  257.2 1.3 copy.135
  258.5 4.3 %all-to-all-start.6 = ((bf16[32,2,2,2048]{3,2,1,0:T(2,128)(2,1)}), bf16[32,2,2,2048]{3,2,1,0:T(2,128)(2,1)S(1)}, u32[]{:S(2)}, u32[]{:S(2)}) async-start(bf16[32,2,2,2048]{3,2,1,0:T(2,128)(2,1)} %copy.135), calls=%async_computation.6 | async-start | bytes 1048576 | tf_op jit(solution)/shard_map/all_to_all | solution.py:258
  262.9 0.6 slice.214
  263.5 14.6 %all-to-all-done.6 = bf16[32,2,2,2048]{3,2,1,0:T(2,128)(2,1)S(1)} async-done(((bf16[32,2,2,2048]{3,2,1,0:T(2,128)(2,1)}), bf16[32,2,2,2048]{3,2,1,0:T(2,128)(2,1)S(1)}, u32[]{:S(2)}, u32[]{:S(2)}) %all-to-all-start.6) | async-done | bytes 524320 | tf_op jit(solution)/shard_map/all_to_all | solution.py:258
  278.3 0.9 fusion.17
  (115 shorter events, 16.2 us)
Async XLA Ops:
  7.2 213.9 %copy-start = (bf16[1,256,2048]{2,1,0:T(8,128)(2,1)S(1)}, bf16[1,256,2048]{2,1,0:T(8,128)(2,1)}, u32[]{:S(2)}) copy-start(bf16[1,256,2048]{2,1,0:T(8,128)(2,1)} %param.33) | copy-start | bytes 3145732
  7.2 78.3 %all-gather.3.cloned.1.call-start = ((), (), s32[]{:S(2)}) async-start(), calls=%async_computation.7 | async-start | bytes 8912896 | tf_op jit(solution)/shard_map/all_gather | solution.py:110
  9.2 15.0 %copy-start.11 = (bf16[64]{0:T(256)(128)(2,1)S(1)}, bf16[64]{0:T(256)(128)(2,1)}, u32[]{:S(2)}) copy-start(bf16[64]{0:T(256)(128)(2,1)} %param.20) | copy-start | bytes 388
  9.2 15.0 %copy-start.12 = (bf16[64]{0:T(256)(128)(2,1)S(1)}, bf16[64]{0:T(256)(128)(2,1)}, u32[]{:S(2)}) copy-start(bf16[64]{0:T(256)(128)(2,1)} %param.21) | copy-start | bytes 388
  9.2 16.3 %copy-start.5 = (s32[2048]{0:T(1024)S(1)}, s32[2048]{0:T(1024)}, u32[]{:S(2)}) copy-start(s32[2048]{0:T(1024)} %param.25) | copy-start | bytes 24580
  9.2 16.4 %copy-start.9 = (s32[32]{0:T(128)S(1)}, s32[32]{0:T(128)}, u32[]{:S(2)}) copy-start(s32[32]{0:T(128)} %param.26) | copy-start | bytes 388
  9.2 16.7 %copy-start.13 = (s32[4]{0:T(128)S(1)}, s32[4]{0:T(128)}, u32[]{:S(2)}) copy-start(s32[4]{0:T(128)} %param.27) | copy-start | bytes 52
  9.2 41.1 %copy-start.1 = (bf16[2048,3,64]{0,2,1:T(8,128)(2,1)S(1)}, bf16[2048,3,64]{0,2,1:T(8,128)(2,1)}, u32[]{:S(2)}) copy-start(bf16[2048,3,64]{0,2,1:T(8,128)(2,1)} %param.19) | copy-start | bytes 2359300
  12.9 37.4 %all-to-all-start = ((bf16[32,8,2048]{2,1,0:T(8,128)(2,1)}), bf16[32,8,2048]{2,1,0:T(8,128)(2,1)S(1)}, u32[]{:S(2)}, u32[]{:S(2)}) async-start(bf16[32,8,2048]{2,1,0:T(8,128)(2,1)} %broadcast_in_dim.209), calls=%async_computation | async-start | bytes 2097152 | tf_op jit(solution)/shard_map/all_to_all | solution.py:26
  24.2 3.7 %collective-permute-start.1 = (bf16[2,64]{1,0:T(2,128)(2,1)S(1)}, bf16[2,64]{1,0:T(2,128)(2,1)S(1)}, u32[]{:S(2)}, u32[]{:S(2)}) collective-permute-start(bf16[2,64]{1,0:T(2,128)(2,1)S(1)} %pad_maximum_fusion.4), channel_id=1, source_target_pairs={{0,1},{1,0},{2,3},{3,2},{4,5},{5,4},{6,7},{7,6},{8,9},{9,8},{10,11... | collective-permute-start | bytes 776 | tf_op jit(solution)/shard_map/ppermute | solution.py:14
  51.7 15.2 %all-to-all-start.1 = ((f32[32,2,256]{2,1,0:T(2,128)}), f32[32,2,256]{2,1,0:T(2,128)S(1)}, u32[]{:S(2)}, u32[]{:S(2)}) async-start(f32[32,2,256]{2,1,0:T(2,128)} %broadcast_in_dim.210), calls=%async_computation.1 | async-start | bytes 131072 | tf_op jit(solution)/shard_map/all_to_all | solution.py:26
  58.1 9.0 %collective-permute-start = (f32[640,64]{0,1:T(8,128)S(1)}, f32[640,64]{0,1:T(8,128)S(1)}, u32[]{:S(2)}, u32[]{:S(2)}) collective-permute-start(f32[640,64]{0,1:T(8,128)S(1)} %pad_maximum_fusion.1), channel_id=1, source_target_pairs={{0,1},{1,0},{2,3},{3,2},{4,5},{5,4},{6,7},{7,6},{8,9},{9,8},{10,11... | collective-permute-start | bytes 491528 | tf_op jit(solution)/shard_map/ppermute | solution.py:14
  67.2 31.2 %copy-start.4 = (bf16[256,64]{0,1:T(8,128)(2,1)}, bf16[256,64]{0,1:T(8,128)(2,1)S(1)}, u32[]{:S(2)}) copy-start(bf16[256,64]{0,1:T(8,128)(2,1)S(1)} %get-tuple-element.53) | copy-start | bytes 98308
  67.2 5.9 %collective-permute-start.2 = (bf16[256,2,128]{0,2,1:T(8,128)(2,1)S(1)}, bf16[256,2,128]{0,2,1:T(8,128)(2,1)S(1)}, u32[]{:S(2)}, u32[]{:S(2)}) collective-permute-start(bf16[256,2,128]{0,2,1:T(8,128)(2,1)S(1)} %maximum_select_fusion), channel_id=1, source_target_pairs={{0,32},{32,64},{64,96},{96,128},{128,160},{160,192},{192,224},{1,3... | collective-permute-start | bytes 393224 | tf_op jit(solution)/shard_map/ppermute | solution.py:20
  123.9 3.5 %copy-start.3 = (bf16[64,2048]{1,0:T(8,128)(2,1)S(1)}, bf16[64,2048]{1,0:T(8,128)(2,1)}, u32[]{:S(2)}) copy-start(bf16[64,2048]{1,0:T(8,128)(2,1)} %param.22) | copy-start | bytes 786436
  124.7 13.5 %copy-start.6 = (s32[8,8]{1,0:T(8,128)S(1)}, s32[8,8]{1,0:T(8,128)}, u32[]{:S(2)}) copy-start(s32[8,8]{1,0:T(8,128)} %param.29) | copy-start | bytes 772
  124.7 13.6 %copy-start.7 = (bf16[2048]{0:T(1024)(128)(2,1)S(1)}, bf16[2048]{0:T(1024)(128)(2,1)}, u32[]{:S(2)}) copy-start(bf16[2048]{0:T(1024)(128)(2,1)} %param.28) | copy-start | bytes 12292
  124.8 2.7 collective-permute-start.3
  127.5 37.1 %copy-start.2 = (bf16[8,2048]{1,0:T(8,128)(2,1)S(1)}, bf16[8,2048]{1,0:T(8,128)(2,1)}, u32[]{:S(2)}) copy-start(bf16[8,2048]{1,0:T(8,128)(2,1)} %param.17) | copy-start | bytes 98308
  128.9 35.5 %all-to-all-start.2 = ((bf16[32,8,2048]{2,1,0:T(8,128)(2,1)}), bf16[32,8,2048]{2,1,0:T(8,128)(2,1)S(1)}, u32[]{:S(2)}, u32[]{:S(2)}) async-start(bf16[32,8,2048]{2,1,0:T(8,128)(2,1)} %fusion), calls=%async_computation.2 | async-start | bytes 2097152 | tf_op jit(solution)/shard_map/all_to_all | solution.py:219
  187.2 32.3 %copy-start.10 = (bf16[1,2048,256]{2,1,0:T(8,128)(2,1)S(1)}, bf16[1,2048,256]{2,1,0:T(8,128)(2,1)}, u32[]{:S(2)}) copy-start(bf16[1,2048,256]{2,1,0:T(8,128)(2,1)} %param.31) | copy-start | bytes 3145732
  256.8 6.0 %copy-start.8 = (f32[8,8]{1,0:T(8,128)S(1)}, f32[8,8]{1,0:T(8,128)}, u32[]{:S(2)}) copy-start(f32[8,8]{1,0:T(8,128)} %param.30) | copy-start | bytes 772
  258.5 19.6 %all-to-all-start.6 = ((bf16[32,2,2,2048]{3,2,1,0:T(2,128)(2,1)}), bf16[32,2,2,2048]{3,2,1,0:T(2,128)(2,1)S(1)}, u32[]{:S(2)}, u32[]{:S(2)}) async-start(bf16[32,2,2,2048]{3,2,1,0:T(2,128)(2,1)} %copy.135), calls=%async_computation.6 | async-start | bytes 1048576 | tf_op jit(solution)/shard_map/all_to_all | solution.py:258
Sparse Core Ops, SparseCore 0:
  9.8 75.6 all-gather.2

commit v7 on v6

--- a/solution.py
+++ b/solution.py
@@ -61,7 +61,7 @@
     rows = queries_heads.shape[0]
     split_queries = queries_heads.reshape(rows, 2, HD // 2)
     scores = jnp.einsum(
-        "qcd,ckd->qk", split_queries, halves[:, :, 0], preferred_element_type=jnp.float32
+        "qcd,ckd->qk", split_queries, halves[..., : HD // 2], preferred_element_type=jnp.float32
     )[None] * HD ** (-0.5)
     scores = jnp.where(mask[None], scores, -1e30)
     new_largest = jnp.maximum(largest, jnp.max(scores, axis=-1))
@@ -71,7 +71,7 @@
     update = jnp.einsum(
         "qk,ckd->qcd",
         weights[0].astype(jnp.bfloat16),
-        halves[:, :, 1],
+        halves[..., HD // 2 :],
         preferred_element_type=jnp.float32,
     ).reshape(1, rows, HD)
     accum = accum * factor[:, :, None] + update
@@ -106,7 +106,7 @@
     tok_seq = tok_dev * tensor_size
     columns = w_qkv.shape[2]
     lower_bit = tensor_index % 2
-    prefix_own = jnp.stack([prefix_keys[0], prefix_values[0]], axis=1)
+    prefix_own = jnp.concatenate([prefix_keys[0], prefix_values[0]], axis=-1)
     piece = lax.all_gather(prefix_own[None], ("seq", "tyl"), axis=0, tiled=True)
     gains_in = from_partner(jnp.stack([q_gain, k_gain]))
     normed = rms_scale(tokens.astype(jnp.float32), attn_gain).astype(jnp.bfloat16)

time: 291 us -> 315 us (1.082)
  matrix products: 16.9 us -> 34 us
  other arithmetic: 9.28 us -> 24.8 us
  waiting for transfers between devices: 90.8 us -> 83.2 us
    dot_general x16, matrix products: 6.55 us -> 19.5 us  [the longest x8 16.4 us: attend_halves(): jnp.einsum('qcd,ckd->qk', split_queries, halves[..., :HD // 2], preferred...]
    unnamed x29 -> x92, local copies, waits for them, and re-layouts: 13 us -> 3.47 us
    reduce_sum x8, other arithmetic: 2.63 us -> 11.5 us  [attend_halves(): total = total * factor + jnp.sum(weights, axis=-1)]
    dot_general x9, local copies, waits for them, and re-layouts: 16.5 us -> 23.5 us  [attend_halves(): jnp.einsum('qk,ckd->qcd', weights[0].astype(jnp.bfloat16), halves[..., HD...]
    all_to_all x2, waiting for transfers between devices: 29.9 us -> 26.6 us  [gather_by_exchange(): got = lax.all_to_all(copies, axis, 0, 0, tiled=True)]
  transfers between devices with their start and end apart: 9 -> 9, of which waited for: 8 -> 7; matrix products, arithmetic and copies ran while one was open for 3% -> 5% of each run, Pallas kernels for 0% -> 0%
where the time goes in v7:
time: 315 us; the launch traced here: 310 us
  blocking collectives  84.1 us (27%)
  waiting for transfers between devices  83.2 us (26%)
  starting transfers between devices  35.7 us (11%)
  matrix products  34 us (11%)
  local copies, waits for them, and re-layouts  32.9 us (10%)
  other arithmetic  24.8 us (8%)
  between operations  14.8 us (5%)
    all_to_all x1, blocking collectives, local(): lax.all_to_all(jnp.repeat(per_expert, holders, axis=0), 'seq', 0, 0, tile...  32.2 us
    all_to_all x1, blocking collectives, local(): back = lax.all_to_all(result.astype(jnp.bfloat16), 'seq', 0, 0, tiled=True)  30.7 us
    all_to_all x2, waiting for transfers between devices, gather_by_exchange(): got = lax.all_to_all(copies, axis, 0, 0, tiled=True)  26.6 us
    all_to_all x1, waiting for transfers between devices, local(): lax.all_to_all(attn_partial, TENSOR, 0, 0, tiled=True).astype(jnp.float32)  25.5 us
    dot_general x9, local copies, waits for them, and re-layouts, attend_halves(): jnp.einsum('qk,ckd->qcd', weights[0].astype(jnp.bfloat16), halves[..., HD...  23.5 us
    all_to_all x1, blocking collectives, local(): lax.all_to_all(buffer, TENSOR, split_axis=0, concat_axis=0, tiled=True)  21.2 us
    all_to_all x2, starting transfers between devices, gather_by_exchange(): got = lax.all_to_all(copies, axis, 0, 0, tiled=True)  17.6 us
    dot_general x8, matrix products, attend_halves(): jnp.einsum('qcd,ckd->qk', split_queries, halves[..., :HD // 2], preferred...  16.4 us
  transfers between devices with their start and end apart: 9, of which 7 were waited for; matrix products, arithmetic and copies ran while one was open for 5% of the time, Pallas kernels for 0%

profile of v7, /device:TPU:7, one launch (start us, length us, event | category | flops | bytes accessed | tf_op | source)
XLA Modules:
  0.0 309.5 jit_solution(5779638101638588737)
XLA Ops:
  14.5 11.2 %all-to-all-start = ((bf16[32,8,2048]{2,1,0:T(8,128)(2,1)}), bf16[32,8,2048]{2,1,0:T(8,128)(2,1)S(1)}, u32[]{:S(2)}, u32[]{:S(2)}) async-start(bf16[32,8,2048]{2,1,0:T(8,128)(2,1)} %broadcast_in_dim.209), calls=%async_computation | async-start | bytes 2097152 | tf_op jit(solution)/shard_map/all_to_all | solution.py:26
  32.8 19.1 %all-to-all-done = bf16[32,8,2048]{2,1,0:T(8,128)(2,1)S(1)} async-done(((bf16[32,8,2048]{2,1,0:T(8,128)(2,1)}), bf16[32,8,2048]{2,1,0:T(8,128)(2,1)S(1)}, u32[]{:S(2)}, u32[]{:S(2)}) %all-to-all-start) | async-done | bytes 1048608 | tf_op jit(solution)/shard_map/all_to_all | solution.py:26
  54.4 6.4 %all-to-all-start.1 = ((f32[32,2,256]{2,1,0:T(2,128)}), f32[32,2,256]{2,1,0:T(2,128)S(1)}, u32[]{:S(2)}, u32[]{:S(2)}) async-start(f32[32,2,256]{2,1,0:T(2,128)} %broadcast_in_dim.210), calls=%async_computation.1 | async-start | bytes 131072 | tf_op jit(solution)/shard_map/all_to_all | solution.py:26
  62.1 7.5 %all-to-all-done.1 = f32[32,2,256]{2,1,0:T(2,128)S(1)} async-done(((f32[32,2,256]{2,1,0:T(2,128)}), f32[32,2,256]{2,1,0:T(2,128)S(1)}, u32[]{:S(2)}, u32[]{:S(2)}) %all-to-all-start.1) | async-done | bytes 65568 | tf_op jit(solution)/shard_map/all_to_all | solution.py:26
  71.5 4.5 %collective-permute-done.2 = bf16[256,2,128]{0,2,1:T(8,128)(2,1)S(1)} collective-permute-done((bf16[256,2,128]{0,2,1:T(8,128)(2,1)S(1)}, bf16[256,2,128]{0,2,1:T(8,128)(2,1)S(1)}, u32[]{:S(2)}, u32[]{:S(2)}) %collective-permute-start.2) | collective-permute-done | bytes 131104 | tf_op jit(solution)/shard_map/ppermute | solution.py:20
  77.4 9.6 %all-gather.3.cloned.1.call-done = bf16[32768,128]{1,0:T(8,128)(2,1)} async-done(((bf16[2048,128]{1,0:T(8,128)(2,1)}), bf16[32768,128]{1,0:T(8,128)(2,1)}) %all-gather.3.cloned.1.call-update) | async-done | bytes 8388624 | tf_op jit(solution)/shard_map/all_gather | solution.py:110
  87.0 7.0 %slice_bitcast_fusion = (bf16[2,64,2048]{1,2,0:T(8,128)(2,1)S(1)}, bf16[2,64,2048]{1,2,0:T(8,128)(2,1)}, bf16[2,64,2048]{1,2,0:T(8,128)(2,1)}, bf16[2,64,2048]{1...) fusion(bf16[16,2048,128]{2,1,0:T(8,128)(2,1)} %bitcast.172), kind=kLoop, calls=%fused_computation.55 | loop fusion | bytes 8388608 | tf_op jit(solution)/shard_map/qk,ckd->qcd/dot_general | solution.py:71
  94.9 2.0 fusion.172
  96.9 2.0 fusion.173
  98.9 2.1 fusion.174
  101.0 2.0 fusion.171
  103.0 2.0 fusion.170
  105.0 2.1 fusion.169
  107.1 2.1 fusion.168
  109.2 2.1 fusion.167
  111.3 2.4 copy.131
  113.7 2.3 copy.133
  116.0 2.3 copy.135
  118.3 2.3 copy.137
  120.7 2.4 copy.139
  123.1 2.4 copy.141
  128.7 1.7 fusion.99
  147.4 2.5 collective-permute-done.3
  151.3 9.3 %all-to-all-start.2 = ((bf16[32,8,2048]{2,1,0:T(8,128)(2,1)}), bf16[32,8,2048]{2,1,0:T(8,128)(2,1)S(1)}, u32[]{:S(2)}, u32[]{:S(2)}) async-start(bf16[32,8,2048]{2,1,0:T(8,128)(2,1)} %fusion), calls=%async_computation.2 | async-start | bytes 2097152 | tf_op jit(solution)/shard_map/all_to_all | solution.py:219
  161.3 25.5 %all-to-all-done.2 = bf16[32,8,2048]{2,1,0:T(8,128)(2,1)S(1)} async-done(((bf16[32,8,2048]{2,1,0:T(8,128)(2,1)}), bf16[32,8,2048]{2,1,0:T(8,128)(2,1)S(1)}, u32[]{:S(2)}, u32[]{:S(2)}) %all-to-all-start.2) | async-done | bytes 1048608 | tf_op jit(solution)/shard_map/all_to_all | solution.py:219
  187.8 21.2 %all_to_all.35 = bf16[32,2,2,2048]{3,2,1,0:T(2,128)(2,1)S(1)} all-to-all(bf16[32,2,2,2048]{3,2,1,0:T(2,128)(2,1)S(1)} %reshape.835), channel_id=1, replica_groups=mesh['seq'=8,'th'=16,'tyl'=2] {'th','tyl'}, dimensions={0} | all-to-all | bytes 1048576 | tf_op jit(solution)/shard_map/all_to_all | solution.py:242
  209.5 32.2 %all_to_all.36 = bf16[8,32,2,2048]{3,1,2,0:T(8,128)(2,1)S(1)} all-to-all(bf16[8,32,2,2048]{3,1,2,0:T(8,128)(2,1)S(1)} %bitcast.171), channel_id=1, replica_groups=mesh['seq'=8,'th'=16,'tyl'=2] {'seq'}, dimensions={0} | all-to-all | bytes 4194304 | tf_op jit(solution)/shard_map/all_to_all | solution.py:248
  241.7 2.7 fusion.41
  244.5 5.0 %convolution_convert_fusion = bf16[8,32,2,2048]{3,1,2,0:T(8,128)(2,1)} fusion(bf16[8,32,2,2048]{3,1,2,0:T(8,128)(2,1)S(1)} %all_to_all.36, bf16[1,256,2048]{2,1,0:T(8,128)(2,1)S(1)} %copy-done, bf16[1,2048,256]{2,1,0:T(8,128)(2,1)} %param.32, f32[8,32,2,256]{3,1,2,0:T(8,128)} %fusion.41), kind=kOutput, calls=%fused_computation | convolution fusion | flops 1075576832 | bytes 6815744 | tf_op jit(solution)/shard_map/srcf,fd->srcd/dot_general | solution.py:252
  249.5 30.7 %all_to_all.37 = bf16[8,32,2,2048]{3,1,2,0:T(8,128)(2,1)S(1)} all-to-all(bf16[8,32,2,2048]{3,1,2,0:T(8,128)(2,1)} %convolution_convert_fusion), channel_id=1, replica_groups=mesh['seq'=8,'th'=16,'tyl'=2] {'seq'}, dimensions={0} | all-to-all | bytes 4194304 | tf_op jit(solution)/shard_map/all_to_all | solution.py:253
  281.9 4.3 %all-to-all-start.6 = ((bf16[32,2,2,2048]{3,2,1,0:T(2,128)(2,1)}), bf16[32,2,2,2048]{3,2,1,0:T(2,128)(2,1)S(1)}, u32[]{:S(2)}, u32[]{:S(2)}) async-start(bf16[32,2,2,2048]{3,2,1,0:T(2,128)(2,1)} %copy.147), calls=%async_computation.6 | async-start | bytes 1048576 | tf_op jit(solution)/shard_map/all_to_all | solution.py:258
  286.9 14.6 %all-to-all-done.6 = bf16[32,2,2,2048]{3,2,1,0:T(2,128)(2,1)S(1)} async-done(((bf16[32,2,2,2048]{3,2,1,0:T(2,128)(2,1)}), bf16[32,2,2,2048]{3,2,1,0:T(2,128)(2,1)S(1)}, u32[]{:S(2)}, u32[]{:S(2)}) %all-to-all-start.6) | async-done | bytes 524320 | tf_op jit(solution)/shard_map/all_to_all | solution.py:258
  (178 shorter events, 49.3 us)
Async XLA Ops:
  7.2 237.3 %copy-start = (bf16[1,256,2048]{2,1,0:T(8,128)(2,1)S(1)}, bf16[1,256,2048]{2,1,0:T(8,128)(2,1)}, u32[]{:S(2)}) copy-start(bf16[1,256,2048]{2,1,0:T(8,128)(2,1)} %param.33) | copy-start | bytes 3145732
  7.2 79.8 %all-gather.3.cloned.1.call-start = ((), (), s32[]{:S(2)}) async-start(), calls=%async_computation.7 | async-start | bytes 8912896 | tf_op jit(solution)/shard_map/all_gather | solution.py:110
  14.5 37.4 %all-to-all-start = ((bf16[32,8,2048]{2,1,0:T(8,128)(2,1)}), bf16[32,8,2048]{2,1,0:T(8,128)(2,1)S(1)}, u32[]{:S(2)}, u32[]{:S(2)}) async-start(bf16[32,8,2048]{2,1,0:T(8,128)(2,1)} %broadcast_in_dim.209), calls=%async_computation | async-start | bytes 2097152 | tf_op jit(solution)/shard_map/all_to_all | solution.py:26
  26.4 6.4 %collective-permute-start.1 = (bf16[2,64]{1,0:T(2,128)(2,1)S(1)}, bf16[2,64]{1,0:T(2,128)(2,1)S(1)}, u32[]{:S(2)}, u32[]{:S(2)}) collective-permute-start(bf16[2,64]{1,0:T(2,128)(2,1)S(1)} %pad_maximum_fusion.4), channel_id=1, source_target_pairs={{0,1},{1,0},{2,3},{3,2},{4,5},{5,4},{6,7},{7,6},{8,9},{9,8},{10,11... | collective-permute-start | bytes 776 | tf_op jit(solution)/shard_map/ppermute | solution.py:14
  29.8 57.2 %copy-start.39 = (s32[128]{0:T(128)}, s32[128]{0:T(128)S(1)}, u32[]{:S(2)}) copy-start(s32[128]{0:T(128)S(1)} %dynamic_slice.28) | copy-start | bytes 1540
  30.7 56.3 %copy-start.40 = (s32[128]{0:T(128)}, s32[128]{0:T(128)S(1)}, u32[]{:S(2)}) copy-start(s32[128]{0:T(128)S(1)} %iota_add_fusion.1) | copy-start | bytes 1540
  54.4 15.2 %all-to-all-start.1 = ((f32[32,2,256]{2,1,0:T(2,128)}), f32[32,2,256]{2,1,0:T(2,128)S(1)}, u32[]{:S(2)}, u32[]{:S(2)}) async-start(f32[32,2,256]{2,1,0:T(2,128)} %broadcast_in_dim.210), calls=%async_computation.1 | async-start | bytes 131072 | tf_op jit(solution)/shard_map/all_to_all | solution.py:26
  60.8 9.0 %collective-permute-start = (f32[640,64]{0,1:T(8,128)S(1)}, f32[640,64]{0,1:T(8,128)S(1)}, u32[]{:S(2)}, u32[]{:S(2)}) collective-permute-start(f32[640,64]{0,1:T(8,128)S(1)} %pad_maximum_fusion.1), channel_id=1, source_target_pairs={{0,1},{1,0},{2,3},{3,2},{4,5},{5,4},{6,7},{7,6},{8,9},{9,8},{10,11... | collective-permute-start | bytes 491528 | tf_op jit(solution)/shard_map/ppermute | solution.py:14
  69.9 24.2 %copy-start.21 = (bf16[256,64]{0,1:T(8,128)(2,1)}, bf16[256,64]{0,1:T(8,128)(2,1)S(1)}, u32[]{:S(2)}) copy-start(bf16[256,64]{0,1:T(8,128)(2,1)S(1)} %get-tuple-element.45) | copy-start | bytes 98308
  69.9 6.0 %collective-permute-start.2 = (bf16[256,2,128]{0,2,1:T(8,128)(2,1)S(1)}, bf16[256,2,128]{0,2,1:T(8,128)(2,1)S(1)}, u32[]{:S(2)}, u32[]{:S(2)}) collective-permute-start(bf16[256,2,128]{0,2,1:T(8,128)(2,1)S(1)} %maximum_select_fusion), channel_id=1, source_target_pairs={{0,32},{32,64},{64,96},{96,128},{128,160},{160,192},{192,224},{1,3... | collective-permute-start | bytes 393224 | tf_op jit(solution)/shard_map/ppermute | solution.py:20
  107.1 20.7 %copy-start.38 = (f32[128]{0:T(128)S(1)}, f32[128]{0:T(128)}, u32[]{:S(2)}) copy-start(f32[128]{0:T(128)} %get-tuple-element.77) | copy-start | bytes 1540
  107.1 23.3 %copy-start.32 = (pred[128]{0:T(512)(128)(4,1)S(1)}, pred[128]{0:T(512)(128)(4,1)}, u32[]{:S(2)}) copy-start(pred[128]{0:T(512)(128)(4,1)} %get-tuple-element.49) | copy-start | bytes 388
  109.2 22.8 %copy-start.30 = (pred[128]{0:T(512)(128)(4,1)S(1)}, pred[128]{0:T(512)(128)(4,1)}, u32[]{:S(2)}) copy-start(pred[128]{0:T(512)(128)(4,1)} %get-tuple-element.56) | copy-start | bytes 388
  109.2 24.5 %copy-start.28 = (pred[128]{0:T(512)(128)(4,1)S(1)}, pred[128]{0:T(512)(128)(4,1)}, u32[]{:S(2)}) copy-start(pred[128]{0:T(512)(128)(4,1)} %get-tuple-element.55) | copy-start | bytes 388
  111.3 16.5 %copy-start.41 = (f32[128]{0:T(128)S(1)}, f32[128]{0:T(128)}, u32[]{:S(2)}) copy-start(f32[128]{0:T(128)} %get-tuple-element.63) | copy-start | bytes 1540
  111.3 16.5 %copy-start.42 = (f32[128]{0:T(128)S(1)}, f32[128]{0:T(128)}, u32[]{:S(2)}) copy-start(f32[128]{0:T(128)} %get-tuple-element.61) | copy-start | bytes 1540
  111.3 23.9 %copy-start.26 = (pred[128]{0:T(512)(128)(4,1)S(1)}, pred[128]{0:T(512)(128)(4,1)}, u32[]{:S(2)}) copy-start(pred[128]{0:T(512)(128)(4,1)} %get-tuple-element.54) | copy-start | bytes 388
  111.3 25.5 %copy-start.24 = (pred[128]{0:T(512)(128)(4,1)S(1)}, pred[128]{0:T(512)(128)(4,1)}, u32[]{:S(2)}) copy-start(pred[128]{0:T(512)(128)(4,1)} %get-tuple-element.53) | copy-start | bytes 388
  116.0 24.4 %copy-start.36 = (pred[128]{0:T(512)(128)(4,1)S(1)}, pred[128]{0:T(512)(128)(4,1)}, u32[]{:S(2)}) copy-start(pred[128]{0:T(512)(128)(4,1)} %get-tuple-element.50) | copy-start | bytes 388
  127.7 16.7 %copy-start.5 = (f32[128,2048]{1,0:T(8,128)S(1)}, f32[128,2048]{1,0:T(8,128)}, u32[]{:S(2)}) copy-start(f32[128,2048]{1,0:T(8,128)} %get-tuple-element.72) | copy-start | bytes 3145732
  127.8 16.7 %copy-start.13 = (bf16[2,64,2048]{2,1,0:T(8,128)(2,1)S(1)}, bf16[2,64,2048]{2,1,0:T(8,128)(2,1)}, u32[]{:S(2)}) copy-start(bf16[2,64,2048]{2,1,0:T(8,128)(2,1)} %copy.135) | copy-start | bytes 1572868
  127.8 17.1 %copy-start.6 = (f32[128,2048]{1,0:T(8,128)S(1)}, f32[128,2048]{1,0:T(8,128)}, u32[]{:S(2)}) copy-start(f32[128,2048]{1,0:T(8,128)} %get-tuple-element.70) | copy-start | bytes 3145732
  127.8 17.1 %copy-start.12 = (bf16[2,64,2048]{2,1,0:T(8,128)(2,1)S(1)}, bf16[2,64,2048]{2,1,0:T(8,128)(2,1)}, u32[]{:S(2)}) copy-start(bf16[2,64,2048]{2,1,0:T(8,128)(2,1)} %copy.137) | copy-start | bytes 1572868
  127.8 17.5 %copy-start.4 = (f32[128,2048]{1,0:T(8,128)S(1)}, f32[128,2048]{1,0:T(8,128)}, u32[]{:S(2)}) copy-start(f32[128,2048]{1,0:T(8,128)} %get-tuple-element.68) | copy-start | bytes 3145732
  127.8 17.5 %copy-start.11 = (bf16[2,64,2048]{2,1,0:T(8,128)(2,1)S(1)}, bf16[2,64,2048]{2,1,0:T(8,128)(2,1)}, u32[]{:S(2)}) copy-start(bf16[2,64,2048]{2,1,0:T(8,128)(2,1)} %copy.139) | copy-start | bytes 1572868
  143.6 17.0 %copy-start.22 = (s32[8,8]{1,0:T(8,128)S(1)}, s32[8,8]{1,0:T(8,128)}, u32[]{:S(2)}) copy-start(s32[8,8]{1,0:T(8,128)} %param.29) | copy-start | bytes 772
  143.6 17.5 %copy-start.33 = (bf16[2048]{0:T(1024)(128)(2,1)S(1)}, bf16[2048]{0:T(1024)(128)(2,1)}, u32[]{:S(2)}) copy-start(bf16[2048]{0:T(1024)(128)(2,1)} %param.28) | copy-start | bytes 12292
  144.1 42.9 %copy-start.18 = (bf16[8,2048]{1,0:T(8,128)(2,1)S(1)}, bf16[8,2048]{1,0:T(8,128)(2,1)}, u32[]{:S(2)}) copy-start(bf16[8,2048]{1,0:T(8,128)(2,1)} %param.17) | copy-start | bytes 98308
  147.0 2.9 collective-permute-start.3
  151.3 35.4 %all-to-all-start.2 = ((bf16[32,8,2048]{2,1,0:T(8,128)(2,1)}), bf16[32,8,2048]{2,1,0:T(8,128)(2,1)S(1)}, u32[]{:S(2)}, u32[]{:S(2)}) async-start(bf16[32,8,2048]{2,1,0:T(8,128)(2,1)} %fusion), calls=%async_computation.2 | async-start | bytes 2097152 | tf_op jit(solution)/shard_map/all_to_all | solution.py:219
  244.5 41.7 %copy-start.34 = (f32[8,8]{1,0:T(8,128)S(1)}, f32[8,8]{1,0:T(8,128)}, u32[]{:S(2)}) copy-start(f32[8,8]{1,0:T(8,128)} %param.30) | copy-start | bytes 772
  281.9 19.6 %all-to-all-start.6 = ((bf16[32,2,2,2048]{3,2,1,0:T(2,128)(2,1)}), bf16[32,2,2,2048]{3,2,1,0:T(2,128)(2,1)S(1)}, u32[]{:S(2)}, u32[]{:S(2)}) async-start(bf16[32,2,2,2048]{3,2,1,0:T(2,128)(2,1)} %copy.147), calls=%async_computation.6 | async-start | bytes 1048576 | tf_op jit(solution)/shard_map/all_to_all | solution.py:258
  (22 other events, 271.7 us)
Sparse Core Ops, SparseCore 0:
  11.0 75.9 all-gather.2

commit v8 on v6

--- a/solution.py
+++ b/solution.py
@@ -52,28 +52,6 @@
         value_block,
         preferred_element_type=jnp.float32,
     )
-    accum = accum * factor[:, :, None] + update
-    return (new_largest, total, accum)
-
-
-def attend_halves(carry, queries_heads, halves, mask):
-    largest, total, accum = carry
-    rows = queries_heads.shape[0]
-    split_queries = queries_heads.reshape(rows, 2, HD // 2)
-    scores = jnp.einsum(
-        "qcd,ckd->qk", split_queries, halves[:, :, 0], preferred_element_type=jnp.float32
-    )[None] * HD ** (-0.5)
-    scores = jnp.where(mask[None], scores, -1e30)
-    new_largest = jnp.maximum(largest, jnp.max(scores, axis=-1))
-    weights = jnp.where(mask[None], jnp.exp(scores - new_largest[:, :, None]), 0.0)
-    factor = jnp.exp(largest - new_largest)
-    total = total * factor + jnp.sum(weights, axis=-1)
-    update = jnp.einsum(
-        "qk,ckd->qcd",
-        weights[0].astype(jnp.bfloat16),
-        halves[:, :, 1],
-        preferred_element_type=jnp.float32,
-    ).reshape(1, rows, HD)
     accum = accum * factor[:, :, None] + update
     return (new_largest, total, accum)
 
@@ -107,8 +85,20 @@
     columns = w_qkv.shape[2]
     lower_bit = tensor_index % 2
     prefix_own = jnp.stack([prefix_keys[0], prefix_values[0]], axis=1)
-    piece = lax.all_gather(prefix_own[None], ("seq", "tyl"), axis=0, tiled=True)
+    prefix_partner = from_partner(prefix_own)
+    prefix_full = jnp.where(
+        lower_bit == 0,
+        jnp.concatenate([prefix_own, prefix_partner], axis=-1),
+        jnp.concatenate([prefix_partner, prefix_own], axis=-1),
+    )
+    piece = lax.all_gather(prefix_full[None], "seq", axis=0, tiled=True)
     gains_in = from_partner(jnp.stack([q_gain, k_gain]))
+    out_partner = from_partner(w_out)
+    out_head = jnp.where(
+        lower_bit == 0,
+        jnp.concatenate([w_out, out_partner], axis=0),
+        jnp.concatenate([out_partner, w_out], axis=0),
+    )
     normed = rms_scale(tokens.astype(jnp.float32), attn_gain).astype(jnp.bfloat16)
     w_flat = w_qkv.reshape(width, 3 * columns)
     rows = gather_by_exchange(normed, TENSOR).reshape(tok_seq, width)
@@ -124,9 +114,15 @@
         [jnp.sum(query_part * query_part, axis=-1), jnp.sum(key_part * key_part, axis=-1)]
     )
     half_rows = tok_seq // 2
-    query_halves = query_part.reshape(2, half_rows, columns)
-    own_half = lax.dynamic_index_in_dim(query_halves, lower_bit, 0, keepdims=False)
-    send_half = lax.dynamic_index_in_dim(query_halves, 1 - lower_bit, 0, keepdims=False)
+    row_blocks = half_rows // tok_dev
+
+    def own_rows(values, mine=True):
+        blocks = values.reshape((row_blocks, 2, tok_dev) + values.shape[1:])
+        first, second = (blocks[:, 0], blocks[:, 1]) if mine else (blocks[:, 1], blocks[:, 0])
+        return jnp.where(lower_bit == 0, first, second).reshape((half_rows,) + values.shape[1:])
+
+    own_half = own_rows(query_part)
+    send_half = own_rows(query_part, mine=False)
     raw_out = jnp.concatenate([send_half, key_part, value_part], axis=0)
     raw_out, partial_squares = lax.optimization_barrier((raw_out, partial_squares))
     raw_in = from_partner(raw_out)
@@ -136,9 +132,7 @@
     squares = jnp.sum(gather_by_exchange(partial_squares, TENSOR), axis=0)
     query_scale = lax.rsqrt(squares[0] / width + 1e-05)[:, None]
     key_scale = lax.rsqrt(squares[1] / width + 1e-05)[:, None]
-    own_scale = lax.dynamic_index_in_dim(
-        query_scale.reshape(2, half_rows, 1), lower_bit, 0, keepdims=False
-    )
+    own_scale = own_rows(query_scale)
     own_query = (own_half * own_scale * q_gain.astype(jnp.float32)).astype(jnp.bfloat16)
     got_query = (got_half * own_scale * gains_in[0].astype(jnp.float32)).astype(jnp.bfloat16)
     new_keys = (key_part * key_scale * k_gain.astype(jnp.float32)).astype(jnp.bfloat16)
@@ -156,7 +150,6 @@
         jnp.concatenate([own_query, got_query], axis=-1),
         jnp.concatenate([got_query, own_query], axis=-1),
     )
-    query_offset = lower_bit * half_rows
     heads_local = 1
     queries_heads = query_full.reshape(half_rows, heads_local, HD)
     groups_count = prefix_owner.shape[0]
@@ -170,10 +163,9 @@
         axis=1,
     )
     base_row = seq_index * tok_seq
-    query_start = base_row + query_offset
-    query_seg = lax.dynamic_slice_in_dim(segments, query_start, half_rows, 0)
-    query_group = lax.dynamic_slice_in_dim(token_group, query_start, half_rows, 0)
-    query_pos = query_start + jnp.arange(half_rows, dtype=jnp.int32)
+    query_seg = own_rows(lax.dynamic_slice_in_dim(segments, base_row, tok_seq, 0))
+    query_group = own_rows(lax.dynamic_slice_in_dim(token_group, base_row, tok_seq, 0))
+    query_pos = own_rows(base_row + jnp.arange(tok_seq, dtype=jnp.int32))
     padded_seg = jnp.concatenate([jnp.full((tok_seq,), -1, jnp.int32), segments], axis=0)
     key_seg = lax.dynamic_slice_in_dim(padded_seg, base_row, 2 * tok_seq, 0)
     key_pos = base_row - tok_seq + jnp.arange(2 * tok_seq, dtype=jnp.int32)
@@ -198,25 +190,16 @@
     )
     state = carry
     start = jnp.int32(0)
-    for offset in range(seq_size):
+    for offset in range(piece.shape[0]):
         slot_mask = (owner_of_query == start + offset)[:, None]
-        state = attend_halves(state, queries_heads, piece[2 * offset : 2 * offset + 2], slot_mask)
+        state = attend_block(state, queries_heads, piece[offset], slot_mask)
     carry = state
     attended = (carry[2] / carry[1][:, :, None]).astype(jnp.bfloat16)
     attended = jnp.transpose(attended, (1, 0, 2)).reshape(half_rows, heads_local * HD)
-    split_out = attended.reshape(half_rows, 2, columns)
-    own_out = lax.dynamic_index_in_dim(split_out, lower_bit, 1, keepdims=False)
-    send_out = lax.dynamic_index_in_dim(split_out, 1 - lower_bit, 1, keepdims=False)
-    got_out = from_partner(send_out)
-    attended_local = jnp.where(
-        lower_bit == 0,
-        jnp.concatenate([own_out, got_out], axis=0),
-        jnp.concatenate([got_out, own_out], axis=0),
-    )
-    attn_partial = jnp.dot(attended_local, w_out, preferred_element_type=jnp.float32)
-    attn_partial = attn_partial.astype(jnp.bfloat16).reshape(tensor_size, tok_dev, width)
+    attn_partial = jnp.dot(attended, out_head, preferred_element_type=jnp.float32)
+    attn_partial = attn_partial.astype(jnp.bfloat16).reshape(row_blocks, tok_dev, width)
     attn_sum = jnp.sum(
-        lax.all_to_all(attn_partial, TENSOR, 0, 0, tiled=True).astype(jnp.float32), axis=0
+        lax.all_to_all(attn_partial, "th", 0, 0, tiled=True).astype(jnp.float32), axis=0
     )
     mixed_rows = (tokens.astype(jnp.float32) + attn_sum).astype(jnp.bfloat16)
     expert_in = rms_scale(mixed_rows.astype(jnp.float32), mlp_gain).astype(jnp.bfloat16)

time: 291 us -> 249 us (0.86)
  local copies, waits for them, and re-layouts: 34.7 us -> 11.2 us
  waiting for transfers between devices: 90.8 us -> 74.5 us
  starting transfers between devices: 35.6 us -> 32.2 us
    dot_general x9 -> x0, local copies, waits for them, and re-layouts: 16.5 us -> none  [attend_halves(): jnp.einsum('qk,ckd->qcd', weights[0].astype(jnp.bfloat16), halves[:, :, 1...]
    unnamed x29 -> x70, local copies, waits for them, and re-layouts: 13 us -> 0.17 us
    all_to_all x1, waiting for transfers between devices: 25.5 us -> 13.5 us  [local(): lax.all_to_all(attn_partial, 'th', 0, 0, tiled=True).astype(jnp.float32)]
    all_gather x1, waiting for transfers between devices: 12 us -> 0.01 us  [local(): piece = lax.all_gather(prefix_full[None], 'seq', axis=0, tiled=True)]
    ppermute x3 -> x4, waiting for transfers between devices: 4.22 us -> 11.8 us  [from_partner(): return lax.ppermute(value, 'tyl', [(0, 1), (1, 0)])]
    all_to_all x1, blocking collectives: 32.3 us -> 38.3 us  [local(): lax.all_to_all(jnp.repeat(per_expert, holders, axis=0), 'seq', 0, 0, tile...]
    dot_general x17 -> x1, matrix products: 8 us -> 2.6 us  [local(): jnp.dot(attended, out_head, preferred_element_type=jnp.float32)]
    all_to_all x1, starting transfers between devices: 9.33 us -> 4.35 us  [local(): lax.all_to_all(attn_partial, 'th', 0, 0, tiled=True).astype(jnp.float32)]
  transfers between devices with their start and end apart: 9 -> 10, of which waited for: 8 -> 7; matrix products, arithmetic and copies ran while one was open for 3% -> 8% of each run, Pallas kernels for 0% -> 0%
where the time goes in v8:
time: 249 us; the launch traced here: 245 us
  blocking collectives  86.9 us (35%)
  waiting for transfers between devices  74.5 us (30%)
  starting transfers between devices  32.2 us (13%)
  matrix products  18.5 us (7%)
  between operations  14.8 us (6%)
  local copies, waits for them, and re-layouts  11.2 us (4%)
  other arithmetic  6.98 us (3%)
    all_to_all x1, blocking collectives, local(): lax.all_to_all(jnp.repeat(per_expert, holders, axis=0), 'seq', 0, 0, tile...  38.3 us
    all_to_all x1, blocking collectives, local(): back = lax.all_to_all(result.astype(jnp.bfloat16), 'seq', 0, 0, tiled=True)  30.7 us
    all_to_all x2, waiting for transfers between devices, gather_by_exchange(): got = lax.all_to_all(copies, axis, 0, 0, tiled=True)  30.1 us
    all_to_all x1, blocking collectives, local(): lax.all_to_all(buffer, TENSOR, split_axis=0, concat_axis=0, tiled=True)  17.9 us
    all_to_all x2, starting transfers between devices, gather_by_exchange(): got = lax.all_to_all(copies, axis, 0, 0, tiled=True)  17.8 us
    all_to_all x1, waiting for transfers between devices, local(): lax.all_to_all(summed.astype(jnp.bfloat16), TENSOR, split_axis=0, concat_...  14.6 us
    all_to_all x1, waiting for transfers between devices, local(): lax.all_to_all(attn_partial, 'th', 0, 0, tiled=True).astype(jnp.float32)  13.5 us
    ppermute x4, waiting for transfers between devices, from_partner(): return lax.ppermute(value, 'tyl', [(0, 1), (1, 0)])  11.8 us
  transfers between devices with their start and end apart: 10, of which 7 were waited for; matrix products, arithmetic and copies ran while one was open for 8% of the time, Pallas kernels for 0%

profile of v8, /device:TPU:7, one launch (start us, length us, event | category | flops | bytes accessed | tf_op | source)
XLA Modules:
  0.0 245.1 jit_solution(16104287990824385249)
XLA Ops:
  7.2 1.2 fusion.151
  8.4 1.4 collective-permute-start.3
  9.8 11.5 %collective-permute-done.3 = bf16[2048,2,64]{0,2,1:T(8,128)(2,1)S(1)} collective-permute-done((bf16[2048,2,64]{0,2,1:T(8,128)(2,1)S(1)}, bf16[2048,2,64]{0,2,1:T(8,128)(2,1)S(1)}, u32[]{:S(2)}, u32[]{:S(2)}) %collective-permute-start.3) | collective-permute-done | bytes 524320 | tf_op jit(solution)/shard_map/ppermute | solution.py:14
  21.6 1.4 copy.50
  23.3 1.1 broadcast_in_dim.196
  24.4 11.2 %all-to-all-start = ((bf16[32,8,2048]{2,1,0:T(8,128)(2,1)}), bf16[32,8,2048]{2,1,0:T(8,128)(2,1)S(1)}, u32[]{:S(2)}, u32[]{:S(2)}) async-start(bf16[32,8,2048]{2,1,0:T(8,128)(2,1)} %broadcast_in_dim.196), calls=%async_computation | async-start | bytes 2097152 | tf_op jit(solution)/shard_map/all_to_all | solution.py:26
  35.6 1.3 collective-permute-start.1
  38.7 22.7 %all-to-all-done = bf16[32,8,2048]{2,1,0:T(8,128)(2,1)S(1)} async-done(((bf16[32,8,2048]{2,1,0:T(8,128)(2,1)}), bf16[32,8,2048]{2,1,0:T(8,128)(2,1)S(1)}, u32[]{:S(2)}, u32[]{:S(2)}) %all-to-all-start) | async-done | bytes 1048608 | tf_op jit(solution)/shard_map/all_to_all | solution.py:26
  61.3 0.5 fusion.27
  62.1 0.6 broadcast_in_dim.197
  62.8 6.6 %all-to-all-start.1 = ((f32[32,2,256]{2,1,0:T(2,128)}), f32[32,2,256]{2,1,0:T(2,128)S(1)}, u32[]{:S(2)}, u32[]{:S(2)}) async-start(f32[32,2,256]{2,1,0:T(2,128)} %broadcast_in_dim.197), calls=%async_computation.1 | async-start | bytes 131072 | tf_op jit(solution)/shard_map/all_to_all | solution.py:26
  69.4 1.3 collective-permute-start
  70.8 7.5 %all-to-all-done.1 = f32[32,2,256]{2,1,0:T(2,128)S(1)} async-done(((f32[32,2,256]{2,1,0:T(2,128)}), f32[32,2,256]{2,1,0:T(2,128)S(1)}, u32[]{:S(2)}, u32[]{:S(2)}) %all-to-all-start.1) | async-done | bytes 65568 | tf_op jit(solution)/shard_map/all_to_all | solution.py:26
  78.7 1.5 collective-permute-start.2
  80.3 4.5 %collective-permute-done.2 = bf16[256,2,128]{0,2,1:T(8,128)(2,1)S(1)} collective-permute-done((bf16[256,2,128]{0,2,1:T(8,128)(2,1)S(1)}, bf16[256,2,128]{0,2,1:T(8,128)(2,1)S(1)}, u32[]{:S(2)}, u32[]{:S(2)}) %collective-permute-start.2) | collective-permute-done | bytes 131104 | tf_op jit(solution)/shard_map/ppermute | solution.py:20
  84.8 1.4 fusion.163
  86.2 3.7 %slice_bitcast_fusion.7 = (bf16[2048,2,128]{2,0,1:T(8,128)(2,1)S(1)}, bf16[2048,2,128]{2,0,1:T(8,128)(2,1)S(1)}, bf16[2048,2,128]{2,0,1:T(8,128)(2,1)S(1)}, bf16...) fusion(bf16[8,2048,2,128]{3,1,2,0:T(8,128)(2,1)} %all-gather.2., ...), kind=kLoop, calls=%fused_computation.53 | loop fusion | bytes 16777216 | tf_op jit(solution)/shard_map/squeeze | solution.py:195
  91.7 0.4 fusion.158
  96.4 0.5 multiply_add_fusion.1
  99.8 2.6 %fusion.8 = bf16[16,8,2048]{2,1,0:T(8,128)(2,1)} fusion(f32[128,128]{1,0:T(8,128)S(1)} %fusion.13, f32[128,2048]{1,0:T(8,128)S(1)} %get-tuple-element.62, bf16[2048,2,128]{2,0,1:T(8,128)(2,1)S(1)} %get-tuple-element.29, bf16[64,2048]{1,0:T(8,128)(2,1)} %collective-permute-done.4, bf16[64,2048]{1,0:T(8,128)(2,1)} %param.22, f32[128]{0:T(128)S(1)} %get-tuple-element.20, ...), kind=kOutput, calls=%fused_computation.19 | convolution fusion | flops 137674752 | bytes 2688513 | tf_op jit(solution)/shard_map/dot_general | solution.py:199
  102.4 4.4 %all-to-all-start.2 = ((bf16[16,8,2048]{2,1,0:T(8,128)(2,1)}), bf16[16,8,2048]{2,1,0:T(8,128)(2,1)S(1)}, u32[]{:S(2)}, u32[]{:S(2)}) async-start(bf16[16,8,2048]{2,1,0:T(8,128)(2,1)} %fusion.8), calls=%async_computation.2 | async-start | bytes 1048576 | tf_op jit(solution)/shard_map/all_to_all | solution.py:202
  107.4 13.5 %all-to-all-done.2 = bf16[16,8,2048]{2,1,0:T(8,128)(2,1)S(1)} async-done(((bf16[16,8,2048]{2,1,0:T(8,128)(2,1)}), bf16[16,8,2048]{2,1,0:T(8,128)(2,1)S(1)}, u32[]{:S(2)}, u32[]{:S(2)}) %all-to-all-start.2) | async-done | bytes 524320 | tf_op jit(solution)/shard_map/all_to_all | solution.py:202
  121.8 17.9 %all_to_all.35 = bf16[32,2,2,2048]{3,2,1,0:T(2,128)(2,1)S(1)} all-to-all(bf16[32,2,2,2048]{3,2,1,0:T(2,128)(2,1)S(1)} %reshape.1034), channel_id=1, replica_groups=mesh['seq'=8,'th'=16,'tyl'=2] {'th','tyl'}, dimensions={0} | all-to-all | bytes 1048576 | tf_op jit(solution)/shard_map/all_to_all | solution.py:225
  140.3 38.3 %all_to_all.36 = bf16[8,32,2,2048]{3,1,2,0:T(8,128)(2,1)S(1)} all-to-all(bf16[8,32,2,2048]{3,1,2,0:T(8,128)(2,1)S(1)} %bitcast.156), channel_id=1, replica_groups=mesh['seq'=8,'th'=16,'tyl'=2] {'seq'}, dimensions={0} | all-to-all | bytes 4194304 | tf_op jit(solution)/shard_map/all_to_all | solution.py:231
  178.5 1.5 fusion.25
  180.0 5.0 %convolution_convert_fusion = bf16[8,32,2,2048]{3,1,2,0:T(8,128)(2,1)} fusion(bf16[8,32,2,2048]{3,1,2,0:T(8,128)(2,1)S(1)} %all_to_all.36, bf16[1,256,2048]{2,1,0:T(8,128)(2,1)S(1)} %copy-done, bf16[1,2048,256]{2,1,0:T(8,128)(2,1)} %param.32, f32[8,32,2,256]{3,1,2,0:T(8,128)} %fusion.25), kind=kOutput, calls=%fused_computation | convolution fusion | flops 1075576832 | bytes 6815744 | tf_op jit(solution)/shard_map/srcf,fd->srcd/dot_general | solution.py:235
  185.1 30.7 %all_to_all.37 = bf16[8,32,2,2048]{3,1,2,0:T(8,128)(2,1)S(1)} all-to-all(bf16[8,32,2,2048]{3,1,2,0:T(8,128)(2,1)} %convolution_convert_fusion), channel_id=1, replica_groups=mesh['seq'=8,'th'=16,'tyl'=2] {'seq'}, dimensions={0} | all-to-all | bytes 4194304 | tf_op jit(solution)/shard_map/all_to_all | solution.py:236
  216.2 1.3 copy.52
  217.5 4.3 %all-to-all-start.6 = ((bf16[32,2,2,2048]{3,2,1,0:T(2,128)(2,1)}), bf16[32,2,2,2048]{3,2,1,0:T(2,128)(2,1)S(1)}, u32[]{:S(2)}, u32[]{:S(2)}) async-start(bf16[32,2,2,2048]{3,2,1,0:T(2,128)(2,1)} %copy.52), calls=%async_computation.6 | async-start | bytes 1048576 | tf_op jit(solution)/shard_map/all_to_all | solution.py:241
  221.9 0.6 slice.327
  222.5 14.6 %all-to-all-done.6 = bf16[32,2,2,2048]{3,2,1,0:T(2,128)(2,1)S(1)} async-done(((bf16[32,2,2,2048]{3,2,1,0:T(2,128)(2,1)}), bf16[32,2,2,2048]{3,2,1,0:T(2,128)(2,1)S(1)}, u32[]{:S(2)}, u32[]{:S(2)}) %all-to-all-start.6) | async-done | bytes 524320 | tf_op jit(solution)/shard_map/all_to_all | solution.py:241
  237.3 0.9 fusion.9
  (160 shorter events, 14.3 us)
Async XLA Ops:
  7.2 172.9 %copy-start = (bf16[1,256,2048]{2,1,0:T(8,128)(2,1)S(1)}, bf16[1,256,2048]{2,1,0:T(8,128)(2,1)}, u32[]{:S(2)}) copy-start(bf16[1,256,2048]{2,1,0:T(8,128)(2,1)} %param.33) | copy-start | bytes 3145732
  7.2 79.0 %all-gather.2.cloned.1.call-start = ((), (), s32[]{:S(2)}) async-start(), calls=%async_computation.7 | async-start | bytes 9437184 | tf_op jit(solution)/shard_map/all_gather | solution.py:94
  8.4 12.9 %collective-permute-start.3 = (bf16[2048,2,64]{0,2,1:T(8,128)(2,1)S(1)}, bf16[2048,2,64]{0,2,1:T(8,128)(2,1)S(1)}, u32[]{:S(2)}, u32[]{:S(2)}) collective-permute-start(bf16[2048,2,64]{0,2,1:T(8,128)(2,1)S(1)} %get-tuple-element.37), channel_id=1, source_target_pairs={{0,1},{1,0},{2,3},{3,2},{4,5},{5,4},{6,7},{7,6},{8,9},{9,8},{10,11... | collective-permute-start | bytes 1572872 | tf_op jit(solution)/shard_map/ppermute | solution.py:14
  23.0 12.6 %copy-start.32 = (bf16[64]{0:T(256)(128)(2,1)S(1)}, bf16[64]{0:T(256)(128)(2,1)}, u32[]{:S(2)}) copy-start(bf16[64]{0:T(256)(128)(2,1)} %param.20) | copy-start | bytes 388
  23.0 12.6 %copy-start.34 = (bf16[64]{0:T(256)(128)(2,1)S(1)}, bf16[64]{0:T(256)(128)(2,1)}, u32[]{:S(2)}) copy-start(bf16[64]{0:T(256)(128)(2,1)} %param.21) | copy-start | bytes 388
  23.0 14.2 %copy-start.5 = (s32[2048]{0:T(1024)S(1)}, s32[2048]{0:T(1024)}, u32[]{:S(2)}) copy-start(s32[2048]{0:T(1024)} %param.25) | copy-start | bytes 24580
  23.0 14.3 %copy-start.28 = (s32[32]{0:T(128)S(1)}, s32[32]{0:T(128)}, u32[]{:S(2)}) copy-start(s32[32]{0:T(128)} %param.26) | copy-start | bytes 388
  23.0 14.9 %copy-start.33 = (s32[4]{0:T(128)S(1)}, s32[4]{0:T(128)}, u32[]{:S(2)}) copy-start(s32[4]{0:T(128)} %param.27) | copy-start | bytes 52
  23.0 38.3 %copy-start.1 = (bf16[2048,3,64]{0,2,1:T(8,128)(2,1)S(1)}, bf16[2048,3,64]{0,2,1:T(8,128)(2,1)}, u32[]{:S(2)}) copy-start(bf16[2048,3,64]{0,2,1:T(8,128)(2,1)} %param.19) | copy-start | bytes 2359300
  24.4 37.0 %all-to-all-start = ((bf16[32,8,2048]{2,1,0:T(8,128)(2,1)}), bf16[32,8,2048]{2,1,0:T(8,128)(2,1)S(1)}, u32[]{:S(2)}, u32[]{:S(2)}) async-start(bf16[32,8,2048]{2,1,0:T(8,128)(2,1)} %broadcast_in_dim.196), calls=%async_computation | async-start | bytes 2097152 | tf_op jit(solution)/shard_map/all_to_all | solution.py:26
  35.6 3.0 %collective-permute-start.1 = (bf16[2,64]{1,0:T(2,128)(2,1)S(1)}, bf16[2,64]{1,0:T(2,128)(2,1)S(1)}, u32[]{:S(2)}, u32[]{:S(2)}) collective-permute-start(bf16[2,64]{1,0:T(2,128)(2,1)S(1)} %pad_maximum_fusion.4), channel_id=1, source_target_pairs={{0,1},{1,0},{2,3},{3,2},{4,5},{5,4},{6,7},{7,6},{8,9},{9,8},{10,11... | collective-permute-start | bytes 776 | tf_op jit(solution)/shard_map/ppermute | solution.py:14
  37.0 62.8 %collective-permute-start.4 = (bf16[64,2048]{1,0:T(8,128)(2,1)}, bf16[64,2048]{1,0:T(8,128)(2,1)}, u32[]{:S(2)}, u32[]{:S(2)}) collective-permute-start(bf16[64,2048]{1,0:T(8,128)(2,1)} %param.22), channel_id=1, source_target_pairs={{0,1},{1,0},{2,3},{3,2},{4,5},{5,4},{6,7},{7,6},{8,9},{9,8},{10,11... | collective-permute-start | bytes 786440 | tf_op jit(solution)/shard_map/ppermute | solution.py:14
  38.1 51.9 %copy-start.14 = (pred[128]{0:T(512)(128)(4,1)}, pred[128]{0:T(512)(128)(4,1)S(1)}, u32[]{:S(2)}) copy-start(pred[128]{0:T(512)(128)(4,1)S(1)} %get-tuple-element.54) | copy-start | bytes 388
  38.1 52.3 %copy-start.16 = (pred[128]{0:T(512)(128)(4,1)}, pred[128]{0:T(512)(128)(4,1)S(1)}, u32[]{:S(2)}) copy-start(pred[128]{0:T(512)(128)(4,1)S(1)} %get-tuple-element.55) | copy-start | bytes 388
  38.1 52.7 %copy-start.18 = (pred[128]{0:T(512)(128)(4,1)}, pred[128]{0:T(512)(128)(4,1)S(1)}, u32[]{:S(2)}) copy-start(pred[128]{0:T(512)(128)(4,1)S(1)} %get-tuple-element.56) | copy-start | bytes 388
  38.1 53.1 %copy-start.20 = (pred[128]{0:T(512)(128)(4,1)}, pred[128]{0:T(512)(128)(4,1)S(1)}, u32[]{:S(2)}) copy-start(pred[128]{0:T(512)(128)(4,1)S(1)} %get-tuple-element.49) | copy-start | bytes 388
  38.1 53.5 %copy-start.12 = (pred[128]{0:T(512)(128)(4,1)}, pred[128]{0:T(512)(128)(4,1)S(1)}, u32[]{:S(2)}) copy-start(pred[128]{0:T(512)(128)(4,1)S(1)} %get-tuple-element.53) | copy-start | bytes 388
  38.1 53.9 %copy-start.10 = (pred[128]{0:T(512)(128)(4,1)}, pred[128]{0:T(512)(128)(4,1)S(1)}, u32[]{:S(2)}) copy-start(pred[128]{0:T(512)(128)(4,1)S(1)} %get-tuple-element.52) | copy-start | bytes 388
  38.2 46.5 %copy-start.22 = (s32[128]{0:T(128)}, s32[128]{0:T(128)S(1)}, u32[]{:S(2)}) copy-start(s32[128]{0:T(128)S(1)} %select_n.228) | copy-start | bytes 1540
  38.3 46.4 %copy-start.24 = (s32[128]{0:T(128)}, s32[128]{0:T(128)S(1)}, u32[]{:S(2)}) copy-start(s32[128]{0:T(128)S(1)} %select_n.230) | copy-start | bytes 1540
  62.8 15.5 %all-to-all-start.1 = ((f32[32,2,256]{2,1,0:T(2,128)}), f32[32,2,256]{2,1,0:T(2,128)S(1)}, u32[]{:S(2)}, u32[]{:S(2)}) async-start(f32[32,2,256]{2,1,0:T(2,128)} %broadcast_in_dim.197), calls=%async_computation.1 | async-start | bytes 131072 | tf_op jit(solution)/shard_map/all_to_all | solution.py:26
  69.4 9.2 %collective-permute-start = (f32[640,64]{0,1:T(8,128)S(1)}, f32[640,64]{0,1:T(8,128)S(1)}, u32[]{:S(2)}, u32[]{:S(2)}) collective-permute-start(f32[640,64]{0,1:T(8,128)S(1)} %pad_maximum_fusion.1), channel_id=1, source_target_pairs={{0,1},{1,0},{2,3},{3,2},{4,5},{5,4},{6,7},{7,6},{8,9},{9,8},{10,11... | collective-permute-start | bytes 491528 | tf_op jit(solution)/shard_map/ppermute | solution.py:14
  78.7 7.6 %copy-start.4 = (bf16[256,64]{0,1:T(8,128)(2,1)}, bf16[256,64]{0,1:T(8,128)(2,1)S(1)}, u32[]{:S(2)}) copy-start(bf16[256,64]{0,1:T(8,128)(2,1)S(1)} %get-tuple-element.45) | copy-start | bytes 98308
  78.7 6.0 %collective-permute-start.2 = (bf16[256,2,128]{0,2,1:T(8,128)(2,1)S(1)}, bf16[256,2,128]{0,2,1:T(8,128)(2,1)S(1)}, u32[]{:S(2)}, u32[]{:S(2)}) collective-permute-start(bf16[256,2,128]{0,2,1:T(8,128)(2,1)S(1)} %maximum_select_fusion.3), channel_id=1, source_target_pairs={{0,32},{32,64},{64,96},{96,128},{128,160},{160,192},{192,224},{1,3... | collective-permute-start | bytes 393224 | tf_op jit(solution)/shard_map/ppermute | solution.py:20
  84.8 5.2 %copy-start.30 = (bf16[256,2,128]{0,2,1:T(8,128)(2,1)}, bf16[256,2,128]{0,2,1:T(8,128)(2,1)S(1)}, u32[]{:S(2)}) copy-start(bf16[256,2,128]{0,2,1:T(8,128)(2,1)S(1)} %collective-permute-done.2) | copy-start | bytes 393220
  95.0 1.9 copy-start.31
  99.7 7.0 %copy-start.6 = (s32[8,8]{1,0:T(8,128)S(1)}, s32[8,8]{1,0:T(8,128)}, u32[]{:S(2)}) copy-start(s32[8,8]{1,0:T(8,128)} %param.29) | copy-start | bytes 772
  99.8 7.5 %copy-start.8 = (bf16[2048]{0:T(1024)(128)(2,1)S(1)}, bf16[2048]{0:T(1024)(128)(2,1)}, u32[]{:S(2)}) copy-start(bf16[2048]{0:T(1024)(128)(2,1)} %param.28) | copy-start | bytes 12292
  102.4 18.5 %all-to-all-start.2 = ((bf16[16,8,2048]{2,1,0:T(8,128)(2,1)}), bf16[16,8,2048]{2,1,0:T(8,128)(2,1)S(1)}, u32[]{:S(2)}, u32[]{:S(2)}) async-start(bf16[16,8,2048]{2,1,0:T(8,128)(2,1)} %fusion.8), calls=%async_computation.2 | async-start | bytes 1048576 | tf_op jit(solution)/shard_map/all_to_all | solution.py:202
  140.3 38.3 %copy-start.29 = (bf16[1,2048,256]{2,1,0:T(8,128)(2,1)S(1)}, bf16[1,2048,256]{2,1,0:T(8,128)(2,1)}, u32[]{:S(2)}) copy-start(bf16[1,2048,256]{2,1,0:T(8,128)(2,1)} %param.31) | copy-start | bytes 3145732
  215.8 6.0 %copy-start.9 = (f32[8,8]{1,0:T(8,128)S(1)}, f32[8,8]{1,0:T(8,128)}, u32[]{:S(2)}) copy-start(f32[8,8]{1,0:T(8,128)} %param.30) | copy-start | bytes 772
  217.5 19.6 %all-to-all-start.6 = ((bf16[32,2,2,2048]{3,2,1,0:T(2,128)(2,1)}), bf16[32,2,2,2048]{3,2,1,0:T(2,128)(2,1)S(1)}, u32[]{:S(2)}, u32[]{:S(2)}) async-start(bf16[32,2,2,2048]{3,2,1,0:T(2,128)(2,1)} %copy.52), calls=%async_computation.6 | async-start | bytes 1048576 | tf_op jit(solution)/shard_map/all_to_all | solution.py:241
  (13 other events, 17.0 us)
Sparse Core Ops, SparseCore 0:
  23.2 54.4 all-gather.1

commit v9 on v8

--- a/solution.py
+++ b/solution.py
@@ -8,6 +8,7 @@
 TOP = 8
 EXP_DEV = 2
 TENSOR = ("th", "tyl")
+SEQ = ("sx", "sc")
 
 
 def from_partner(value):
@@ -76,8 +77,8 @@
     w_down,
 ):
     tensor_size = lax.axis_size(TENSOR)
-    seq_size = lax.axis_size("seq")
-    seq_index = lax.axis_index("seq")
+    seq_size = lax.axis_size(SEQ)
+    seq_index = lax.axis_index(SEQ)
     tensor_index = lax.axis_index(TENSOR)
     tok_dev = tokens.shape[0]
     width = tokens.shape[1]
@@ -91,7 +92,7 @@
         jnp.concatenate([prefix_own, prefix_partner], axis=-1),
         jnp.concatenate([prefix_partner, prefix_own], axis=-1),
     )
-    piece = lax.all_gather(prefix_full[None], "seq", axis=0, tiled=True)
+    piece = lax.all_gather(prefix_full[None], SEQ, axis=0, tiled=True)
     gains_in = from_partner(jnp.stack([q_gain, k_gain]))
     out_partner = from_partner(w_out)
     out_head = jnp.where(
@@ -169,7 +170,7 @@
     padded_seg = jnp.concatenate([jnp.full((tok_seq,), -1, jnp.int32), segments], axis=0)
     key_seg = lax.dynamic_slice_in_dim(padded_seg, base_row, 2 * tok_seq, 0)
     key_pos = base_row - tok_seq + jnp.arange(2 * tok_seq, dtype=jnp.int32)
-    previous = passed_along(suffix_full, "seq", 1)
+    previous = passed_along(suffix_full, SEQ, 1)
     suffix_keys = jnp.concatenate([previous, suffix_full], axis=0)
     suffix_mask = (key_seg[None, :] == query_seg[:, None]) & (
         key_pos[None, :] <= query_pos[:, None]
@@ -226,16 +227,26 @@
     gate_local = w_gate[0]
     up_local = w_up[0]
     down_local = w_down[0]
-    holders = seq_size // exp_local
+    chips = lax.axis_size("sx")
+    core = lax.axis_index("sc")
     per_expert = jnp.transpose(received, (1, 0, 2, 3))
-    chosen = lax.all_to_all(jnp.repeat(per_expert, holders, axis=0), "seq", 0, 0, tiled=True)
+    got = lax.all_to_all(
+        jnp.repeat(per_expert, chips // exp_local, axis=0), "sx", 0, 0, tiled=True
+    )
+    chosen = lax.all_gather(got, "sc", axis=1).reshape((seq_size,) + got.shape[1:])
     gated = jnp.einsum("srcd,df->srcf", chosen, gate_local, preferred_element_type=jnp.float32)
     upward = jnp.einsum("srcd,df->srcf", chosen, up_local, preferred_element_type=jnp.float32)
     activity = (jax.nn.silu(gated) * upward).astype(jnp.bfloat16)
     result = jnp.einsum("srcf,fd->srcd", activity, down_local, preferred_element_type=jnp.float32)
-    back = lax.all_to_all(result.astype(jnp.bfloat16), "seq", 0, 0, tiled=True)
+    by_core = result.astype(jnp.bfloat16).reshape((chips, 2) + result.shape[1:])
+    keep = jnp.where(core == 0, by_core[:, 0], by_core[:, 1])
+    give = jnp.where(core == 0, by_core[:, 1], by_core[:, 0])
+    sibling = lax.ppermute(give, "sc", [(0, 1), (1, 0)])
+    pair_sum = keep.astype(jnp.float32) + sibling.astype(jnp.float32)
+    back = lax.all_to_all(pair_sum.astype(jnp.bfloat16), "sx", 0, 0, tiled=True)
     summed = jnp.sum(
-        back.astype(jnp.float32).reshape((exp_local, holders) + back.shape[1:]), axis=1
+        back.astype(jnp.float32).reshape((exp_local, chips // exp_local) + back.shape[1:]),
+        axis=1,
     )
     summed = jnp.transpose(summed, (1, 0, 2, 3))
     returned = lax.all_to_all(
@@ -253,29 +264,31 @@
 
 def solution(mesh):
     seq_size, tensor_size = mesh.devices.shape
-    grid = Mesh(mesh.devices.reshape(seq_size, tensor_size // 2, 2), ("seq",) + TENSOR)
+    grid = Mesh(
+        mesh.devices.reshape(seq_size // 2, 2, tensor_size // 2, 2), SEQ + TENSOR
+    )
     return jax.shard_map(
         local,
         mesh=grid,
         in_specs=(
-            P(("seq",) + TENSOR, None),
+            P(SEQ + TENSOR, None),
             P(),
             P(None, None, TENSOR),
             P(TENSOR),
             P(TENSOR),
             P(TENSOR, None),
-            P("seq", None, TENSOR),
-            P("seq", None, TENSOR),
-            P(),
-            P(),
-            P(),
-            P(),
-            P(("seq",) + TENSOR, None),
-            P(("seq",) + TENSOR, None),
-            P(TENSOR + ("seq",), None, None),
-            P(TENSOR + ("seq",), None, None),
-            P(TENSOR + ("seq",), None, None),
+            P(SEQ, None, TENSOR),
+            P(SEQ, None, TENSOR),
+            P(),
+            P(),
+            P(),
+            P(),
+            P(SEQ + TENSOR, None),
+            P(SEQ + TENSOR, None),
+            P(TENSOR + SEQ, None, None),
+            P(TENSOR + SEQ, None, None),
+            P(TENSOR + SEQ, None, None),
         ),
-        out_specs=(P(("seq",) + TENSOR, None), P("seq", TENSOR), P("seq", TENSOR)),
+        out_specs=(P(SEQ + TENSOR, None), P(SEQ, TENSOR), P(SEQ, TENSOR)),
         check_vma=False,
     )

time: 249 us -> 245 us (0.984)
  blocking collectives: 86.9 us -> 53.5 us
  waiting for transfers between devices: 74.5 us -> 95.5 us
  starting transfers between devices: 32.2 us -> 37.8 us
    all_to_all x2, blocking collectives: 69 us -> 35.6 us  [the longest x1 18.6 us: local(): lax.all_to_all(jnp.repeat(per_expert, chips // exp_local, axis=0), 'sx',...]
    all_gather x1 -> x2, waiting for transfers between devices: 0.01 us -> 18.5 us  [the longest x1 18.5 us: local(): lax.all_gather(got, 'sc', axis=1).reshape((seq_size,) + got.shape[1:])]
    all_to_all x1, starting transfers between devices: 4.26 us -> 9.57 us  [local(): lax.all_to_all(summed.astype(jnp.bfloat16), TENSOR, split_axis=0, concat_...]
  transfers between devices with their start and end apart: 10 -> 12, of which waited for: 7 -> 9; matrix products, arithmetic and copies ran while one was open for 8% -> 8% of each run, Pallas kernels for 0% -> 0%
where the time goes in v9:
time: 245 us; the launch traced here: 241 us
  waiting for transfers between devices  95.5 us (39%)
  blocking collectives  53.5 us (22%)
  starting transfers between devices  37.8 us (15%)
  matrix products  19.3 us (8%)
  between operations  14.8 us (6%)
  local copies, waits for them, and re-layouts  12.1 us (5%)
  other arithmetic  7.4 us (3%)
    all_to_all x2, waiting for transfers between devices, gather_by_exchange(): got = lax.all_to_all(copies, axis, 0, 0, tiled=True)  30.1 us
    all_to_all x1, blocking collectives, local(): lax.all_to_all(jnp.repeat(per_expert, chips // exp_local, axis=0), 'sx',...  18.6 us
    all_gather x1, waiting for transfers between devices, local(): lax.all_gather(got, 'sc', axis=1).reshape((seq_size,) + got.shape[1:])  18.5 us
    all_to_all x1, blocking collectives, local(): lax.all_to_all(buffer, TENSOR, split_axis=0, concat_axis=0, tiled=True)  17.9 us
    all_to_all x2, starting transfers between devices, gather_by_exchange(): got = lax.all_to_all(copies, axis, 0, 0, tiled=True)  17.8 us
    all_to_all x1, blocking collectives, local(): back = lax.all_to_all(pair_sum.astype(jnp.bfloat16), 'sx', 0, 0, tiled=True)  16.9 us
    all_to_all x1, waiting for transfers between devices, local(): lax.all_to_all(summed.astype(jnp.bfloat16), TENSOR, split_axis=0, concat_...  14.7 us
    all_to_all x1, waiting for transfers between devices, local(): lax.all_to_all(attn_partial, 'th', 0, 0, tiled=True).astype(jnp.float32)  13.4 us
  transfers between devices with their start and end apart: 12, of which 9 were waited for; matrix products, arithmetic and copies ran while one was open for 8% of the time, Pallas kernels for 0%

profile of v9, /device:TPU:7, one launch (start us, length us, event | category | flops | bytes accessed | tf_op | source)
XLA Modules:
  0.0 240.6 jit_solution(2152705746825452924)
XLA Ops:
  7.2 1.2 fusion.164
  8.4 1.4 collective-permute-start.3
  9.8 11.5 %collective-permute-done.3 = bf16[2048,2,64]{0,2,1:T(8,128)(2,1)S(1)} collective-permute-done((bf16[2048,2,64]{0,2,1:T(8,128)(2,1)S(1)}, bf16[2048,2,64]{0,2,1:T(8,128)(2,1)S(1)}, u32[]{:S(2)}, u32[]{:S(2)}) %collective-permute-start.3) | collective-permute-done | bytes 524320 | tf_op jit(solution)/shard_map/ppermute | solution.py:15
  21.6 1.4 copy.80
  23.3 1.1 broadcast_in_dim.196
  24.4 11.2 %all-to-all-start = ((bf16[32,8,2048]{2,1,0:T(8,128)(2,1)}), bf16[32,8,2048]{2,1,0:T(8,128)(2,1)S(1)}, u32[]{:S(2)}, u32[]{:S(2)}) async-start(bf16[32,8,2048]{2,1,0:T(8,128)(2,1)} %broadcast_in_dim.196), calls=%async_computation | async-start | bytes 2097152 | tf_op jit(solution)/shard_map/all_to_all | solution.py:27
  35.6 1.3 collective-permute-start.1
  38.7 22.7 %all-to-all-done = bf16[32,8,2048]{2,1,0:T(8,128)(2,1)S(1)} async-done(((bf16[32,8,2048]{2,1,0:T(8,128)(2,1)}), bf16[32,8,2048]{2,1,0:T(8,128)(2,1)S(1)}, u32[]{:S(2)}, u32[]{:S(2)}) %all-to-all-start) | async-done | bytes 1048608 | tf_op jit(solution)/shard_map/all_to_all | solution.py:27
  62.1 0.6 broadcast_in_dim.197
  62.8 6.6 %all-to-all-start.1 = ((f32[32,2,256]{2,1,0:T(2,128)}), f32[32,2,256]{2,1,0:T(2,128)S(1)}, u32[]{:S(2)}, u32[]{:S(2)}) async-start(f32[32,2,256]{2,1,0:T(2,128)} %broadcast_in_dim.197), calls=%async_computation.1 | async-start | bytes 131072 | tf_op jit(solution)/shard_map/all_to_all | solution.py:27
  69.4 1.3 collective-permute-start
  70.8 7.5 %all-to-all-done.1 = f32[32,2,256]{2,1,0:T(2,128)S(1)} async-done(((f32[32,2,256]{2,1,0:T(2,128)}), f32[32,2,256]{2,1,0:T(2,128)S(1)}, u32[]{:S(2)}, u32[]{:S(2)}) %all-to-all-start.1) | async-done | bytes 65568 | tf_op jit(solution)/shard_map/all_to_all | solution.py:27
  78.7 1.5 collective-permute-start.2
  80.3 4.5 %collective-permute-done.2 = bf16[256,2,128]{0,2,1:T(8,128)(2,1)S(1)} collective-permute-done((bf16[256,2,128]{0,2,1:T(8,128)(2,1)S(1)}, bf16[256,2,128]{0,2,1:T(8,128)(2,1)S(1)}, u32[]{:S(2)}, u32[]{:S(2)}) %collective-permute-start.2) | collective-permute-done | bytes 131104 | tf_op jit(solution)/shard_map/ppermute | solution.py:21
  84.8 1.4 fusion.176
  86.2 3.7 %slice_bitcast_fusion.7 = (bf16[2048,2,128]{2,0,1:T(8,128)(2,1)S(1)}, bf16[2048,2,128]{2,0,1:T(8,128)(2,1)S(1)}, bf16[2048,2,128]{2,0,1:T(8,128)(2,1)S(1)}, bf16...) fusion(bf16[8,2048,2,128]{3,1,2,0:T(8,128)(2,1)} %all-gather.4., ...), kind=kLoop, calls=%fused_computation.60 | loop fusion | bytes 16777216 | tf_op jit(solution)/shard_map/squeeze | solution.py:196
  99.8 2.6 %fusion.8 = bf16[16,8,2048]{2,1,0:T(8,128)(2,1)} fusion(f32[128,128]{1,0:T(8,128)S(1)} %fusion.25, f32[128,2048]{1,0:T(8,128)S(1)} %get-tuple-element.62, bf16[2048,2,128]{2,0,1:T(8,128)(2,1)S(1)} %get-tuple-element.29, bf16[64,2048]{1,0:T(8,128)(2,1)} %collective-permute-done.4, bf16[64,2048]{1,0:T(8,128)(2,1)} %param.22, f32[128]{0:T(128)S(1)} %get-tuple-element.20, ...), kind=kOutput, calls=%fused_computation.19 | convolution fusion | flops 137674752 | bytes 2688513 | tf_op jit(solution)/shard_map/dot_general | solution.py:200
  102.4 4.3 %all-to-all-start.2 = ((bf16[16,8,2048]{2,1,0:T(8,128)(2,1)}), bf16[16,8,2048]{2,1,0:T(8,128)(2,1)S(1)}, u32[]{:S(2)}, u32[]{:S(2)}) async-start(bf16[16,8,2048]{2,1,0:T(8,128)(2,1)} %fusion.8), calls=%async_computation.2 | async-start | bytes 1048576 | tf_op jit(solution)/shard_map/all_to_all | solution.py:203
  107.4 13.4 %all-to-all-done.2 = bf16[16,8,2048]{2,1,0:T(8,128)(2,1)S(1)} async-done(((bf16[16,8,2048]{2,1,0:T(8,128)(2,1)}), bf16[16,8,2048]{2,1,0:T(8,128)(2,1)S(1)}, u32[]{:S(2)}, u32[]{:S(2)}) %all-to-all-start.2) | async-done | bytes 524320 | tf_op jit(solution)/shard_map/all_to_all | solution.py:203
  121.8 17.9 %all_to_all.35 = bf16[32,2,2,2048]{3,2,1,0:T(2,128)(2,1)S(1)} all-to-all(bf16[32,2,2,2048]{3,2,1,0:T(2,128)(2,1)S(1)} %reshape.1046), channel_id=1, replica_groups=mesh['sx'=4,'sc'=2,'th'=16,'tyl'=2] {'th','tyl'}, dimensions={0} | all-to-all | bytes 1048576 | tf_op jit(solution)/shard_map/all_to_all | solution.py:226
  140.1 18.6 %all_to_all.36 = bf16[4,32,2,2048]{3,1,2,0:T(8,128)(2,1)S(1)} all-to-all(bf16[4,32,2,2048]{3,1,2,0:T(8,128)(2,1)S(1)} %bitcast.179), channel_id=1, replica_groups=mesh['sx'=4,'sc'=2,'th'=16,'tyl'=2] {'sx'}, dimensions={0} | all-to-all | bytes 2097152 | tf_op jit(solution)/shard_map/all_to_all | solution.py:233
  158.7 1.1 copy.82
  159.8 18.5 %all-gather.6.cloned.1.call-done = bf16[4,64,2,2048]{3,1,0,2:T(8,128)(2,1)} async-done(((bf16[4,32,2,2048]{3,1,0,2:T(8,128)(2,1)}), bf16[4,64,2,2048]{3,1,0,2:T(8,128)(2,1)}) %all-gather.6.cloned.1.call-update) | async-done | bytes 2097168 | tf_op jit(solution)/shard_map/all_gather | solution.py:236
  178.3 3.1 %fusion.13 = f32[8,32,2,256]{3,1,2,0:T(8,128)} fusion(bf16[8,32,2,2048]{3,1,0,2:T(8,128)(2,1)} %bitcast.191, bf16[1,2048,256]{2,1,0:T(8,128)(2,1)S(1)} %copy-done.29), kind=kOutput, calls=%fused_computation.27 | convolution fusion | flops 536870912 | bytes 3670016 | tf_op jit(solution)/shard_map/srcd,df->srcf/dot_general | solution.py:237
  181.4 4.3 %convolution_convert_fusion = bf16[8,32,2,2048]{3,1,2,0:T(8,128)(2,1)S(1)} fusion(bf16[8,32,2,2048]{3,1,0,2:T(8,128)(2,1)} %bitcast.192, bf16[1,256,2048]{2,1,0:T(8,128)(2,1)S(1)} %copy-done, bf16[1,2048,256]{2,1,0:T(8,128)(2,1)} %param.32, f32[8,32,2,256]{3,1,2,0:T(8,128)} %fusion.13), kind=kOutput, calls=%fused_computation | convolution fusion | flops 1075576832 | bytes 6815744 | tf_op jit(solution)/shard_map/srcf,fd->srcd/dot_general | solution.py:240
  186.1 2.4 %collective-permute-done.5 = bf16[4,32,2,2048]{3,1,2,0:T(8,128)(2,1)S(1)} collective-permute-done((bf16[4,32,2,2048]{3,1,2,0:T(8,128)(2,1)S(1)}, bf16[4,32,2,2048]{3,1,2,0:T(8,128)(2,1)S(1)}, u32[]{:S(2)}, u32[]{:S(2)}) %collective-permute-start.5) | collective-permute-done | bytes 1048608 | tf_op jit(solution)/shard_map/ppermute | solution.py:244
  189.1 16.9 %all_to_all.37 = bf16[4,32,2,2048]{3,1,2,0:T(8,128)(2,1)S(1)} all-to-all(bf16[4,32,2,2048]{3,1,2,0:T(8,128)(2,1)S(1)} %fusion.10), channel_id=1, replica_groups=mesh['sx'=4,'sc'=2,'th'=16,'tyl'=2] {'sx'}, dimensions={0} | all-to-all | bytes 2097152 | tf_op jit(solution)/shard_map/all_to_all | solution.py:246
  206.2 1.3 copy.89
  207.6 9.6 %all-to-all-start.6 = ((bf16[32,2,2,2048]{3,2,1,0:T(2,128)(2,1)}), bf16[32,2,2,2048]{3,2,1,0:T(2,128)(2,1)S(1)}, u32[]{:S(2)}, u32[]{:S(2)}) async-start(bf16[32,2,2,2048]{3,2,1,0:T(2,128)(2,1)} %copy.89), calls=%async_computation.6 | async-start | bytes 1048576 | tf_op jit(solution)/shard_map/all_to_all | solution.py:252
  217.3 0.6 slice.343
  217.9 14.7 %all-to-all-done.6 = bf16[32,2,2,2048]{3,2,1,0:T(2,128)(2,1)S(1)} async-done(((bf16[32,2,2,2048]{3,2,1,0:T(2,128)(2,1)}), bf16[32,2,2,2048]{3,2,1,0:T(2,128)(2,1)S(1)}, u32[]{:S(2)}, u32[]{:S(2)}) %all-to-all-start.6) | async-done | bytes 524320 | tf_op jit(solution)/shard_map/all_to_all | solution.py:252
  232.8 0.9 fusion.9
  (168 shorter events, 16.5 us)
Async XLA Ops:
  7.2 174.2 %copy-start = (bf16[1,256,2048]{2,1,0:T(8,128)(2,1)S(1)}, bf16[1,256,2048]{2,1,0:T(8,128)(2,1)}, u32[]{:S(2)}) copy-start(bf16[1,256,2048]{2,1,0:T(8,128)(2,1)} %param.33) | copy-start | bytes 3145732
  7.2 79.1 %all-gather.4.cloned.1.call-start = ((), (), s32[]{:S(2)}) async-start(), calls=%async_computation.7 | async-start | bytes 9437184 | tf_op jit(solution)/shard_map/all_gather | solution.py:95
  8.4 12.9 %collective-permute-start.3 = (bf16[2048,2,64]{0,2,1:T(8,128)(2,1)S(1)}, bf16[2048,2,64]{0,2,1:T(8,128)(2,1)S(1)}, u32[]{:S(2)}, u32[]{:S(2)}) collective-permute-start(bf16[2048,2,64]{0,2,1:T(8,128)(2,1)S(1)} %get-tuple-element.37), channel_id=1, source_target_pairs={{0,1},{1,0},{2,3},{3,2},{4,5},{5,4},{6,7},{7,6},{8,9},{9,8},{10,11... | collective-permute-start | bytes 1572872 | tf_op jit(solution)/shard_map/ppermute | solution.py:15
  23.0 12.6 %copy-start.32 = (bf16[64]{0:T(256)(128)(2,1)S(1)}, bf16[64]{0:T(256)(128)(2,1)}, u32[]{:S(2)}) copy-start(bf16[64]{0:T(256)(128)(2,1)} %param.20) | copy-start | bytes 388
  23.0 12.6 %copy-start.34 = (bf16[64]{0:T(256)(128)(2,1)S(1)}, bf16[64]{0:T(256)(128)(2,1)}, u32[]{:S(2)}) copy-start(bf16[64]{0:T(256)(128)(2,1)} %param.21) | copy-start | bytes 388
  23.0 14.2 %copy-start.5 = (s32[2048]{0:T(1024)S(1)}, s32[2048]{0:T(1024)}, u32[]{:S(2)}) copy-start(s32[2048]{0:T(1024)} %param.25) | copy-start | bytes 24580
  23.0 14.3 %copy-start.28 = (s32[32]{0:T(128)S(1)}, s32[32]{0:T(128)}, u32[]{:S(2)}) copy-start(s32[32]{0:T(128)} %param.26) | copy-start | bytes 388
  23.0 14.9 %copy-start.33 = (s32[4]{0:T(128)S(1)}, s32[4]{0:T(128)}, u32[]{:S(2)}) copy-start(s32[4]{0:T(128)} %param.27) | copy-start | bytes 52
  23.0 38.3 %copy-start.1 = (bf16[2048,3,64]{0,2,1:T(8,128)(2,1)S(1)}, bf16[2048,3,64]{0,2,1:T(8,128)(2,1)}, u32[]{:S(2)}) copy-start(bf16[2048,3,64]{0,2,1:T(8,128)(2,1)} %param.19) | copy-start | bytes 2359300
  24.4 37.0 %all-to-all-start = ((bf16[32,8,2048]{2,1,0:T(8,128)(2,1)}), bf16[32,8,2048]{2,1,0:T(8,128)(2,1)S(1)}, u32[]{:S(2)}, u32[]{:S(2)}) async-start(bf16[32,8,2048]{2,1,0:T(8,128)(2,1)} %broadcast_in_dim.196), calls=%async_computation | async-start | bytes 2097152 | tf_op jit(solution)/shard_map/all_to_all | solution.py:27
  35.6 3.0 %collective-permute-start.1 = (bf16[2,64]{1,0:T(2,128)(2,1)S(1)}, bf16[2,64]{1,0:T(2,128)(2,1)S(1)}, u32[]{:S(2)}, u32[]{:S(2)}) collective-permute-start(bf16[2,64]{1,0:T(2,128)(2,1)S(1)} %pad_maximum_fusion.4), channel_id=1, source_target_pairs={{0,1},{1,0},{2,3},{3,2},{4,5},{5,4},{6,7},{7,6},{8,9},{9,8},{10,11... | collective-permute-start | bytes 776 | tf_op jit(solution)/shard_map/ppermute | solution.py:15
  37.0 62.8 %collective-permute-start.4 = (bf16[64,2048]{1,0:T(8,128)(2,1)}, bf16[64,2048]{1,0:T(8,128)(2,1)}, u32[]{:S(2)}, u32[]{:S(2)}) collective-permute-start(bf16[64,2048]{1,0:T(8,128)(2,1)} %param.22), channel_id=1, source_target_pairs={{0,1},{1,0},{2,3},{3,2},{4,5},{5,4},{6,7},{7,6},{8,9},{9,8},{10,11... | collective-permute-start | bytes 786440 | tf_op jit(solution)/shard_map/ppermute | solution.py:15
  38.1 51.9 %copy-start.14 = (pred[128]{0:T(512)(128)(4,1)}, pred[128]{0:T(512)(128)(4,1)S(1)}, u32[]{:S(2)}) copy-start(pred[128]{0:T(512)(128)(4,1)S(1)} %get-tuple-element.54) | copy-start | bytes 388
  38.1 52.3 %copy-start.16 = (pred[128]{0:T(512)(128)(4,1)}, pred[128]{0:T(512)(128)(4,1)S(1)}, u32[]{:S(2)}) copy-start(pred[128]{0:T(512)(128)(4,1)S(1)} %get-tuple-element.55) | copy-start | bytes 388
  38.1 52.7 %copy-start.18 = (pred[128]{0:T(512)(128)(4,1)}, pred[128]{0:T(512)(128)(4,1)S(1)}, u32[]{:S(2)}) copy-start(pred[128]{0:T(512)(128)(4,1)S(1)} %get-tuple-element.56) | copy-start | bytes 388
  38.1 53.1 %copy-start.20 = (pred[128]{0:T(512)(128)(4,1)}, pred[128]{0:T(512)(128)(4,1)S(1)}, u32[]{:S(2)}) copy-start(pred[128]{0:T(512)(128)(4,1)S(1)} %get-tuple-element.49) | copy-start | bytes 388
  38.1 53.5 %copy-start.12 = (pred[128]{0:T(512)(128)(4,1)}, pred[128]{0:T(512)(128)(4,1)S(1)}, u32[]{:S(2)}) copy-start(pred[128]{0:T(512)(128)(4,1)S(1)} %get-tuple-element.53) | copy-start | bytes 388
  38.1 53.9 %copy-start.10 = (pred[128]{0:T(512)(128)(4,1)}, pred[128]{0:T(512)(128)(4,1)S(1)}, u32[]{:S(2)}) copy-start(pred[128]{0:T(512)(128)(4,1)S(1)} %get-tuple-element.52) | copy-start | bytes 388
  38.2 46.5 %copy-start.22 = (s32[128]{0:T(128)}, s32[128]{0:T(128)S(1)}, u32[]{:S(2)}) copy-start(s32[128]{0:T(128)S(1)} %select_n.244) | copy-start | bytes 1540
  38.3 46.4 %copy-start.24 = (s32[128]{0:T(128)}, s32[128]{0:T(128)S(1)}, u32[]{:S(2)}) copy-start(s32[128]{0:T(128)S(1)} %select_n.246) | copy-start | bytes 1540
  62.8 15.5 %all-to-all-start.1 = ((f32[32,2,256]{2,1,0:T(2,128)}), f32[32,2,256]{2,1,0:T(2,128)S(1)}, u32[]{:S(2)}, u32[]{:S(2)}) async-start(f32[32,2,256]{2,1,0:T(2,128)} %broadcast_in_dim.197), calls=%async_computation.1 | async-start | bytes 131072 | tf_op jit(solution)/shard_map/all_to_all | solution.py:27
  69.4 9.2 %collective-permute-start = (f32[640,64]{0,1:T(8,128)S(1)}, f32[640,64]{0,1:T(8,128)S(1)}, u32[]{:S(2)}, u32[]{:S(2)}) collective-permute-start(f32[640,64]{0,1:T(8,128)S(1)} %pad_maximum_fusion.1), channel_id=1, source_target_pairs={{0,1},{1,0},{2,3},{3,2},{4,5},{5,4},{6,7},{7,6},{8,9},{9,8},{10,11... | collective-permute-start | bytes 491528 | tf_op jit(solution)/shard_map/ppermute | solution.py:15
  78.7 7.6 %copy-start.4 = (bf16[256,64]{0,1:T(8,128)(2,1)}, bf16[256,64]{0,1:T(8,128)(2,1)S(1)}, u32[]{:S(2)}) copy-start(bf16[256,64]{0,1:T(8,128)(2,1)S(1)} %get-tuple-element.45) | copy-start | bytes 98308
  78.7 6.0 %collective-permute-start.2 = (bf16[256,2,128]{0,2,1:T(8,128)(2,1)S(1)}, bf16[256,2,128]{0,2,1:T(8,128)(2,1)S(1)}, u32[]{:S(2)}, u32[]{:S(2)}) collective-permute-start(bf16[256,2,128]{0,2,1:T(8,128)(2,1)S(1)} %maximum_select_fusion.3), channel_id=1, source_target_pairs={{0,32},{32,64},{64,96},{96,128},{128,160},{160,192},{192,224},{1,3... | collective-permute-start | bytes 393224 | tf_op jit(solution)/shard_map/ppermute | solution.py:21
  99.8 7.0 %copy-start.6 = (s32[8,8]{1,0:T(8,128)S(1)}, s32[8,8]{1,0:T(8,128)}, u32[]{:S(2)}) copy-start(s32[8,8]{1,0:T(8,128)} %param.29) | copy-start | bytes 772
  99.8 7.5 %copy-start.8 = (bf16[2048]{0:T(1024)(128)(2,1)S(1)}, bf16[2048]{0:T(1024)(128)(2,1)}, u32[]{:S(2)}) copy-start(bf16[2048]{0:T(1024)(128)(2,1)} %param.28) | copy-start | bytes 12292
  102.4 18.4 %all-to-all-start.2 = ((bf16[16,8,2048]{2,1,0:T(8,128)(2,1)}), bf16[16,8,2048]{2,1,0:T(8,128)(2,1)S(1)}, u32[]{:S(2)}, u32[]{:S(2)}) async-start(bf16[16,8,2048]{2,1,0:T(8,128)(2,1)} %fusion.8), calls=%async_computation.2 | async-start | bytes 1048576 | tf_op jit(solution)/shard_map/all_to_all | solution.py:203
  106.7 71.6 %all-gather.6.cloned.1.call-start = ((), (), s32[]{:S(2)}) async-start(), calls=%async_computation.8 | async-start | bytes 3145728 | tf_op jit(solution)/shard_map/all_gather | solution.py:236
  158.7 19.6 %copy-start.29 = (bf16[1,2048,256]{2,1,0:T(8,128)(2,1)S(1)}, bf16[1,2048,256]{2,1,0:T(8,128)(2,1)}, u32[]{:S(2)}) copy-start(bf16[1,2048,256]{2,1,0:T(8,128)(2,1)} %param.31) | copy-start | bytes 3145732
  185.8 2.7 %collective-permute-start.5 = (bf16[4,32,2,2048]{3,1,2,0:T(8,128)(2,1)S(1)}, bf16[4,32,2,2048]{3,1,2,0:T(8,128)(2,1)S(1)}, u32[]{:S(2)}, u32[]{:S(2)}) collective-permute-start(bf16[4,32,2,2048]{3,1,2,0:T(8,128)(2,1)S(1)} %fusion.34), channel_id=1, source_target_pairs={{0,32},{32,0},{1,33},{33,1},{2,34},{34,2},{3,35},{35,3},{4,36},{36... | collective-permute-start | bytes 3145736 | tf_op jit(solution)/shard_map/ppermute | solution.py:244
  206.0 11.1 %copy-start.9 = (f32[8,8]{1,0:T(8,128)S(1)}, f32[8,8]{1,0:T(8,128)}, u32[]{:S(2)}) copy-start(f32[8,8]{1,0:T(8,128)} %param.30) | copy-start | bytes 772
  207.6 25.0 %all-to-all-start.6 = ((bf16[32,2,2,2048]{3,2,1,0:T(2,128)(2,1)}), bf16[32,2,2,2048]{3,2,1,0:T(2,128)(2,1)S(1)}, u32[]{:S(2)}, u32[]{:S(2)}) async-start(bf16[32,2,2,2048]{3,2,1,0:T(2,128)(2,1)} %copy.89), calls=%async_computation.6 | async-start | bytes 1048576 | tf_op jit(solution)/shard_map/all_to_all | solution.py:252
  (15 other events, 24.1 us)
Sparse Core Ops, SparseCore 0:
  23.2 54.4 all-gather.3
  159.9 18.3 all-gather.5

commit v10 on v9

--- a/solution.py
+++ b/solution.py
@@ -233,7 +233,10 @@
     got = lax.all_to_all(
         jnp.repeat(per_expert, chips // exp_local, axis=0), "sx", 0, 0, tiled=True
     )
-    chosen = lax.all_gather(got, "sc", axis=1).reshape((seq_size,) + got.shape[1:])
+    from_sibling = lax.ppermute(got, "sc", [(0, 1), (1, 0)])
+    chosen = jnp.where(
+        core == 0, jnp.stack([got, from_sibling], axis=1), jnp.stack([from_sibling, got], axis=1)
+    ).reshape((seq_size,) + got.shape[1:])
     gated = jnp.einsum("srcd,df->srcf", chosen, gate_local, preferred_element_type=jnp.float32)
     upward = jnp.einsum("srcd,df->srcf", chosen, up_local, preferred_element_type=jnp.float32)
     activity = (jax.nn.silu(gated) * upward).astype(jnp.bfloat16)

time: 245 us -> 229 us (0.935)
  waiting for transfers between devices: 95.5 us -> 79.2 us
    all_gather x1 -> x0, waiting for transfers between devices: 18.5 us -> none  [local(): lax.all_gather(got, 'sc', axis=1).reshape((seq_size,) + got.shape[1:])]
    ppermute x0 -> x1, starting transfers between devices: none -> 5.27 us  [local(): from_sibling = lax.ppermute(got, 'sc', [(0, 1), (1, 0)])]
    all_to_all x1, starting transfers between devices: 9.57 us -> 5.93 us  [local(): lax.all_to_all(summed.astype(jnp.bfloat16), TENSOR, split_axis=0, concat_...]
  transfers between devices with their start and end apart: 12 -> 12, of which waited for: 9 -> 9; matrix products, arithmetic and copies ran while one was open for 8% -> 9% of each run, Pallas kernels for 0% -> 0%
where the time goes in v10:
time: 229 us; the launch traced here: 225 us
  waiting for transfers between devices  79.2 us (35%)
  blocking collectives  53.8 us (23%)
  starting transfers between devices  39.6 us (17%)
  matrix products  17.7 us (8%)
  between operations  14.8 us (6%)
  local copies, waits for them, and re-layouts  12.4 us (5%)
  other arithmetic  7.69 us (3%)
    all_to_all x2, waiting for transfers between devices, gather_by_exchange(): got = lax.all_to_all(copies, axis, 0, 0, tiled=True)  30.1 us
    all_to_all x1, blocking collectives, local(): lax.all_to_all(jnp.repeat(per_expert, chips // exp_local, axis=0), 'sx',...  18.6 us
    all_to_all x1, blocking collectives, local(): lax.all_to_all(buffer, TENSOR, split_axis=0, concat_axis=0, tiled=True)  17.9 us
    all_to_all x2, starting transfers between devices, gather_by_exchange(): got = lax.all_to_all(copies, axis, 0, 0, tiled=True)  17.8 us
    all_to_all x1, blocking collectives, local(): back = lax.all_to_all(pair_sum.astype(jnp.bfloat16), 'sx', 0, 0, tiled=True)  17.2 us
    all_to_all x1, waiting for transfers between devices, local(): lax.all_to_all(summed.astype(jnp.bfloat16), TENSOR, split_axis=0, concat_...  14.7 us
    all_to_all x1, waiting for transfers between devices, local(): lax.all_to_all(attn_partial, 'th', 0, 0, tiled=True).astype(jnp.float32)  13.4 us
    ppermute x4, waiting for transfers between devices, from_partner(): return lax.ppermute(value, 'tyl', [(0, 1), (1, 0)])  11.8 us
  transfers between devices with their start and end apart: 12, of which 9 were waited for; matrix products, arithmetic and copies ran while one was open for 9% of the time, Pallas kernels for 0%

profile of v10, /device:TPU:7, one launch (start us, length us, event | category | flops | bytes accessed | tf_op | source)
XLA Modules:
  0.0 225.3 jit_solution(4002586612880419272)
XLA Ops:
  7.2 1.2 fusion.152
  8.4 1.4 collective-permute-start.3
  9.8 11.5 %collective-permute-done.3 = bf16[2048,2,64]{0,2,1:T(8,128)(2,1)S(1)} collective-permute-done((bf16[2048,2,64]{0,2,1:T(8,128)(2,1)S(1)}, bf16[2048,2,64]{0,2,1:T(8,128)(2,1)S(1)}, u32[]{:S(2)}, u32[]{:S(2)}) %collective-permute-start.3) | collective-permute-done | bytes 524320 | tf_op jit(solution)/shard_map/ppermute | solution.py:15
  21.6 1.4 copy.70
  23.3 1.1 broadcast_in_dim.196
  24.4 11.2 %all-to-all-start = ((bf16[32,8,2048]{2,1,0:T(8,128)(2,1)}), bf16[32,8,2048]{2,1,0:T(8,128)(2,1)S(1)}, u32[]{:S(2)}, u32[]{:S(2)}) async-start(bf16[32,8,2048]{2,1,0:T(8,128)(2,1)} %broadcast_in_dim.196), calls=%async_computation | async-start | bytes 2097152 | tf_op jit(solution)/shard_map/all_to_all | solution.py:27
  35.6 1.3 collective-permute-start.1
  38.7 22.7 %all-to-all-done = bf16[32,8,2048]{2,1,0:T(8,128)(2,1)S(1)} async-done(((bf16[32,8,2048]{2,1,0:T(8,128)(2,1)}), bf16[32,8,2048]{2,1,0:T(8,128)(2,1)S(1)}, u32[]{:S(2)}, u32[]{:S(2)}) %all-to-all-start) | async-done | bytes 1048608 | tf_op jit(solution)/shard_map/all_to_all | solution.py:27
  62.1 0.6 broadcast_in_dim.197
  62.8 6.6 %all-to-all-start.1 = ((f32[32,2,256]{2,1,0:T(2,128)}), f32[32,2,256]{2,1,0:T(2,128)S(1)}, u32[]{:S(2)}, u32[]{:S(2)}) async-start(f32[32,2,256]{2,1,0:T(2,128)} %broadcast_in_dim.197), calls=%async_computation.1 | async-start | bytes 131072 | tf_op jit(solution)/shard_map/all_to_all | solution.py:27
  69.4 1.3 collective-permute-start
  70.8 7.5 %all-to-all-done.1 = f32[32,2,256]{2,1,0:T(2,128)S(1)} async-done(((f32[32,2,256]{2,1,0:T(2,128)}), f32[32,2,256]{2,1,0:T(2,128)S(1)}, u32[]{:S(2)}, u32[]{:S(2)}) %all-to-all-start.1) | async-done | bytes 65568 | tf_op jit(solution)/shard_map/all_to_all | solution.py:27
  78.7 1.5 collective-permute-start.2
  80.3 4.5 %collective-permute-done.2 = bf16[256,2,128]{0,2,1:T(8,128)(2,1)S(1)} collective-permute-done((bf16[256,2,128]{0,2,1:T(8,128)(2,1)S(1)}, bf16[256,2,128]{0,2,1:T(8,128)(2,1)S(1)}, u32[]{:S(2)}, u32[]{:S(2)}) %collective-permute-start.2) | collective-permute-done | bytes 131104 | tf_op jit(solution)/shard_map/ppermute | solution.py:21
  84.8 1.4 fusion.164
  86.2 3.7 %slice_bitcast_fusion.7 = (bf16[2048,2,128]{2,0,1:T(8,128)(2,1)S(1)}, bf16[2048,2,128]{2,0,1:T(8,128)(2,1)S(1)}, bf16[2048,2,128]{2,0,1:T(8,128)(2,1)S(1)}, bf16...) fusion(bf16[8,2048,2,128]{3,1,2,0:T(8,128)(2,1)} %all-gather.2., ...), kind=kLoop, calls=%fused_computation.55 | loop fusion | bytes 16777216 | tf_op jit(solution)/shard_map/squeeze | solution.py:196
  99.8 2.6 %fusion.8 = bf16[16,8,2048]{2,1,0:T(8,128)(2,1)} fusion(f32[128,128]{1,0:T(8,128)S(1)} %fusion.13, f32[128,2048]{1,0:T(8,128)S(1)} %get-tuple-element.62, bf16[2048,2,128]{2,0,1:T(8,128)(2,1)S(1)} %get-tuple-element.29, bf16[64,2048]{1,0:T(8,128)(2,1)} %collective-permute-done.4, bf16[64,2048]{1,0:T(8,128)(2,1)} %param.22, f32[128]{0:T(128)S(1)} %get-tuple-element.20, ...), kind=kOutput, calls=%fused_computation.19 | convolution fusion | flops 137674752 | bytes 2688513 | tf_op jit(solution)/shard_map/dot_general | solution.py:200
  102.4 4.3 %all-to-all-start.2 = ((bf16[16,8,2048]{2,1,0:T(8,128)(2,1)}), bf16[16,8,2048]{2,1,0:T(8,128)(2,1)S(1)}, u32[]{:S(2)}, u32[]{:S(2)}) async-start(bf16[16,8,2048]{2,1,0:T(8,128)(2,1)} %fusion.8), calls=%async_computation.2 | async-start | bytes 1048576 | tf_op jit(solution)/shard_map/all_to_all | solution.py:203
  107.4 13.4 %all-to-all-done.2 = bf16[16,8,2048]{2,1,0:T(8,128)(2,1)S(1)} async-done(((bf16[16,8,2048]{2,1,0:T(8,128)(2,1)}), bf16[16,8,2048]{2,1,0:T(8,128)(2,1)S(1)}, u32[]{:S(2)}, u32[]{:S(2)}) %all-to-all-start.2) | async-done | bytes 524320 | tf_op jit(solution)/shard_map/all_to_all | solution.py:203
  121.8 17.9 %all_to_all.35 = bf16[32,2,2,2048]{3,2,1,0:T(2,128)(2,1)S(1)} all-to-all(bf16[32,2,2,2048]{3,2,1,0:T(2,128)(2,1)S(1)} %reshape.1060), channel_id=1, replica_groups=mesh['sx'=4,'sc'=2,'th'=16,'tyl'=2] {'th','tyl'}, dimensions={0} | all-to-all | bytes 1048576 | tf_op jit(solution)/shard_map/all_to_all | solution.py:226
  140.1 18.6 %all_to_all.36 = bf16[4,32,2,2048]{3,1,2,0:T(8,128)(2,1)S(1)} all-to-all(bf16[4,32,2,2048]{3,1,2,0:T(8,128)(2,1)S(1)} %bitcast.187), channel_id=1, replica_groups=mesh['sx'=4,'sc'=2,'th'=16,'tyl'=2] {'sx'}, dimensions={0} | all-to-all | bytes 2097152 | tf_op jit(solution)/shard_map/all_to_all | solution.py:233
  158.7 5.3 %collective-permute-start.5 = (bf16[4,32,2,2048]{3,1,2,0:T(8,128)(2,1)S(1)}, bf16[4,32,2,2048]{3,1,2,0:T(8,128)(2,1)S(1)}, u32[]{:S(2)}, u32[]{:S(2)}) collective-permute-start(bf16[4,32,2,2048]{3,1,2,0:T(8,128)(2,1)S(1)} %all_to_all.36), channel_id=1, source_target_pairs={{0,32},{32,0},{1,33},{33,1},{2,34},{34,2},{3,35},{35,3},{4,36},{36... | collective-permute-start | bytes 3145736 | tf_op jit(solution)/shard_map/ppermute | solution.py:236
  164.0 2.3 %collective-permute-done.5 = bf16[4,32,2,2048]{3,1,2,0:T(8,128)(2,1)S(1)} collective-permute-done((bf16[4,32,2,2048]{3,1,2,0:T(8,128)(2,1)S(1)}, bf16[4,32,2,2048]{3,1,2,0:T(8,128)(2,1)S(1)}, u32[]{:S(2)}, u32[]{:S(2)}) %collective-permute-start.5) | collective-permute-done | bytes 1048608 | tf_op jit(solution)/shard_map/ppermute | solution.py:236
  166.6 1.3 copy-done.1
  168.0 1.5 fusion.25
  169.5 4.3 %convolution_convert_fusion = bf16[8,32,2,2048]{3,1,2,0:T(8,128)(2,1)S(1)} fusion(bf16[1,256,2048]{2,1,0:T(8,128)(2,1)S(1)} %copy-done, f32[8,32,2,256]{3,1,2,0:T(8,128)} %fusion.25, bf16[8,32,2,2048]{3,1,2,0:T(8,128)(2,1)} %bitcast.190, bf16[1,2048,256]{2,1,0:T(8,128)(2,1)} %param.31), kind=kOutput, calls=%fused_computation | convolution fusion | flops 1075576832 | bytes 6815744 | tf_op jit(solution)/shard_map/srcf,fd->srcd/dot_general | solution.py:243
  174.4 2.3 %collective-permute-done.6 = bf16[4,32,2,2048]{3,1,2,0:T(8,128)(2,1)S(1)} collective-permute-done((bf16[4,32,2,2048]{3,1,2,0:T(8,128)(2,1)S(1)}, bf16[4,32,2,2048]{3,1,2,0:T(8,128)(2,1)S(1)}, u32[]{:S(2)}, u32[]{:S(2)}) %collective-permute-start.6) | collective-permute-done | bytes 1048608 | tf_op jit(solution)/shard_map/ppermute | solution.py:247
  177.2 17.2 %all_to_all.37 = bf16[4,32,2,2048]{3,1,2,0:T(8,128)(2,1)S(1)} all-to-all(bf16[4,32,2,2048]{3,1,2,0:T(8,128)(2,1)S(1)} %fusion.10), channel_id=1, replica_groups=mesh['sx'=4,'sc'=2,'th'=16,'tyl'=2] {'sx'}, dimensions={0} | all-to-all | bytes 2097152 | tf_op jit(solution)/shard_map/all_to_all | solution.py:249
  194.6 1.3 copy.76
  195.9 5.9 %all-to-all-start.6 = ((bf16[32,2,2,2048]{3,2,1,0:T(2,128)(2,1)}), bf16[32,2,2,2048]{3,2,1,0:T(2,128)(2,1)S(1)}, u32[]{:S(2)}, u32[]{:S(2)}) async-start(bf16[32,2,2,2048]{3,2,1,0:T(2,128)(2,1)} %copy.76), calls=%async_computation.6 | async-start | bytes 1048576 | tf_op jit(solution)/shard_map/all_to_all | solution.py:255
  202.6 14.7 %all-to-all-done.6 = bf16[32,2,2,2048]{3,2,1,0:T(2,128)(2,1)S(1)} async-done(((bf16[32,2,2,2048]{3,2,1,0:T(2,128)(2,1)}), bf16[32,2,2,2048]{3,2,1,0:T(2,128)(2,1)S(1)}, u32[]{:S(2)}, u32[]{:S(2)}) %all-to-all-start.6) | async-done | bytes 524320 | tf_op jit(solution)/shard_map/all_to_all | solution.py:255
  217.5 0.9 fusion.9
  (169 shorter events, 17.5 us)
Async XLA Ops:
  7.2 162.3 %copy-start = (bf16[1,256,2048]{2,1,0:T(8,128)(2,1)S(1)}, bf16[1,256,2048]{2,1,0:T(8,128)(2,1)}, u32[]{:S(2)}) copy-start(bf16[1,256,2048]{2,1,0:T(8,128)(2,1)} %param.33) | copy-start | bytes 3145732
  7.2 79.1 %all-gather.2.cloned.1.call-start = ((), (), s32[]{:S(2)}) async-start(), calls=%async_computation.7 | async-start | bytes 9437184 | tf_op jit(solution)/shard_map/all_gather | solution.py:95
  8.4 12.9 %collective-permute-start.3 = (bf16[2048,2,64]{0,2,1:T(8,128)(2,1)S(1)}, bf16[2048,2,64]{0,2,1:T(8,128)(2,1)S(1)}, u32[]{:S(2)}, u32[]{:S(2)}) collective-permute-start(bf16[2048,2,64]{0,2,1:T(8,128)(2,1)S(1)} %get-tuple-element.37), channel_id=1, source_target_pairs={{0,1},{1,0},{2,3},{3,2},{4,5},{5,4},{6,7},{7,6},{8,9},{9,8},{10,11... | collective-permute-start | bytes 1572872 | tf_op jit(solution)/shard_map/ppermute | solution.py:15
  23.0 12.6 %copy-start.33 = (bf16[64]{0:T(256)(128)(2,1)S(1)}, bf16[64]{0:T(256)(128)(2,1)}, u32[]{:S(2)}) copy-start(bf16[64]{0:T(256)(128)(2,1)} %param.20) | copy-start | bytes 388
  23.0 12.6 %copy-start.35 = (bf16[64]{0:T(256)(128)(2,1)S(1)}, bf16[64]{0:T(256)(128)(2,1)}, u32[]{:S(2)}) copy-start(bf16[64]{0:T(256)(128)(2,1)} %param.21) | copy-start | bytes 388
  23.0 14.2 %copy-start.6 = (s32[2048]{0:T(1024)S(1)}, s32[2048]{0:T(1024)}, u32[]{:S(2)}) copy-start(s32[2048]{0:T(1024)} %param.25) | copy-start | bytes 24580
  23.0 14.3 %copy-start.29 = (s32[32]{0:T(128)S(1)}, s32[32]{0:T(128)}, u32[]{:S(2)}) copy-start(s32[32]{0:T(128)} %param.26) | copy-start | bytes 388
  23.0 14.9 %copy-start.34 = (s32[4]{0:T(128)S(1)}, s32[4]{0:T(128)}, u32[]{:S(2)}) copy-start(s32[4]{0:T(128)} %param.27) | copy-start | bytes 52
  23.0 38.3 %copy-start.2 = (bf16[2048,3,64]{0,2,1:T(8,128)(2,1)S(1)}, bf16[2048,3,64]{0,2,1:T(8,128)(2,1)}, u32[]{:S(2)}) copy-start(bf16[2048,3,64]{0,2,1:T(8,128)(2,1)} %param.19) | copy-start | bytes 2359300
  24.4 37.0 %all-to-all-start = ((bf16[32,8,2048]{2,1,0:T(8,128)(2,1)}), bf16[32,8,2048]{2,1,0:T(8,128)(2,1)S(1)}, u32[]{:S(2)}, u32[]{:S(2)}) async-start(bf16[32,8,2048]{2,1,0:T(8,128)(2,1)} %broadcast_in_dim.196), calls=%async_computation | async-start | bytes 2097152 | tf_op jit(solution)/shard_map/all_to_all | solution.py:27
  35.6 3.0 %collective-permute-start.1 = (bf16[2,64]{1,0:T(2,128)(2,1)S(1)}, bf16[2,64]{1,0:T(2,128)(2,1)S(1)}, u32[]{:S(2)}, u32[]{:S(2)}) collective-permute-start(bf16[2,64]{1,0:T(2,128)(2,1)S(1)} %pad_maximum_fusion.4), channel_id=1, source_target_pairs={{0,1},{1,0},{2,3},{3,2},{4,5},{5,4},{6,7},{7,6},{8,9},{9,8},{10,11... | collective-permute-start | bytes 776 | tf_op jit(solution)/shard_map/ppermute | solution.py:15
  37.0 62.8 %collective-permute-start.4 = (bf16[64,2048]{1,0:T(8,128)(2,1)}, bf16[64,2048]{1,0:T(8,128)(2,1)}, u32[]{:S(2)}, u32[]{:S(2)}) collective-permute-start(bf16[64,2048]{1,0:T(8,128)(2,1)} %param.22), channel_id=1, source_target_pairs={{0,1},{1,0},{2,3},{3,2},{4,5},{5,4},{6,7},{7,6},{8,9},{9,8},{10,11... | collective-permute-start | bytes 786440 | tf_op jit(solution)/shard_map/ppermute | solution.py:15
  38.1 51.9 %copy-start.15 = (pred[128]{0:T(512)(128)(4,1)}, pred[128]{0:T(512)(128)(4,1)S(1)}, u32[]{:S(2)}) copy-start(pred[128]{0:T(512)(128)(4,1)S(1)} %get-tuple-element.54) | copy-start | bytes 388
  38.1 52.3 %copy-start.17 = (pred[128]{0:T(512)(128)(4,1)}, pred[128]{0:T(512)(128)(4,1)S(1)}, u32[]{:S(2)}) copy-start(pred[128]{0:T(512)(128)(4,1)S(1)} %get-tuple-element.55) | copy-start | bytes 388
  38.1 52.7 %copy-start.19 = (pred[128]{0:T(512)(128)(4,1)}, pred[128]{0:T(512)(128)(4,1)S(1)}, u32[]{:S(2)}) copy-start(pred[128]{0:T(512)(128)(4,1)S(1)} %get-tuple-element.56) | copy-start | bytes 388
  38.1 53.1 %copy-start.21 = (pred[128]{0:T(512)(128)(4,1)}, pred[128]{0:T(512)(128)(4,1)S(1)}, u32[]{:S(2)}) copy-start(pred[128]{0:T(512)(128)(4,1)S(1)} %get-tuple-element.49) | copy-start | bytes 388
  38.1 53.5 %copy-start.13 = (pred[128]{0:T(512)(128)(4,1)}, pred[128]{0:T(512)(128)(4,1)S(1)}, u32[]{:S(2)}) copy-start(pred[128]{0:T(512)(128)(4,1)S(1)} %get-tuple-element.53) | copy-start | bytes 388
  38.1 53.9 %copy-start.11 = (pred[128]{0:T(512)(128)(4,1)}, pred[128]{0:T(512)(128)(4,1)S(1)}, u32[]{:S(2)}) copy-start(pred[128]{0:T(512)(128)(4,1)S(1)} %get-tuple-element.52) | copy-start | bytes 388
  38.2 46.5 %copy-start.23 = (s32[128]{0:T(128)}, s32[128]{0:T(128)S(1)}, u32[]{:S(2)}) copy-start(s32[128]{0:T(128)S(1)} %select_n.266) | copy-start | bytes 1540
  38.3 46.4 %copy-start.25 = (s32[128]{0:T(128)}, s32[128]{0:T(128)S(1)}, u32[]{:S(2)}) copy-start(s32[128]{0:T(128)S(1)} %select_n.268) | copy-start | bytes 1540
  62.8 15.5 %all-to-all-start.1 = ((f32[32,2,256]{2,1,0:T(2,128)}), f32[32,2,256]{2,1,0:T(2,128)S(1)}, u32[]{:S(2)}, u32[]{:S(2)}) async-start(f32[32,2,256]{2,1,0:T(2,128)} %broadcast_in_dim.197), calls=%async_computation.1 | async-start | bytes 131072 | tf_op jit(solution)/shard_map/all_to_all | solution.py:27
  69.4 9.2 %collective-permute-start = (f32[640,64]{0,1:T(8,128)S(1)}, f32[640,64]{0,1:T(8,128)S(1)}, u32[]{:S(2)}, u32[]{:S(2)}) collective-permute-start(f32[640,64]{0,1:T(8,128)S(1)} %pad_maximum_fusion.1), channel_id=1, source_target_pairs={{0,1},{1,0},{2,3},{3,2},{4,5},{5,4},{6,7},{7,6},{8,9},{9,8},{10,11... | collective-permute-start | bytes 491528 | tf_op jit(solution)/shard_map/ppermute | solution.py:15
  78.7 7.6 %copy-start.5 = (bf16[256,64]{0,1:T(8,128)(2,1)}, bf16[256,64]{0,1:T(8,128)(2,1)S(1)}, u32[]{:S(2)}) copy-start(bf16[256,64]{0,1:T(8,128)(2,1)S(1)} %get-tuple-element.45) | copy-start | bytes 98308
  78.7 6.0 %collective-permute-start.2 = (bf16[256,2,128]{0,2,1:T(8,128)(2,1)S(1)}, bf16[256,2,128]{0,2,1:T(8,128)(2,1)S(1)}, u32[]{:S(2)}, u32[]{:S(2)}) collective-permute-start(bf16[256,2,128]{0,2,1:T(8,128)(2,1)S(1)} %maximum_select_fusion.4), channel_id=1, source_target_pairs={{0,32},{32,64},{64,96},{96,128},{128,160},{160,192},{192,224},{1,3... | collective-permute-start | bytes 393224 | tf_op jit(solution)/shard_map/ppermute | solution.py:21
  84.8 5.2 %copy-start.31 = (bf16[256,2,128]{0,2,1:T(8,128)(2,1)}, bf16[256,2,128]{0,2,1:T(8,128)(2,1)S(1)}, u32[]{:S(2)}) copy-start(bf16[256,2,128]{0,2,1:T(8,128)(2,1)S(1)} %collective-permute-done.2) | copy-start | bytes 393220
  99.8 7.0 %copy-start.7 = (s32[8,8]{1,0:T(8,128)S(1)}, s32[8,8]{1,0:T(8,128)}, u32[]{:S(2)}) copy-start(s32[8,8]{1,0:T(8,128)} %param.29) | copy-start | bytes 772
  99.8 7.5 %copy-start.9 = (bf16[2048]{0:T(1024)(128)(2,1)S(1)}, bf16[2048]{0:T(1024)(128)(2,1)}, u32[]{:S(2)}) copy-start(bf16[2048]{0:T(1024)(128)(2,1)} %param.28) | copy-start | bytes 12292
  102.4 18.4 %all-to-all-start.2 = ((bf16[16,8,2048]{2,1,0:T(8,128)(2,1)}), bf16[16,8,2048]{2,1,0:T(8,128)(2,1)S(1)}, u32[]{:S(2)}, u32[]{:S(2)}) async-start(bf16[16,8,2048]{2,1,0:T(8,128)(2,1)} %fusion.8), calls=%async_computation.2 | async-start | bytes 1048576 | tf_op jit(solution)/shard_map/all_to_all | solution.py:203
  158.7 7.6 %collective-permute-start.5 = (bf16[4,32,2,2048]{3,1,2,0:T(8,128)(2,1)S(1)}, bf16[4,32,2,2048]{3,1,2,0:T(8,128)(2,1)S(1)}, u32[]{:S(2)}, u32[]{:S(2)}) collective-permute-start(bf16[4,32,2,2048]{3,1,2,0:T(8,128)(2,1)S(1)} %all_to_all.36), channel_id=1, source_target_pairs={{0,32},{32,0},{1,33},{33,1},{2,34},{34,2},{3,35},{35,3},{4,36},{36... | collective-permute-start | bytes 3145736 | tf_op jit(solution)/shard_map/ppermute | solution.py:236
  173.9 2.7 %collective-permute-start.6 = (bf16[4,32,2,2048]{3,1,2,0:T(8,128)(2,1)S(1)}, bf16[4,32,2,2048]{3,1,2,0:T(8,128)(2,1)S(1)}, u32[]{:S(2)}, u32[]{:S(2)}) collective-permute-start(bf16[4,32,2,2048]{3,1,2,0:T(8,128)(2,1)S(1)} %fusion.22), channel_id=1, source_target_pairs={{0,32},{32,0},{1,33},{33,1},{2,34},{34,2},{3,35},{35,3},{4,36},{36... | collective-permute-start | bytes 3145736 | tf_op jit(solution)/shard_map/ppermute | solution.py:247
  194.4 7.5 %copy-start.10 = (f32[8,8]{1,0:T(8,128)S(1)}, f32[8,8]{1,0:T(8,128)}, u32[]{:S(2)}) copy-start(f32[8,8]{1,0:T(8,128)} %param.30) | copy-start | bytes 772
  195.9 21.4 %all-to-all-start.6 = ((bf16[32,2,2,2048]{3,2,1,0:T(2,128)(2,1)}), bf16[32,2,2,2048]{3,2,1,0:T(2,128)(2,1)S(1)}, u32[]{:S(2)}, u32[]{:S(2)}) async-start(bf16[32,2,2,2048]{3,2,1,0:T(2,128)(2,1)} %copy.76), calls=%async_computation.6 | async-start | bytes 1048576 | tf_op jit(solution)/shard_map/all_to_all | solution.py:255
  (16 other events, 21.9 us)
Sparse Core Ops, SparseCore 0:
  23.2 54.4 all-gather.1
